TPU v7x, 256 devices: a whole 4x4x8 slice. The times are simulated.
256 devices in a mesh: ctx: 16 (over x, y), tp: 8 (over z), dp: 2 (over core).
Axes of the slice: x: 4, y: 4, z: 8, core: 2. Of those that a mesh axis runs over, the one named last changes fastest.
Arguments:
- attn_out: bfloat16 [32768, 2048], P(('dp', 'ctx'), 'tp'), parts along dimension 0, may hold values from -6 to 6
- routing: int32 [32768, 8], P(('dp', 'ctx', 'tp')), parts along dimension 0, may hold values from 0 to 127, all different within a row; in each aligned block of 128 rows (0 to 127, 128 to 255, ...) at most 12 rows name the same one
- gates: float32 [32768, 8], P(('dp', 'ctx', 'tp')), parts along dimension 0, may hold values from 0.1 to 1
- w_gate: bfloat16 [256, 2048, 768], P(('dp', 'ctx', 'tp')), parts along dimension 0, may hold values from -0.125 to 0.125
- w_up: bfloat16 [256, 2048, 768], P(('dp', 'ctx', 'tp')), parts along dimension 0, may hold values from -0.125 to 0.125
- w_down: bfloat16 [256, 768, 2048], P(('dp', 'ctx', 'tp')), parts along dimension 0, may hold values from -0.21875 to 0.21875
Outputs:
- moe_out: bfloat16 [32768, 2048], P(('dp', 'ctx'), 'tp'), parts along dimension 0
There are 2 independent parts, one for each index of `dp`. A program takes and returns all parts, laid end to end along the dimension named above; each array names one. Nothing has to cross between parts.
Inputs may be any that keep to these rules, and one draw needn't show every extreme that they name: `routing`: each row names 8 different experts. In each aligned block of 128 rows (the rows of one device of ctx and tp), no expert is named by more than 12 rows, a bound that some block reaches.
All inputs are finite; a program needn't handle non-finite values.
Results may differ from a plain program's by a relative error of at most 0.0057.
Values may be sent and summed in bfloat16 or wider, within the bound.
No kernel may reach another device: no remote copies, remote signals or barrier semaphores. Data moves between devices by JAX's collectives and lax.ppermute only.
A program may use at most 192 MiB of HBM per device.

v0:
```python
import jax
import jax.numpy as jnp
from jax import lax
from jax.sharding import PartitionSpec as P


def slot_numbers(expert_ids, experts):
    one_hot = (
        expert_ids[:, :, None] == jnp.arange(experts, dtype=jnp.int32)[None, None, :]
    ).astype(jnp.int32)
    return jnp.sum(jnp.cumsum(one_hot, axis=1) * one_hot, axis=2) - 1


def expert_rows(features, w_gate, w_up, w_down, form):
    hidden_form = form[:-1] + "f"
    gate_proj = jnp.einsum(
        form + ",ldf->" + hidden_form, features, w_gate, preferred_element_type=jnp.float32
    )
    up_proj = jnp.einsum(
        form + ",ldf->" + hidden_form, features, w_up, preferred_element_type=jnp.float32
    )
    hidden = (jax.nn.silu(gate_proj) * up_proj).astype(jnp.bfloat16)
    result = jnp.einsum(
        hidden_form + ",lfd->" + form, hidden, w_down, preferred_element_type=jnp.float32
    )
    return result.astype(jnp.bfloat16)


def fill_buffer(rows_in, slot_table):
    picked = rows_in[jnp.maximum(slot_table, 0)]
    return jnp.where((slot_table >= 0)[:, None], picked, jnp.zeros((), rows_in.dtype))


def combine(flat_out, target, weights):
    picked = flat_out[target]
    return jnp.sum(weights[:, :, None] * picked.astype(jnp.float32), axis=1).astype(jnp.bfloat16)


def on_device(attn_out, routing, gates, w_gate, w_up, w_down):
    n_ctx = lax.axis_size("ctx")
    n_tp = lax.axis_size("tp")
    exp_dev = w_gate.shape[0]
    experts = exp_dev * n_ctx * n_tp
    top_count = routing.shape[1]
    features = lax.all_to_all(attn_out, "tp", split_axis=0, concat_axis=1, tiled=True)
    tok_dev = features.shape[0]
    width = features.shape[1]
    capacity = 3 * tok_dev * top_count // (2 * experts)
    expert_ids = routing.reshape(1, tok_dev * top_count)
    slot_of = slot_numbers(expert_ids, experts)
    target = (expert_ids * capacity + slot_of).reshape(-1)
    source_row = jnp.arange(tok_dev * top_count, dtype=jnp.int32) // top_count
    slot_table = jnp.full((experts * capacity,), -1, jnp.int32).at[target].set(source_row)
    outgoing = fill_buffer(features, slot_table).reshape(n_ctx * n_tp, exp_dev, capacity, width)
    result = expert_rows(
        lax.all_to_all(outgoing, ("ctx", "tp"), split_axis=0, concat_axis=0, tiled=True),
        w_gate,
        w_up,
        w_down,
        "alsd",
    )
    returned = lax.all_to_all(result, ("ctx", "tp"), split_axis=0, concat_axis=0, tiled=True)
    flat_out = returned.reshape(experts * capacity, width)
    mixed = combine(flat_out, target.reshape(tok_dev, top_count), gates)
    return lax.all_to_all(mixed, "tp", split_axis=1, concat_axis=0, tiled=True)


def solution(mesh):
    in_specs = (
        P(("dp", "ctx"), "tp"),
        P(("dp", "ctx", "tp"), None),
        P(("dp", "ctx", "tp"), None),
        P(("dp", "ctx", "tp"), None, None),
        P(("dp", "ctx", "tp"), None, None),
        P(("dp", "ctx", "tp"), None, None),
    )
    out_specs = P(("dp", "ctx"), "tp")
    return jax.shard_map(
        on_device, mesh=mesh, in_specs=in_specs, out_specs=out_specs, check_vma=False
    )
```

profile of v0, /device:TPU:2, one launch (start us, length us, event | category | flops | bytes accessed | tf_op | source)
XLA Modules:
  0.0 540.3 jit_solution(18035569003555551119)
XLA Ops:
  0.0 0.0 copy-start
  0.0 8.7 %all-to-all-start = ((bf16[8,128,256]{2,1,0:T(8,128)(2,1)}), bf16[8,128,256]{2,1,0:T(8,128)(2,1)}, u32[]{:S(2)}, u32[]{:S(2)}) async-start(bf16[8,128,256]{2,1,0:T(8,128)(2,1)} %bitcast.90), calls=%async_computation | async-start | bytes 1048576 | tf_op jit(solution)/shard_map/all_to_all | solution.py:45
  8.7 0.8 copy.29
  9.5 0.1 eq.27
  9.6 0.2 fusion.19
  9.8 0.3 fusion.17
  10.1 0.9 copy.32
  11.1 1.4 fusion.16
  12.5 0.1 sub.17
  12.6 0.1 mul.41
  12.8 4.3 scatter_custom_fusion
  17.1 0.1 broadcast_in_dim.28
  17.2 9.1 %all-to-all-done = bf16[8,128,256]{2,1,0:T(8,128)(2,1)} async-done(((bf16[8,128,256]{2,1,0:T(8,128)(2,1)}), bf16[8,128,256]{2,1,0:T(8,128)(2,1)}, u32[]{:S(2)}, u32[]{:S(2)}) %all-to-all-start) | async-done | bytes 524320 | tf_op jit(solution)/shard_map/all_to_all | solution.py:45
  26.3 1.9 copy.39
  28.2 13.8 %gather_fusion = bf16[1536,2048]{1,0:T(8,128)(2,1)} fusion(bf16[128,2048]{1,0:T(8,128)(2,1)} %bitcast.84, s32[2048]{0:T(1024)S(1)} %pad_clamp_fusion), kind=kCustom, calls=%fused_computation | custom fusion | bytes 12589056 | tf_op jit(solution)/shard_map/gather | solution.py:30
  42.0 10.6 %gather.9 = bf16[128,1,12,2048]{3,2,0,1:T(8,128)(2,1)} reshape(bf16[1536,2048]{1,0:T(8,128)(2,1)} %gather_fusion) | data formatting | bytes 12582912 | tf_op jit(solution)/shard_map/gather | solution.py:30
  52.6 7.3 %select_bitcast_fusion = bf16[128,1,12,2048]{3,2,1,0:T(8,128)(2,1)} fusion(bf16[128,1,12,2048]{3,2,0,1:T(8,128)(2,1)} %gather.9, pred[128,12]{1,0:T(8,128)(4,1)S(1)} %broadcast_in_dim.28), kind=kLoop, calls=%fused_computation.5 | loop fusion | flops 3145728 | bytes 12584448 | tf_op jit(solution)/shard_map/jit(_where)/select_n | solution.py:31
  59.9 196.0 %all_to_all.45 = bf16[128,1,12,2048]{3,2,1,0:T(8,128)(2,1)S(1)} all-to-all(bf16[128,1,12,2048]{3,2,1,0:T(8,128)(2,1)} %select_bitcast_fusion), channel_id=1, replica_groups=mesh['ctx'=16,'tp'=8,'dp'=2] {'ctx','tp'}, dimensions={0} | all-to-all | bytes 12582912 | tf_op jit(solution)/shard_map/all_to_all | solution.py:56
  255.9 12.6 %fusion.1 = f32[128,12,768]{2,0,1:T(8,128)S(1)} fusion(bf16[128,1,12,2048]{3,2,1,0:T(8,128)(2,1)S(1)} %all_to_all.45, bf16[1,2048,768]{2,1,0:T(8,128)(2,1)S(1)} %copy-done.3), kind=kOutput, calls=%fused_computation.6 | convolution fusion | flops 4831838208 | bytes 14155776 | tf_op jit(solution)/shard_map/alsd,ldf->alsf/dot_general | solution.py:19
  268.6 12.5 %fusion.3 = f32[128,12,768]{2,0,1:T(8,128)S(1)} fusion(bf16[128,1,12,2048]{3,2,1,0:T(8,128)(2,1)S(1)} %all_to_all.45, bf16[1,2048,768]{2,1,0:T(8,128)(2,1)S(1)} %copy-done.4), kind=kOutput, calls=%fused_computation.8 | convolution fusion | flops 4831838208 | bytes 14155776 | tf_op jit(solution)/shard_map/alsd,ldf->alsf/dot_general | solution.py:16
  281.3 5.3 convert_bitcast_fusion
  286.6 6.8 %copy.36 = bf16[128,1,12,2048]{3,2,1,0:T(8,128)(2,1)} copy(bf16[128,1,12,2048]{3,0,2,1:T(8,128)(2,1)S(1)} %convert_bitcast_fusion) | data formatting | bytes 12582912 | tf_op jit(solution)/shard_map/convert_element_type | solution.py:26
  293.5 10.5 %all-to-all-start.2 = ((bf16[128,1,12,2048]{3,2,1,0:T(8,128)(2,1)}), bf16[128,1,12,2048]{3,2,1,0:T(8,128)(2,1)}, u32[]{:S(2)}, u32[]{:S(2)}) async-start(bf16[128,1,12,2048]{3,2,1,0:T(8,128)(2,1)} %copy.36), calls=%async_computation.2 | async-start | bytes 16777216 | tf_op jit(solution)/shard_map/all_to_all | solution.py:62
  304.0 0.1 reshape.237
  304.1 0.1 copy.28
  304.2 182.5 %all-to-all-done.2 = bf16[128,1,12,2048]{3,2,1,0:T(8,128)(2,1)} async-done(((bf16[128,1,12,2048]{3,2,1,0:T(8,128)(2,1)}), bf16[128,1,12,2048]{3,2,1,0:T(8,128)(2,1)}, u32[]{:S(2)}, u32[]{:S(2)}) %all-to-all-start.2) | async-done | bytes 6291488 | tf_op jit(solution)/shard_map/all_to_all | solution.py:62
  486.7 10.7 %reshape.225 = bf16[1536,2048]{1,0:T(8,128)(2,1)} reshape(bf16[128,1,12,2048]{3,2,1,0:T(8,128)(2,1)} %all-to-all-done.2) | data formatting | bytes 12582912 | tf_op jit(solution)/shard_map/reshape | solution.py:63
  497.4 12.6 %gather_fusion.1 = bf16[1024,2048]{1,0:T(8,128)(2,1)} fusion(bf16[1536,2048]{1,0:T(8,128)(2,1)} %reshape.225, s32[1024]{0:T(1024)S(1)} %broadcast_clamp_fusion), kind=kCustom, calls=%fused_computation.1 | custom fusion | bytes 8392704 | tf_op jit(solution)/shard_map/gather | solution.py:35
  510.0 7.3 %fusion = bf16[128,2048]{1,0:T(8,128)(2,1)} fusion(bf16[1024,2048]{1,0:T(8,128)(2,1)} %gather_fusion.1, f32[128,8]{1,0:T(8,128)S(1)} %copy.28), kind=kLoop, calls=%fused_computation.4 | loop fusion | flops 6029312 | bytes 4722688 | tf_op jit(solution)/shard_map/reduce_sum | solution.py:36
  517.3 2.0 copy.37
  519.4 18.6 %all_to_all.46 = bf16[128,8,256]{0,2,1:T(8,128)(2,1)} all-to-all(bf16[128,8,256]{0,2,1:T(8,128)(2,1)} %bitcast.87), channel_id=1, replica_groups=mesh['ctx'=16,'tp'=8,'dp'=2] {'tp'}, dimensions={1} | all-to-all | bytes 1048576 | tf_op jit(solution)/shard_map/all_to_all | solution.py:65
  538.0 2.0 copy.38
  (21 shorter events, 0.1 us)
Async XLA Ops:
  0.0 281.2 %copy-start = (bf16[1,768,2048]{2,1,0:T(8,128)(2,1)S(1)}, bf16[1,768,2048]{2,1,0:T(8,128)(2,1)}, u32[]{:S(2)}) copy-start(bf16[1,768,2048]{2,1,0:T(8,128)(2,1)} %param.11) | copy-start | bytes 9437188
  0.0 26.3 %all-to-all-start = ((bf16[8,128,256]{2,1,0:T(8,128)(2,1)}), bf16[8,128,256]{2,1,0:T(8,128)(2,1)}, u32[]{:S(2)}, u32[]{:S(2)}) async-start(bf16[8,128,256]{2,1,0:T(8,128)(2,1)} %bitcast.90), calls=%async_computation | async-start | bytes 1048576 | tf_op jit(solution)/shard_map/all_to_all | solution.py:45
  59.9 196.0 %copy-start.3 = (bf16[1,2048,768]{2,1,0:T(8,128)(2,1)S(1)}, bf16[1,2048,768]{2,1,0:T(8,128)(2,1)}, u32[]{:S(2)}) copy-start(bf16[1,2048,768]{2,1,0:T(8,128)(2,1)} %param.10) | copy-start | bytes 9437188
  255.9 12.7 %copy-start.4 = (bf16[1,2048,768]{2,1,0:T(8,128)(2,1)S(1)}, bf16[1,2048,768]{2,1,0:T(8,128)(2,1)}, u32[]{:S(2)}) copy-start(bf16[1,2048,768]{2,1,0:T(8,128)(2,1)} %param.9) | copy-start | bytes 9437188
  293.5 10.6 %copy-start.2 = (f32[128,8]{0,1:T(8,128)S(1)}, f32[128,8]{0,1:T(8,128)}, u32[]{:S(2)}) copy-start(f32[128,8]{0,1:T(8,128)} %param.8) | copy-start | bytes 12292
  293.5 193.3 %all-to-all-start.2 = ((bf16[128,1,12,2048]{3,2,1,0:T(8,128)(2,1)}), bf16[128,1,12,2048]{3,2,1,0:T(8,128)(2,1)}, u32[]{:S(2)}, u32[]{:S(2)}) async-start(bf16[128,1,12,2048]{3,2,1,0:T(8,128)(2,1)} %copy.36), calls=%async_computation.2 | async-start | bytes 16777216 | tf_op jit(solution)/shard_map/all_to_all | solution.py:62
  497.4 42.6 %copy-start.1 = (bf16[1,768,2048]{2,1,0:T(8,128)(2,1)S(1)}, bf16[1,768,2048]{2,1,0:T(8,128)(2,1)}, u32[]{:S(2)}) copy-start(bf16[1,768,2048]{2,1,0:T(8,128)(2,1)} %param.11) | copy-start | bytes 9437188
where the time goes:
time: 548 us; the launch traced here: 540 us
  blocking collectives  215 us (39%)
  waiting for transfers between devices  192 us (35%)
  local copies, waits for them, and re-layouts  67.1 us (12%)
  matrix products  30.5 us (6%)
  starting transfers between devices  19.2 us (4%)
  other arithmetic  16.6 us (3%)
    all_to_all x1, blocking collectives, on_device(): lax.all_to_all(outgoing, ('ctx', 'tp'), split_axis=0, concat_axis=0, tile...  196 us
    all_to_all x1, waiting for transfers between devices, on_device(): lax.all_to_all(result, ('ctx', 'tp'), split_axis=0, concat_axis=0, tiled=...  183 us
    gather x2, local copies, waits for them, and re-layouts, fill_buffer(): picked = rows_in[jnp.maximum(slot_table, 0)]  24.4 us
    all_to_all x1, blocking collectives, on_device(): return lax.all_to_all(mixed, 'tp', split_axis=1, concat_axis=0, tiled=True)  18.6 us
    dot_general x1, matrix products, expert_rows(): jnp.einsum(form + ',ldf->' + hidden_form, features, w_up, preferred_eleme...  12.6 us
    gather x1, local copies, waits for them, and re-layouts, combine(): picked = flat_out[target]  12.6 us
    dot_general x1, matrix products, expert_rows(): jnp.einsum(form + ',ldf->' + hidden_form, features, w_gate, preferred_ele...  12.5 us
  transfers between devices with their start and end apart: 2, of which 2 were waited for; matrix products, arithmetic and copies ran while one was open for 2% of the time, Pallas kernels for 0%

commit v1 on v0

v1 whole, which is shorter than its diff:
```python
import jax
import jax.numpy as jnp
from jax import lax
from jax.sharding import PartitionSpec as P


def slot_numbers(expert_ids, experts):
    one_hot = (
        expert_ids[:, :, None] == jnp.arange(experts, dtype=jnp.int32)[None, None, :]
    ).astype(jnp.int32)
    return jnp.sum(jnp.cumsum(one_hot, axis=1) * one_hot, axis=2) - 1


def expert_rows(features, w_gate, w_up, w_down, form):
    hidden_form = form[:-1] + "f"
    gate_proj = jnp.einsum(
        form + ",ldf->" + hidden_form, features, w_gate, preferred_element_type=jnp.float32
    )
    up_proj = jnp.einsum(
        form + ",ldf->" + hidden_form, features, w_up, preferred_element_type=jnp.float32
    )
    hidden = (jax.nn.silu(gate_proj) * up_proj).astype(jnp.bfloat16)
    result = jnp.einsum(
        hidden_form + ",lfd->" + form, hidden, w_down, preferred_element_type=jnp.float32
    )
    return result.astype(jnp.bfloat16)


def on_device(attn_out, routing, gates, w_gate, w_up, w_down):
    n_ctx = lax.axis_size("ctx")
    n_tp = lax.axis_size("tp")
    me_tp = lax.axis_index("tp")
    exp_dev = w_gate.shape[0]
    experts = exp_dev * n_ctx * n_tp
    tok_blk, top_count = routing.shape
    width = attn_out.shape[1] * n_tp
    capacity = 3 * tok_blk * top_count // (2 * experts)

    slot_of = slot_numbers(routing.reshape(1, tok_blk * top_count), experts)
    code = routing * capacity + slot_of.reshape(tok_blk, top_count)
    info = jnp.concatenate([code.astype(jnp.float32), gates], axis=1)
    info_all = lax.all_gather(info, "tp", axis=0)
    code_all = info_all[:, :, :top_count].astype(jnp.int32)
    gates_all = info_all[:, :, top_count:]
    expert_all = code_all // capacity
    slot_all = code_all - expert_all * capacity
    dest_ctx = expert_all // (n_tp * exp_dev)
    dest_tp = (expert_all // exp_dev) % n_tp
    dest_loc = expert_all % exp_dev
    mine = dest_tp == me_tp
    per_dest = exp_dev * capacity
    position = jnp.where(mine, (dest_ctx * exp_dev + dest_loc) * capacity + slot_all, -1)
    slots_all = n_ctx * per_dest
    hits = position[..., None] == jnp.arange(slots_all, dtype=jnp.int32)
    select = jnp.sum(hits.astype(jnp.int32), axis=2).astype(jnp.bfloat16)
    weight = jnp.sum(jnp.where(hits, gates_all[..., None], 0.0), axis=2)

    feats = lax.all_gather(attn_out, "tp", axis=0)
    feats = feats.reshape(n_tp, n_tp, tok_blk, width // n_tp)
    select = select.reshape(n_tp, tok_blk, n_ctx, per_dest)
    outgoing = jnp.einsum(
        "bjcq,sbjf->cbqsf", select, feats, preferred_element_type=jnp.bfloat16
    ).reshape(n_ctx, n_tp * per_dest, width)

    received = lax.all_to_all(outgoing, "ctx", split_axis=0, concat_axis=0, tiled=True)
    rows = received.reshape(n_ctx, n_tp, exp_dev, capacity, width)
    rows = jnp.transpose(rows, (2, 0, 1, 3, 4)).reshape(exp_dev, n_ctx * n_tp * capacity, width)
    result = expert_rows(rows, w_gate, w_up, w_down, "lsd")
    result = jnp.transpose(
        result.reshape(exp_dev, n_ctx, n_tp, capacity, width), (1, 2, 0, 3, 4)
    ).reshape(n_ctx, n_tp * per_dest, width)
    returned = lax.all_to_all(result, "ctx", split_axis=0, concat_axis=0, tiled=True)
    returned = returned.reshape(n_ctx, n_tp, per_dest, width)

    weight = weight.reshape(n_tp, tok_blk, n_ctx, per_dest)
    w_hi = weight.astype(jnp.bfloat16)
    w_lo = (weight - w_hi.astype(jnp.float32)).astype(jnp.bfloat16)
    partial = jnp.einsum(
        "bjcq,cbqd->bjd", w_hi, returned, preferred_element_type=jnp.float32
    ) + jnp.einsum("bjcq,cbqd->bjd", w_lo, returned, preferred_element_type=jnp.float32)
    partial = partial.reshape(n_tp * tok_blk, width)
    total = lax.psum_scatter(partial, "tp", scatter_dimension=1, tiled=True)
    return total.astype(jnp.bfloat16)


def solution(mesh):
    in_specs = (
        P(("dp", "ctx"), "tp"),
        P(("dp", "ctx", "tp"), None),
        P(("dp", "ctx", "tp"), None),
        P(("dp", "ctx", "tp"), None, None),
        P(("dp", "ctx", "tp"), None, None),
        P(("dp", "ctx", "tp"), None, None),
    )
    out_specs = P(("dp", "ctx"), "tp")
    return jax.shard_map(
        on_device, mesh=mesh, in_specs=in_specs, out_specs=out_specs, check_vma=False
    )
```

time: 548 us -> 403 us (0.74); the launches traced: 540 us -> 402 us
  blocking collectives: 215 us -> 108 us
  local copies, waits for them, and re-layouts: 67.1 us -> 25.2 us
  waiting for transfers between devices: 192 us -> 212 us
  starting transfers between devices: 19.2 us -> 6.08 us
  between operations: 0.65 us -> 13.6 us
  other arithmetic: 16.6 us -> 8.29 us
    all_to_all x2 -> x1, blocking collectives: 215 us -> 79.4 us  [on_device(): lax.all_to_all(outgoing, 'ctx', split_axis=0, concat_axis=0, tiled=True)]
    all_to_all x2 -> x1, waiting for transfers between devices: 192 us -> 78.7 us  [on_device(): lax.all_to_all(result, 'ctx', split_axis=0, concat_axis=0, tiled=True)]
    reduce_scatter x0 -> x1, waiting for transfers between devices: none -> 109 us  [on_device(): total = lax.psum_scatter(partial, 'tp', scatter_dimension=1, tiled=True)]
    gather x3 -> x0, local copies, waits for them, and re-layouts: 37 us -> none  [the longest x2 24.4 us: fill_buffer(): picked = rows_in[jnp.maximum(slot_table, 0)]]
    all_gather x0 -> x1, blocking collectives: none -> 28.5 us  [on_device(): info_all = lax.all_gather(info, 'tp', axis=0)]
    all_gather x0 -> x1, waiting for transfers between devices: none -> 24.1 us  [on_device(): feats = lax.all_gather(attn_out, 'tp', axis=0)]
    all_to_all x2 -> x1, starting transfers between devices: 19.2 us -> 5.82 us  [on_device(): lax.all_to_all(result, 'ctx', split_axis=0, concat_axis=0, tiled=True)]
    dot_general x0 -> x3, matrix products: none -> 10.3 us  [the longest x1 5.05 us: on_device(): jnp.einsum('bjcq,cbqd->bjd', w_lo, returned, preferred_element_type=jnp.f...]
  transfers between devices with their start and end apart: 2 -> 3, of which waited for: 2 -> 3; matrix products, arithmetic and copies ran while one was open for 2% -> 2% of each run, Pallas kernels for 0% -> 0%
where the time goes in v1:
time: 403 us; the launch traced here: 402 us
  waiting for transfers between devices  212 us (53%)
  blocking collectives  108 us (27%)
  matrix products  28.2 us (7%)
  local copies, waits for them, and re-layouts  25.2 us (6%)
  between operations  13.6 us (3%)
  other arithmetic  8.29 us (2%)
  starting transfers between devices  6.08 us (2%)
    reduce_scatter x1, waiting for transfers between devices, on_device(): total = lax.psum_scatter(partial, 'tp', scatter_dimension=1, tiled=True)  109 us
    all_to_all x1, blocking collectives, on_device(): lax.all_to_all(outgoing, 'ctx', split_axis=0, concat_axis=0, tiled=True)  79.4 us
    all_to_all x1, waiting for transfers between devices, on_device(): lax.all_to_all(result, 'ctx', split_axis=0, concat_axis=0, tiled=True)  78.7 us
    all_gather x1, blocking collectives, on_device(): info_all = lax.all_gather(info, 'tp', axis=0)  28.5 us
    all_gather x1, waiting for transfers between devices, on_device(): feats = lax.all_gather(attn_out, 'tp', axis=0)  24.1 us
    reshape x1, local copies, waits for them, and re-layouts, on_device(): outgoing = jnp.einsum('bjcq,sbjf->cbqsf', select, feats, preferred_elemen...  10.5 us
  transfers between devices with their start and end apart: 3, of which 3 were waited for; matrix products, arithmetic and copies ran while one was open for 2% of the time, Pallas kernels for 0%

profile of v1, /device:TPU:2, one launch (start us, length us, event | category | flops | bytes accessed | tf_op | source)
XLA Modules:
  0.0 401.6 jit_solution(4884793959239323)
XLA Ops:
  6.5 0.7 all-gather.4.cloned.1.call-update
  7.3 1.0 copy.52
  8.3 0.1 eq.49
  8.4 0.2 fusion.12
  8.6 0.3 fusion.10
  8.9 0.9 copy.54
  9.9 1.4 fusion.9
  11.4 0.7 add_convert_fusion
  12.1 0.7 pad_maximum_fusion
  12.8 28.5 %all-gather = f32[1024,16]{0,1:T(8,128)S(1)} all-gather(f32[128,16]{0,1:T(8,128)S(1)} %pad_maximum_fusion), channel_id=2, replica_groups=mesh['ctx'=16,'tp'=8,'dp'=2] {'tp'}, dimensions={0}, use_global_device_ids=true | all-gather | bytes 73728 | tf_op jit(solution)/shard_map/all_gather | solution.py:42
  41.4 0.5 copy-done.4
  42.0 0.8 convert_reduce_fusion
  42.9 0.3 copy.59
  43.2 24.1 %all-gather.4.cloned.1.call-done = bf16[8192,256]{1,0:T(8,128)(2,1)} async-done(((bf16[1024,256]{1,0:T(8,128)(2,1)}), bf16[8192,256]{1,0:T(8,128)(2,1)}) %all-gather.4.cloned.1.call-update) | async-done | bytes 4194320 | tf_op jit(solution)/shard_map/all_gather | solution.py:58
  67.3 4.0 fusion.6
  71.2 4.9 %copy.62 = bf16[16,8,12,8,256]{4,3,2,1,0:T(8,128)(2,1)} copy(bf16[16,8,12,8,256]{4,0,3,2,1:T(8,128)(2,1)S(1)} %fusion.6) | data formatting | bytes 12582912 | tf_op jit(solution)/shard_map/bjcq,sbjf->cbqsf/transpose | solution.py:61
  76.1 10.5 %reshape.179 = bf16[16,96,2048]{2,1,0:T(8,128)(2,1)} reshape(bf16[16,8,12,8,256]{4,3,2,1,0:T(8,128)(2,1)} %copy.62) | data formatting | bytes 12582912 | tf_op jit(solution)/shard_map/reshape | solution.py:63
  86.6 79.4 %all_to_all.10 = bf16[16,96,2048]{2,1,0:T(8,128)(2,1)S(1)} all-to-all(bf16[16,96,2048]{2,1,0:T(8,128)(2,1)} %reshape.179), channel_id=1, replica_groups=mesh['ctx'=16,'tp'=8,'dp'=2] {'ctx'}, dimensions={0} | all-to-all | bytes 12582912 | tf_op jit(solution)/shard_map/all_to_all | solution.py:65
  166.1 5.2 %fusion.4 = f32[1536,768]{1,0:T(8,128)S(1)} fusion(bf16[1536,2048]{1,0:T(8,128)(2,1)S(1)} %bitcast.57, bf16[1,2048,768]{2,1,0:T(8,128)(2,1)S(1)} %copy-done.6), kind=kOutput, calls=%fused_computation.10 | convolution fusion | flops 4831838208 | bytes 14155776 | tf_op jit(solution)/shard_map/lsd,ldf->lsf/dot_general | solution.py:16
  171.3 5.6 %multiply_convert_fusion = bf16[1536,768]{1,0:T(8,128)(2,1)S(1)} fusion(f32[1536,768]{1,0:T(8,128)S(1)} %fusion.4, bf16[1536,2048]{1,0:T(8,128)(2,1)S(1)} %bitcast.58, bf16[1,2048,768]{2,1,0:T(8,128)(2,1)S(1)} %copy-done.7), kind=kOutput, calls=%fused_computation.5 | convolution fusion | flops 4838916096 | bytes 16515072 | tf_op jit(solution)/shard_map/lsd,ldf->lsf/dot_general | solution.py:19
  176.9 7.0 %convolution_convert_fusion = bf16[1536,2048]{1,0:T(8,128)(2,1)} fusion(bf16[1536,768]{1,0:T(8,128)(2,1)S(1)} %multiply_convert_fusion, bf16[1,768,2048]{2,1,0:T(8,128)(2,1)S(1)} %copy-done), kind=kOutput, calls=%fused_computation.1 | convolution fusion | flops 4834983936 | bytes 11796480 | tf_op jit(solution)/shard_map/lsf,lfd->lsd/dot_general | solution.py:23
  183.9 5.8 %all-to-all-start.1 = ((bf16[16,96,2048]{2,1,0:T(8,128)(2,1)}), bf16[16,96,2048]{2,1,0:T(8,128)(2,1)}, u32[]{:S(2)}, u32[]{:S(2)}) async-start(bf16[16,96,2048]{2,1,0:T(8,128)(2,1)} %bitcast.56), calls=%async_computation.1 | async-start | bytes 12582912 | tf_op jit(solution)/shard_map/all_to_all | solution.py:72
  189.8 0.3 reduce-scatter.2.cloned.1.call-start
  190.1 1.1 select_reduce_fusion
  191.2 0.5 copy.58
  191.6 0.9 subtract_convert_fusion
  192.5 78.7 %all-to-all-done.1 = bf16[16,96,2048]{2,1,0:T(8,128)(2,1)} async-done(((bf16[16,96,2048]{2,1,0:T(8,128)(2,1)}), bf16[16,96,2048]{2,1,0:T(8,128)(2,1)}, u32[]{:S(2)}, u32[]{:S(2)}) %all-to-all-start.1) | async-done | bytes 6291488 | tf_op jit(solution)/shard_map/all_to_all | solution.py:72
  271.2 6.3 %copy.63 = bf16[16,96,2048]{2,0,1:T(8,128)(2,1)S(1)} copy(bf16[16,96,2048]{2,1,0:T(8,128)(2,1)} %all-to-all-done.1) | data formatting | bytes 12582912 | tf_op jit(solution)/shard_map/all_to_all | solution.py:72
  277.5 1.3 fusion.15
  278.8 5.0 %bitcast_add_fusion = f32[8,128,2048]{2,1,0:T(8,128)} fusion(f32[8,128,2048,1]{2,1,3,0:T(8,128)S(1)} %fusion.15, bf16[16,8,12,2048]{3,0,2,1:T(8,128)(2,1)S(1)} %bitcast.53, bf16[8,128,16,12]{1,0,3,2:T(8,128)(2,1)S(1)} %get-tuple-element.5), kind=kOutput, calls=%fused_computation | convolution fusion | flops 807403520 | bytes 23461888 | tf_op jit(solution)/shard_map/bjcq,cbqd->bjd/dot_general | solution.py:80
  283.9 108.9 %reduce-scatter.2.cloned.1.call-done = f32[1024,256]{1,0:T(8,128)} async-done(((f32[1024,2048]{1,0:T(8,128)}), f32[1024,256]{1,0:T(8,128)}) %reduce-scatter.2.cloned.1.call-update) | async-done | bytes 1048592 | tf_op jit(solution)/shard_map/reduce_scatter | solution.py:82
  392.7 2.1 convert_element_type.55
  (30 shorter events, 0.4 us)
Async XLA Ops:
  6.5 170.4 %copy-start = (bf16[1,768,2048]{2,1,0:T(8,128)(2,1)S(1)}, bf16[1,768,2048]{2,1,0:T(8,128)(2,1)}, u32[]{:S(2)}) copy-start(bf16[1,768,2048]{2,1,0:T(8,128)(2,1)} %param.11) | copy-start | bytes 9437188
  6.5 60.7 %all-gather.4.cloned.1.call-start = ((), (), s32[]{:S(2)}) async-start(), calls=%async_computation.4 | async-start | bytes 4718592 | tf_op jit(solution)/shard_map/all_gather | solution.py:58
  41.3 0.6 copy-start.4
  42.0 0.9 copy-start.2
  86.6 79.4 %copy-start.6 = (bf16[1,2048,768]{2,1,0:T(8,128)(2,1)S(1)}, bf16[1,2048,768]{2,1,0:T(8,128)(2,1)}, u32[]{:S(2)}) copy-start(bf16[1,2048,768]{2,1,0:T(8,128)(2,1)} %param.9) | copy-start | bytes 9437188
  166.1 5.2 %copy-start.7 = (bf16[1,2048,768]{2,1,0:T(8,128)(2,1)S(1)}, bf16[1,2048,768]{2,1,0:T(8,128)(2,1)}, u32[]{:S(2)}) copy-start(bf16[1,2048,768]{2,1,0:T(8,128)(2,1)} %param.10) | copy-start | bytes 9437188
  183.9 6.1 %copy-start.5 = (f32[2,8,8,128]{3,2,1,0:T(8,128)S(1)}, f32[2,8,8,128]{3,2,1,0:T(8,128)}, u32[]{:S(2)}) copy-start(f32[2,8,8,128]{3,2,1,0:T(8,128)} %copy-done.4) | copy-start | bytes 196612
  183.9 6.1 %copy-start.3 = (s32[8,128,8]{1,2,0:T(8,128)S(1)}, s32[8,128,8]{1,2,0:T(8,128)}, u32[]{:S(2)}) copy-start(s32[8,128,8]{1,2,0:T(8,128)} %copy-done.2) | copy-start | bytes 98308
  183.9 87.3 %all-to-all-start.1 = ((bf16[16,96,2048]{2,1,0:T(8,128)(2,1)}), bf16[16,96,2048]{2,1,0:T(8,128)(2,1)}, u32[]{:S(2)}, u32[]{:S(2)}) async-start(bf16[16,96,2048]{2,1,0:T(8,128)(2,1)} %bitcast.56), calls=%async_computation.1 | async-start | bytes 12582912 | tf_op jit(solution)/shard_map/all_to_all | solution.py:72
  189.8 203.0 %reduce-scatter.2.cloned.1.call-start = ((), (), s32[]{:S(2)}) async-start(), calls=%async_computation.3 | async-start | bytes 9437184 | tf_op jit(solution)/shard_map/reduce_scatter | solution.py:82
  271.2 6.3 %copy-start.1 = (bf16[8,128,16,12]{1,0,3,2:T(8,128)(2,1)S(1)}, bf16[8,128,16,12]{1,0,3,2:T(8,128)(2,1)}, u32[]{:S(2)}) copy-start(bf16[8,128,16,12]{1,0,3,2:T(8,128)(2,1)} %get-tuple-element.6) | copy-start | bytes 1179652
Sparse Core Ops, SparseCore 0:
  9.1 58.0 all-gather.3
  284.0 108.6 reduce-scatter.1

commit v2 on v0

v2 whole, which is shorter than its diff:
```python
import jax
import jax.numpy as jnp
from jax import lax
from jax.sharding import PartitionSpec as P

CHUNKS = 2


def slot_numbers(expert_ids, experts):
    one_hot = (
        expert_ids[:, :, None] == jnp.arange(experts, dtype=jnp.int32)[None, None, :]
    ).astype(jnp.int32)
    return jnp.sum(jnp.cumsum(one_hot, axis=1) * one_hot, axis=2) - 1


def expert_rows(features, w_gate, w_up, w_down, form):
    hidden_form = form[:-1] + "f"
    gate_proj = jnp.einsum(
        form + ",ldf->" + hidden_form, features, w_gate, preferred_element_type=jnp.float32
    )
    up_proj = jnp.einsum(
        form + ",ldf->" + hidden_form, features, w_up, preferred_element_type=jnp.float32
    )
    hidden = (jax.nn.silu(gate_proj) * up_proj).astype(jnp.bfloat16)
    result = jnp.einsum(
        hidden_form + ",lfd->" + form, hidden, w_down, preferred_element_type=jnp.float32
    )
    return result.astype(jnp.bfloat16)


def bf16_part(x):
    return lax.reduce_precision(x, exponent_bits=8, mantissa_bits=7)


def on_device(attn_out, routing, gates, w_gate, w_up, w_down):
    n_ctx = lax.axis_size("ctx")
    n_tp = lax.axis_size("tp")
    me_tp = lax.axis_index("tp")
    exp_dev = w_gate.shape[0]
    experts = exp_dev * n_ctx * n_tp
    tok_blk, top = routing.shape
    cols = attn_out.shape[1]
    width = cols * n_tp
    capacity = 3 * tok_blk * top // (2 * experts)
    per_dest = exp_dev * capacity

    slot_of = slot_numbers(routing.reshape(1, tok_blk * top), experts).reshape(tok_blk, top)
    g1 = bf16_part(gates)
    rest = gates - g1
    g2 = bf16_part(rest)
    g3 = rest - g2
    info = jnp.concatenate(
        [routing.astype(jnp.float32), slot_of.astype(jnp.float32), g1, g2, g3], axis=1
    ).astype(jnp.bfloat16)
    info_cols = 64
    info = jnp.pad(info, ((0, 0), (0, info_cols - info.shape[1])))
    info_rows = tok_blk * info_cols // cols
    info = info.reshape(info_rows, cols)

    blk_chunk = n_tp // CHUNKS
    rows_chunk = blk_chunk * tok_blk
    outs = []
    for h in range(CHUNKS):
        piece = attn_out[h * rows_chunk:(h + 1) * rows_chunk]
        if h == 0:
            piece = jnp.concatenate([piece, info], axis=0)
        gathered = lax.all_gather(piece, "tp", axis=1, tiled=True)
        feats = gathered[:rows_chunk]
        if h == 0:
            info_all = gathered[rows_chunk:].reshape(info_rows, n_tp, cols)
            info_all = jnp.transpose(info_all, (1, 0, 2)).reshape(n_tp, tok_blk, info_cols)
            info_all = info_all.astype(jnp.float32)
            expert_all = info_all[:, :, 0:top].astype(jnp.int32)
            slot_all = info_all[:, :, top:2 * top].astype(jnp.int32)
            gates_all = (
                info_all[:, :, 2 * top:3 * top] + info_all[:, :, 3 * top:4 * top]
            ) + info_all[:, :, 4 * top:5 * top]
            dest_ctx = expert_all // (n_tp * exp_dev)
            dest_tp = (expert_all // exp_dev) % n_tp
            dest_loc = expert_all % exp_dev
            mine = dest_tp == me_tp

        blocks = slice(h * blk_chunk, (h + 1) * blk_chunk)
        b_loc = jnp.arange(blk_chunk, dtype=jnp.int32)[:, None, None]
        position = ((dest_ctx[blocks] * blk_chunk + b_loc) * exp_dev + dest_loc[blocks]) * capacity
        position = jnp.where(mine[blocks], position + slot_all[blocks], -1)
        n_rows = n_ctx * blk_chunk * per_dest
        hits = position[..., None] == jnp.arange(n_rows, dtype=jnp.int32)
        select = jnp.sum(hits.astype(jnp.int32), axis=2).astype(jnp.bfloat16)
        weight = jnp.sum(jnp.where(hits, gates_all[blocks][..., None], 0.0), axis=2)
        select = select.reshape(rows_chunk, n_rows)
        weight = weight.reshape(rows_chunk, n_rows)

        outgoing = jnp.einsum(
            "tr,td->rd", select, feats, preferred_element_type=jnp.bfloat16
        ).reshape(n_ctx, blk_chunk * per_dest, width)
        received = lax.all_to_all(outgoing, "ctx", split_axis=0, concat_axis=0, tiled=True)
        rows = received.reshape(n_ctx * blk_chunk, exp_dev, capacity, width)
        rows = jnp.transpose(rows, (1, 0, 2, 3)).reshape(exp_dev, n_ctx * blk_chunk * capacity, width)
        result = expert_rows(rows, w_gate, w_up, w_down, "lsd")
        result = jnp.transpose(
            result.reshape(exp_dev, n_ctx * blk_chunk, capacity, width), (1, 0, 2, 3)
        ).reshape(n_ctx, blk_chunk * per_dest, width)
        returned = lax.all_to_all(result, "ctx", split_axis=0, concat_axis=0, tiled=True)
        returned = returned.reshape(n_rows, width)

        w_hi_f = bf16_part(weight)
        w_hi = w_hi_f.astype(jnp.bfloat16)
        w_lo = (weight - w_hi_f).astype(jnp.bfloat16)
        partial = jnp.dot(w_hi, returned, preferred_element_type=jnp.float32) + jnp.dot(
            w_lo, returned, preferred_element_type=jnp.float32
        )
        outs.append(lax.psum_scatter(partial, "tp", scatter_dimension=1, tiled=True))
    total = jnp.concatenate(outs, axis=0)
    return total.astype(jnp.bfloat16)


def solution(mesh):
    in_specs = (
        P(("dp", "ctx"), "tp"),
        P(("dp", "ctx", "tp"), None),
        P(("dp", "ctx", "tp"), None),
        P(("dp", "ctx", "tp"), None, None),
        P(("dp", "ctx", "tp"), None, None),
        P(("dp", "ctx", "tp"), None, None),
    )
    out_specs = P(("dp", "ctx"), "tp")
    return jax.shard_map(
        on_device, mesh=mesh, in_specs=in_specs, out_specs=out_specs, check_vma=False
    )
```

time: 548 us -> 384 us (0.70); the launches traced: 540 us -> 382 us
  blocking collectives: 215 us -> 0 us
  local copies, waits for them, and re-layouts: 67.1 us -> 10.8 us
  matrix products: 30.5 us -> 66.2 us
  other arithmetic: 16.6 us -> 47.5 us
  waiting for transfers between devices: 192 us -> 212 us
  starting transfers between devices: 19.2 us -> 32.6 us
  between operations: 0.65 us -> 13.3 us
    all_to_all x2 -> x0, blocking collectives: 215 us -> none  [the longest x1 196 us: on_device(): lax.all_to_all(outgoing, ('ctx', 'tp'), split_axis=0, concat_axis=0, tile...]
    all_to_all x2 -> x4, waiting for transfers between devices: 192 us -> 106 us  [the longest x2 60.5 us: on_device(): lax.all_to_all(outgoing, 'ctx', split_axis=0, concat_axis=0, tiled=True)]
    reduce_scatter x0 -> x2, waiting for transfers between devices: none -> 53.3 us  [on_device(): lax.psum_scatter(partial, 'tp', scatter_dimension=1, tiled=True)]
    all_gather x0 -> x2, waiting for transfers between devices: none -> 51.7 us  [on_device(): gathered = lax.all_gather(piece, 'tp', axis=1, tiled=True)]
    gather x3 -> x0, local copies, waits for them, and re-layouts: 37 us -> none  [the longest x2 24.4 us: fill_buffer(): picked = rows_in[jnp.maximum(slot_table, 0)]]
    reduce_sum x1 -> x2, other arithmetic: 7.33 us -> 28.5 us  [the longest x1 18.3 us: on_device(): select = jnp.sum(hits.astype(jnp.int32), axis=2).astype(jnp.bfloat16)]
    dot_general x1 -> x6, matrix products: 12.5 us -> 30.3 us  [the longest x2 11.6 us: on_device(): jnp.dot(w_lo, returned, preferred_element_type=jnp.float32)]
    dot_general x1 -> x2, matrix products: 5.35 us -> 22.1 us  [expert_rows(): jnp.einsum(hidden_form + ',lfd->' + form, hidden, w_down, preferred_eleme...]
  transfers between devices with their start and end apart: 2 -> 8, of which waited for: 2 -> 6; matrix products, arithmetic and copies ran while one was open for 2% -> 21% of each run, Pallas kernels for 0% -> 0%
where the time goes in v2:
time: 384 us; the launch traced here: 382 us
  waiting for transfers between devices  212 us (55%)
  matrix products  66.2 us (17%)
  other arithmetic  47.5 us (12%)
  starting transfers between devices  32.6 us (8%)
  between operations  13.3 us (3%)
  local copies, waits for them, and re-layouts  10.8 us (3%)
    all_to_all x2, waiting for transfers between devices, on_device(): lax.all_to_all(outgoing, 'ctx', split_axis=0, concat_axis=0, tiled=True)  60.5 us
    reduce_scatter x2, waiting for transfers between devices, on_device(): lax.psum_scatter(partial, 'tp', scatter_dimension=1, tiled=True)  53.3 us
    all_gather x2, waiting for transfers between devices, on_device(): gathered = lax.all_gather(piece, 'tp', axis=1, tiled=True)  51.7 us
    all_to_all x2, waiting for transfers between devices, on_device(): lax.all_to_all(result, 'ctx', split_axis=0, concat_axis=0, tiled=True)  45.9 us
    dot_general x2, matrix products, expert_rows(): jnp.einsum(hidden_form + ',lfd->' + form, hidden, w_down, preferred_eleme...  22.1 us
    reduce_sum x1, other arithmetic, on_device(): select = jnp.sum(hits.astype(jnp.int32), axis=2).astype(jnp.bfloat16)  18.3 us
    all_to_all x2, starting transfers between devices, on_device(): lax.all_to_all(result, 'ctx', split_axis=0, concat_axis=0, tiled=True)  17.8 us
    all_to_all x2, starting transfers between devices, on_device(): lax.all_to_all(outgoing, 'ctx', split_axis=0, concat_axis=0, tiled=True)  14.3 us
  transfers between devices with their start and end apart: 8, of which 6 were waited for; matrix products, arithmetic and copies ran while one was open for 21% of the time, Pallas kernels for 0%

profile of v2, /device:TPU:2, one launch (start us, length us, event | category | flops | bytes accessed | tf_op | source)
XLA Modules:
  0.0 382.4 jit_solution(18399435698486192118)
XLA Ops:
  9.8 1.4 fusion.24
  11.7 1.8 fusion.42
  14.2 51.7 %all-gather.3.cloned.1.call-done = bf16[544,2048]{1,0:T(8,128)(2,1)} async-done(((bf16[544,256]{1,0:T(8,128)(2,1)}), bf16[544,2048]{1,0:T(8,128)(2,1)}) %all-gather.3.cloned.1.call-update) | async-done | bytes 2228240 | tf_op jit(solution)/shard_map/all_gather | solution.py:67
  67.8 3.2 slice_convert_fusion
  71.9 18.3 %convert_reduce_fusion = (s32[4,128,768]{2,1,0:T(8,128)}, s32[4,128,768]{2,1,0:T(8,128)S(1)}) fusion(s32[4,128,8]{2,1,0:T(8,128)S(1)} %get-tuple-element.12, s32[4,128,8]{2,1,0:T(8,128)S(1)} %get-tuple-element.11), kind=kLoop, calls=%fused_computation | loop fusion | flops 18087936 | bytes 3178496 | tf_op jit(solution)/shard_map/reduce_sum | solution.py:89
  91.2 2.3 copy.27
  93.5 5.3 %fusion.10 = bf16[16,48,2048]{2,1,0:T(8,128)(2,1)} fusion(bf16[16,48,512]{2,1,0:T(8,128)(2,1)} %bitcast.93, bf16[544,2048]{1,0:T(8,128)(2,1)} %all-gather.3.cloned.1.call-done), kind=kOutput, calls=%fused_computation.27 | convolution fusion | flops 1610612736 | bytes 6029312 | tf_op jit(solution)/shard_map/tr,td->rd/dot_general | solution.py:94
  98.9 7.3 %all-to-all-start = ((bf16[16,48,2048]{2,1,0:T(8,128)(2,1)}), bf16[16,48,2048]{2,1,0:T(8,128)(2,1)}, u32[]{:S(2)}, u32[]{:S(2)}) async-start(bf16[16,48,2048]{2,1,0:T(8,128)(2,1)} %fusion.10), calls=%async_computation | async-start | bytes 6291456 | tf_op jit(solution)/shard_map/all_to_all | solution.py:97
  106.9 34.5 %all-to-all-done = bf16[16,48,2048]{2,1,0:T(8,128)(2,1)} async-done(((bf16[16,48,2048]{2,1,0:T(8,128)(2,1)}), bf16[16,48,2048]{2,1,0:T(8,128)(2,1)}, u32[]{:S(2)}, u32[]{:S(2)}) %all-to-all-start) | async-done | bytes 3145760 | tf_op jit(solution)/shard_map/all_to_all | solution.py:97
  141.4 6.9 %fusion.4 = f32[768,768]{1,0:T(8,128)} fusion(bf16[768,2048]{1,0:T(8,128)(2,1)} %bitcast.13, bf16[1,2048,768]{2,1,0:T(8,128)(2,1)} %param.10), kind=kOutput, calls=%fused_computation.12 | convolution fusion | flops 2415919104 | bytes 8650752 | tf_op jit(solution)/shard_map/lsd,ldf->lsf/dot_general | solution.py:21
  148.3 11.0 %convolution_convert_fusion.1 = bf16[768,2048]{1,0:T(8,128)(2,1)} fusion(bf16[1,768,2048]{2,1,0:T(8,128)(2,1)S(1)} %copy-done, f32[768,768]{1,0:T(8,128)} %fusion.4, bf16[768,2048]{1,0:T(8,128)(2,1)} %bitcast.13, bf16[1,2048,768]{2,1,0:T(8,128)(2,1)} %param.9), kind=kOutput, calls=%fused_computation.7 | convolution fusion | flops 4836950016 | bytes 14942208 | tf_op jit(solution)/shard_map/lsf,lfd->lsd/dot_general | solution.py:25
  159.3 10.5 %all-to-all-start.1 = ((bf16[16,48,2048]{2,1,0:T(8,128)(2,1)}), bf16[16,48,2048]{2,1,0:T(8,128)(2,1)}, u32[]{:S(2)}, u32[]{:S(2)}) async-start(bf16[16,48,2048]{2,1,0:T(8,128)(2,1)} %bitcast.81), calls=%async_computation.1 | async-start | bytes 6291456 | tf_op jit(solution)/shard_map/all_to_all | solution.py:104
  169.7 2.4 convert_element_type.145
  172.2 2.3 copy.28
  175.6 10.1 %select_reduce_fusion = (f32[4,128,768]{2,1,0:T(8,128)}, f32[4,128,768]{2,1,0:T(8,128)S(1)}) fusion(f32[4,128,8]{2,1,0:T(8,128)S(1)} %get-tuple-element.14, s32[4,128,8]{2,1,0:T(8,128)} %copy-done.4, f32[4,128,8]{2,1,0:T(8,128)S(1)} %get-tuple-element.13, s32[4,128,8]{2,1,0:T(8,128)S(1)} %get-tuple-element.11), kind=kLoop, calls=%fused_computation.1 | loop fusion | flops 18087936 | bytes 3211264 | tf_op jit(solution)/shard_map/reduce_sum | solution.py:90
  185.7 1.5 fusion.17
  187.2 5.3 %fusion.11 = bf16[16,48,2048]{2,1,0:T(8,128)(2,1)} fusion(bf16[16,48,512]{2,1,0:T(8,128)(2,1)} %bitcast.92, bf16[512,2048]{1,0:T(8,128)(2,1)} %all-gather.5.cloned.1.call-done), kind=kOutput, calls=%fused_computation.28 | convolution fusion | flops 1610612736 | bytes 6029312 | tf_op jit(solution)/shard_map/tr,td->rd/dot_general | solution.py:94
  192.5 10.4 %all-to-all-done.1 = bf16[16,48,2048]{2,1,0:T(8,128)(2,1)} async-done(((bf16[16,48,2048]{2,1,0:T(8,128)(2,1)}), bf16[16,48,2048]{2,1,0:T(8,128)(2,1)}, u32[]{:S(2)}, u32[]{:S(2)}) %all-to-all-start.1) | async-done | bytes 3145760 | tf_op jit(solution)/shard_map/all_to_all | solution.py:104
  202.9 7.0 %all-to-all-start.2 = ((bf16[16,48,2048]{2,1,0:T(8,128)(2,1)}), bf16[16,48,2048]{2,1,0:T(8,128)(2,1)}, u32[]{:S(2)}, u32[]{:S(2)}) async-start(bf16[16,48,2048]{2,1,0:T(8,128)(2,1)} %fusion.11), calls=%async_computation.3 | async-start | bytes 6291456 | tf_op jit(solution)/shard_map/all_to_all | solution.py:97
  210.1 4.0 %fusion.43 = f32[512,2048]{1,0:T(8,128)S(1)} fusion(bf16[512,768]{1,0:T(8,128)(2,1)} %bitcast.94, bf16[768,2048]{1,0:T(8,128)(2,1)} %bitcast.18), kind=kOutput, calls=%fused_computation.84 | convolution fusion | flops 1610612736 | bytes 8126464 | tf_op jit(solution)/shard_map/dot_general | solution.py:110
  214.1 5.8 %convolution_add_fusion.1 = f32[512,2048]{1,0:T(8,128)} fusion(f32[512,2048]{1,0:T(8,128)S(1)} %fusion.43, bf16[512,768]{1,0:T(8,128)(2,1)S(1)} %bitcast.83, bf16[768,2048]{1,0:T(8,128)(2,1)} %bitcast.18), kind=kOutput, calls=%fused_computation.19 | convolution fusion | flops 1611661312 | bytes 12320768 | tf_op jit(solution)/shard_map/dot_general | solution.py:110
  219.9 25.9 %all-to-all-done.2 = bf16[16,48,2048]{2,1,0:T(8,128)(2,1)} async-done(((bf16[16,48,2048]{2,1,0:T(8,128)(2,1)}), bf16[16,48,2048]{2,1,0:T(8,128)(2,1)}, u32[]{:S(2)}, u32[]{:S(2)}) %all-to-all-start.2) | async-done | bytes 3145760 | tf_op jit(solution)/shard_map/all_to_all | solution.py:97
  245.9 7.0 %fusion.2 = f32[768,768]{1,0:T(8,128)} fusion(bf16[768,2048]{1,0:T(8,128)(2,1)} %bitcast.25, bf16[1,2048,768]{2,1,0:T(8,128)(2,1)} %param.10), kind=kOutput, calls=%fused_computation.10 | convolution fusion | flops 2415919104 | bytes 8650752 | tf_op jit(solution)/shard_map/lsd,ldf->lsf/dot_general | solution.py:21
  252.9 11.1 %convolution_convert_fusion = bf16[768,2048]{1,0:T(8,128)(2,1)} fusion(bf16[1,768,2048]{2,1,0:T(8,128)(2,1)S(1)} %copy-done, f32[768,768]{1,0:T(8,128)} %fusion.2, bf16[768,2048]{1,0:T(8,128)(2,1)} %bitcast.25, bf16[1,2048,768]{2,1,0:T(8,128)(2,1)} %param.9), kind=kOutput, calls=%fused_computation.6 | convolution fusion | flops 4836950016 | bytes 14942208 | tf_op jit(solution)/shard_map/lsf,lfd->lsd/dot_general | solution.py:25
  264.0 7.4 %all-to-all-start.3 = ((bf16[16,48,2048]{2,1,0:T(8,128)(2,1)}), bf16[16,48,2048]{2,1,0:T(8,128)(2,1)}, u32[]{:S(2)}, u32[]{:S(2)}) async-start(bf16[16,48,2048]{2,1,0:T(8,128)(2,1)} %bitcast.82), calls=%async_computation.4 | async-start | bytes 6291456 | tf_op jit(solution)/shard_map/all_to_all | solution.py:104
  271.4 2.8 fusion.18
  274.1 35.5 %all-to-all-done.3 = bf16[16,48,2048]{2,1,0:T(8,128)(2,1)} async-done(((bf16[16,48,2048]{2,1,0:T(8,128)(2,1)}), bf16[16,48,2048]{2,1,0:T(8,128)(2,1)}, u32[]{:S(2)}, u32[]{:S(2)}) %all-to-all-start.3) | async-done | bytes 3145760 | tf_op jit(solution)/shard_map/all_to_all | solution.py:104
  309.7 4.0 %fusion.44 = f32[512,2048]{1,0:T(8,128)S(1)} fusion(bf16[512,768]{1,0:T(8,128)(2,1)} %bitcast.95, bf16[768,2048]{1,0:T(8,128)(2,1)} %bitcast.27), kind=kOutput, calls=%fused_computation.85 | convolution fusion | flops 1610612736 | bytes 8126464 | tf_op jit(solution)/shard_map/dot_general | solution.py:110
  313.7 5.9 %convolution_add_fusion = f32[512,2048]{1,0:T(8,128)} fusion(f32[512,2048]{1,0:T(8,128)S(1)} %fusion.44, bf16[512,768]{1,0:T(8,128)(2,1)S(1)} %bitcast.84, bf16[768,2048]{1,0:T(8,128)(2,1)} %bitcast.27), kind=kOutput, calls=%fused_computation.18 | convolution fusion | flops 1611661312 | bytes 12320768 | tf_op jit(solution)/shard_map/dot_general | solution.py:110
  319.6 1.1 convert.35
  320.7 53.3 %reduce-scatter.5.cloned.1.call-done = f32[512,256]{1,0:T(8,128)} async-done(((f32[512,2048]{1,0:T(8,128)}), f32[512,256]{1,0:T(8,128)}) %reduce-scatter.5.cloned.1.call-update) | async-done | bytes 524304 | tf_op jit(solution)/shard_map/reduce_scatter | solution.py:113
  373.9 1.1 convert.36
  (52 shorter events, 11.1 us)
Async XLA Ops:
  6.5 141.8 %copy-start = (bf16[1,768,2048]{2,1,0:T(8,128)(2,1)S(1)}, bf16[1,768,2048]{2,1,0:T(8,128)(2,1)}, u32[]{:S(2)}) copy-start(bf16[1,768,2048]{2,1,0:T(8,128)(2,1)} %param.11) | copy-start | bytes 9437188
  6.5 4.8 %copy-start.5 = (f32[128,8]{0,1:T(8,128)S(1)}, f32[128,8]{0,1:T(8,128)}, u32[]{:S(2)}) copy-start(f32[128,8]{0,1:T(8,128)} %param.8) | copy-start | bytes 12292
  6.5 59.4 %all-gather.3.cloned.1.call-start = ((), (), s32[]{:S(2)}) async-start(), calls=%async_computation.6 | async-start | bytes 2506752 | tf_op jit(solution)/shard_map/all_gather | solution.py:67
  67.8 3.3 copy-start.1
  71.9 19.3 %copy-start.4 = (s32[4,128,8]{2,1,0:T(8,128)}, s32[4,128,8]{2,1,0:T(8,128)S(1)}, u32[]{:S(2)}) copy-start(s32[4,128,8]{2,1,0:T(8,128)S(1)} %get-tuple-element.12) | copy-start | bytes 49156
  98.9 42.6 %all-to-all-start = ((bf16[16,48,2048]{2,1,0:T(8,128)(2,1)}), bf16[16,48,2048]{2,1,0:T(8,128)(2,1)}, u32[]{:S(2)}, u32[]{:S(2)}) async-start(bf16[16,48,2048]{2,1,0:T(8,128)(2,1)} %fusion.10), calls=%async_computation | async-start | bytes 6291456 | tf_op jit(solution)/shard_map/all_to_all | solution.py:97
  106.1 81.0 %all-gather.5.cloned.1.call-start = ((), (), s32[]{:S(2)}) async-start(), calls=%async_computation.8 | async-start | bytes 2359296 | tf_op jit(solution)/shard_map/all_gather | solution.py:67
  159.3 43.6 %all-to-all-start.1 = ((bf16[16,48,2048]{2,1,0:T(8,128)(2,1)}), bf16[16,48,2048]{2,1,0:T(8,128)(2,1)}, u32[]{:S(2)}, u32[]{:S(2)}) async-start(bf16[16,48,2048]{2,1,0:T(8,128)(2,1)} %bitcast.81), calls=%async_computation.1 | async-start | bytes 6291456 | tf_op jit(solution)/shard_map/all_to_all | solution.py:104
  202.9 43.0 %all-to-all-start.2 = ((bf16[16,48,2048]{2,1,0:T(8,128)(2,1)}), bf16[16,48,2048]{2,1,0:T(8,128)(2,1)}, u32[]{:S(2)}, u32[]{:S(2)}) async-start(bf16[16,48,2048]{2,1,0:T(8,128)(2,1)} %fusion.11), calls=%async_computation.3 | async-start | bytes 6291456 | tf_op jit(solution)/shard_map/all_to_all | solution.py:97
  209.9 109.7 %reduce-scatter.3.cloned.1.call-start = ((), (), s32[]{:S(2)}) async-start(), calls=%async_computation.7 | async-start | bytes 4718592 | tf_op jit(solution)/shard_map/reduce_scatter | solution.py:113
  210.1 4.0 %copy-start.2 = (bf16[4,128,768]{2,1,0:T(8,128)(2,1)S(1)}, bf16[4,128,768]{2,1,0:T(8,128)(2,1)}, u32[]{:S(2)}) copy-start(bf16[4,128,768]{2,1,0:T(8,128)(2,1)} %get-tuple-element.7) | copy-start | bytes 2359300
  264.0 45.7 %all-to-all-start.3 = ((bf16[16,48,2048]{2,1,0:T(8,128)(2,1)}), bf16[16,48,2048]{2,1,0:T(8,128)(2,1)}, u32[]{:S(2)}, u32[]{:S(2)}) async-start(bf16[16,48,2048]{2,1,0:T(8,128)(2,1)} %bitcast.82), calls=%async_computation.4 | async-start | bytes 6291456 | tf_op jit(solution)/shard_map/all_to_all | solution.py:104
  271.3 102.6 %reduce-scatter.5.cloned.1.call-start = ((), (), s32[]{:S(2)}) async-start(), calls=%async_computation.9 | async-start | bytes 4718592 | tf_op jit(solution)/shard_map/reduce_scatter | solution.py:113
  309.7 4.0 %copy-start.3 = (bf16[4,128,768]{2,1,0:T(8,128)(2,1)S(1)}, bf16[4,128,768]{2,1,0:T(8,128)(2,1)}, u32[]{:S(2)}) copy-start(bf16[4,128,768]{2,1,0:T(8,128)(2,1)} %get-tuple-element.9) | copy-start | bytes 2359300
Sparse Core Ops, SparseCore 0:
  14.3 51.5 all-gather.2
  108.7 45.3 all-gather.4
  220.1 57.2 reduce-scatter.2
  319.7 54.2 reduce-scatter.4

commit v3 on v2

--- a/solution.py
+++ b/solution.py
@@ -84,15 +84,28 @@
         b_loc = jnp.arange(blk_chunk, dtype=jnp.int32)[:, None, None]
         position = ((dest_ctx[blocks] * blk_chunk + b_loc) * exp_dev + dest_loc[blocks]) * capacity
         position = jnp.where(mine[blocks], position + slot_all[blocks], -1)
+        position = jnp.transpose(position.reshape(rows_chunk, top))
+        g_chunk = jnp.transpose(gates_all[blocks].reshape(rows_chunk, top))
+        g_hi_f = bf16_part(g_chunk)
+        g_hi = g_hi_f.astype(jnp.bfloat16)
+        g_lo = (g_chunk - g_hi_f).astype(jnp.bfloat16)
         n_rows = n_ctx * blk_chunk * per_dest
-        hits = position[..., None] == jnp.arange(n_rows, dtype=jnp.int32)
-        select = jnp.sum(hits.astype(jnp.int32), axis=2).astype(jnp.bfloat16)
-        weight = jnp.sum(jnp.where(hits, gates_all[blocks][..., None], 0.0), axis=2)
-        select = select.reshape(rows_chunk, n_rows)
-        weight = weight.reshape(rows_chunk, n_rows)
+        row_ids = jnp.arange(n_rows, dtype=jnp.int32)
+        select = sum(
+            (position[k][None, :] == row_ids[:, None]).astype(jnp.bfloat16) for k in range(top)
+        )
+        zero = jnp.zeros((), jnp.bfloat16)
+        w_hi = sum(
+            jnp.where(position[k][:, None] == row_ids[None, :], g_hi[k][:, None], zero)
+            for k in range(top)
+        )
+        w_lo = sum(
+            jnp.where(position[k][:, None] == row_ids[None, :], g_lo[k][:, None], zero)
+            for k in range(top)
+        )
 
-        outgoing = jnp.einsum(
-            "tr,td->rd", select, feats, preferred_element_type=jnp.bfloat16
+        outgoing = jnp.dot(
+            select, feats, preferred_element_type=jnp.bfloat16
         ).reshape(n_ctx, blk_chunk * per_dest, width)
         received = lax.all_to_all(outgoing, "ctx", split_axis=0, concat_axis=0, tiled=True)
         rows = received.reshape(n_ctx * blk_chunk, exp_dev, capacity, width)
@@ -104,15 +117,12 @@
         returned = lax.all_to_all(result, "ctx", split_axis=0, concat_axis=0, tiled=True)
         returned = returned.reshape(n_rows, width)
 
-        w_hi_f = bf16_part(weight)
-        w_hi = w_hi_f.astype(jnp.bfloat16)
-        w_lo = (weight - w_hi_f).astype(jnp.bfloat16)
         partial = jnp.dot(w_hi, returned, preferred_element_type=jnp.float32) + jnp.dot(
             w_lo, returned, preferred_element_type=jnp.float32
         )
+        partial = partial.astype(jnp.bfloat16)
         outs.append(lax.psum_scatter(partial, "tp", scatter_dimension=1, tiled=True))
-    total = jnp.concatenate(outs, axis=0)
-    return total.astype(jnp.bfloat16)
+    return jnp.concatenate(outs, axis=0)
 
 
 def solution(mesh):

time: 384 us -> 326 us (0.85)
  other arithmetic: 47.5 us -> 10.3 us
  waiting for transfers between devices: 212 us -> 187 us
  matrix products: 66.2 us -> 71.9 us
    all_to_all x2, waiting for transfers between devices: 60.5 us -> 18.1 us  [on_device(): lax.all_to_all(outgoing, 'ctx', split_axis=0, concat_axis=0, tiled=True)]
    reduce_sum x2 -> x0, other arithmetic: 28.5 us -> none  [the longest x1 18.3 us: on_device(): select = jnp.sum(hits.astype(jnp.int32), axis=2).astype(jnp.bfloat16)]
    all_gather x2, waiting for transfers between devices: 51.7 us -> 77.1 us  [on_device(): gathered = lax.all_gather(piece, 'tp', axis=1, tiled=True)]
    convert_element_type x5 -> x2, other arithmetic: 10.9 us -> 0.02 us  [on_device(): g_lo = (g_chunk - g_hi_f).astype(jnp.bfloat16)]
    all_to_all x2, waiting for transfers between devices: 45.9 us -> 41 us  [on_device(): lax.all_to_all(result, 'ctx', split_axis=0, concat_axis=0, tiled=True)]
    dot_general x2 -> x0, local copies, waits for them, and re-layouts: 4.61 us -> none  [on_device(): jnp.einsum('tr,td->rd', select, feats, preferred_element_type=jnp.bfloat16)]
  transfers between devices with their start and end apart: 8 -> 8, of which waited for: 6 -> 8; matrix products, arithmetic and copies ran while one was open for 21% -> 26% of each run, Pallas kernels for 0% -> 0%
where the time goes in v3:
time: 326 us; the launch traced here: 325 us
  waiting for transfers between devices  187 us (57%)
  matrix products  71.9 us (22%)
  starting transfers between devices  32.7 us (10%)
  between operations  13.3 us (4%)
  other arithmetic  10.3 us (3%)
  local copies, waits for them, and re-layouts  9.4 us (3%)
    all_gather x2, waiting for transfers between devices, on_device(): gathered = lax.all_gather(piece, 'tp', axis=1, tiled=True)  77.1 us
    reduce_scatter x2, waiting for transfers between devices, on_device(): lax.psum_scatter(partial, 'tp', scatter_dimension=1, tiled=True)  50.2 us
    all_to_all x2, waiting for transfers between devices, on_device(): lax.all_to_all(result, 'ctx', split_axis=0, concat_axis=0, tiled=True)  41 us
    dot_general x2, matrix products, expert_rows(): jnp.einsum(hidden_form + ',lfd->' + form, hidden, w_down, preferred_eleme...  22 us
    all_to_all x2, waiting for transfers between devices, on_device(): lax.all_to_all(outgoing, 'ctx', split_axis=0, concat_axis=0, tiled=True)  18.1 us
    all_to_all x2, starting transfers between devices, on_device(): lax.all_to_all(outgoing, 'ctx', split_axis=0, concat_axis=0, tiled=True)  17.7 us
    all_to_all x2, starting transfers between devices, on_device(): lax.all_to_all(result, 'ctx', split_axis=0, concat_axis=0, tiled=True)  14.7 us
    dot_general x2, matrix products, expert_rows(): jnp.einsum(form + ',ldf->' + hidden_form, features, w_up, preferred_eleme...  13.7 us
  transfers between devices with their start and end apart: 8, of which 8 were waited for; matrix products, arithmetic and copies ran while one was open for 26% of the time, Pallas kernels for 0%

profile of v3, /device:TPU:2, one launch (start us, length us, event | category | flops | bytes accessed | tf_op | source)
XLA Modules:
  0.0 324.8 jit_solution(1501843523230390404)
XLA Ops:
  6.5 0.9 copy.18
  9.1 1.4 fusion.210
  11.0 1.8 fusion.270
  14.3 51.0 %all-gather.3.cloned.1.call-done = bf16[544,2048]{1,0:T(8,128)(2,1)} async-done(((bf16[544,256]{1,0:T(8,128)(2,1)}), bf16[544,2048]{1,0:T(8,128)(2,1)}) %all-gather.3.cloned.1.call-update) | async-done | bytes 2228240 | tf_op jit(solution)/shard_map/all_gather | solution.py:67
  65.2 0.9 slice_convert_fusion.2
  66.2 0.9 reshape.278
  67.1 3.3 %slice_add_fusion = (f32[8,128,8]{2,1,0:T(8,128)}, s32[8,128,8]{2,1,0:T(8,128)S(1)}) fusion(f32[8,128,64]{2,1,0:T(8,128)} %reshape.278), kind=kLoop, calls=%fused_computation.197 | loop fusion | flops 24576 | bytes 196608 | tf_op jit(solution)/shard_map/add | solution.py:75
  72.0 1.0 copy.24
  73.0 6.1 %fusion.10 = bf16[768,2048]{1,0:T(8,128)(2,1)} fusion(bf16[544,2048]{1,0:T(8,128)(2,1)} %all-gather.3.cloned.1.call-done, s32[512]{0:T(512)S(1)} %bitcast.130, s32[512]{0:T(512)S(1)} %bitcast.133, s32[512]{0:T(512)S(1)} %bitcast.136, s32[512]{0:T(512)S(1)} %bitcast.139, s32[512]{0:T(512)S(1)} %bitcast.142, s32[512]{0:T(512)S(1)} %bitcast.145, ...), kind=kOutput, calls=%fused_computation.16 | convolution fusion | flops 1623195648 | bytes 5259264 | tf_op jit(solution)/shard_map/dot_general | solution.py:107
  79.2 7.3 %all-to-all-start = ((bf16[16,48,2048]{2,1,0:T(8,128)(2,1)}), bf16[16,48,2048]{2,1,0:T(8,128)(2,1)}, u32[]{:S(2)}, u32[]{:S(2)}) async-start(bf16[16,48,2048]{2,1,0:T(8,128)(2,1)} %bitcast.90), calls=%async_computation | async-start | bytes 6291456 | tf_op jit(solution)/shard_map/all_to_all | solution.py:110
  86.6 26.2 %all-gather.5.cloned.1.call-done = bf16[512,2048]{1,0:T(8,128)(2,1)} async-done(((bf16[512,256]{1,0:T(8,128)(2,1)}), bf16[512,2048]{1,0:T(8,128)(2,1)}) %all-gather.5.cloned.1.call-update) | async-done | bytes 2097168 | tf_op jit(solution)/shard_map/all_gather | solution.py:67
  112.7 6.1 %fusion.65 = bf16[768,2048]{1,0:T(8,128)(2,1)} fusion(bf16[512,2048]{1,0:T(8,128)(2,1)} %all-gather.5.cloned.1.call-done, s32[512]{0:T(512)S(1)} %bitcast.106, s32[512]{0:T(512)S(1)} %bitcast.109, s32[512]{0:T(512)S(1)} %bitcast.112, s32[512]{0:T(512)S(1)} %bitcast.115, s32[512]{0:T(512)S(1)} %bitcast.118, s32[512]{0:T(512)S(1)} %bitcast.121, ...), kind=kOutput, calls=%fused_computation.99 | convolution fusion | flops 1623195648 | bytes 5259264 | tf_op jit(solution)/shard_map/dot_general | solution.py:107
  118.8 2.9 all-to-all-done
  121.7 10.4 %all-to-all-start.2 = ((bf16[16,48,2048]{2,1,0:T(8,128)(2,1)}), bf16[16,48,2048]{2,1,0:T(8,128)(2,1)}, u32[]{:S(2)}, u32[]{:S(2)}) async-start(bf16[16,48,2048]{2,1,0:T(8,128)(2,1)} %bitcast.91), calls=%async_computation.3 | async-start | bytes 6291456 | tf_op jit(solution)/shard_map/all_to_all | solution.py:110
  132.2 6.9 %fusion.4 = f32[768,768]{1,0:T(8,128)} fusion(bf16[768,2048]{1,0:T(8,128)(2,1)} %bitcast.21, bf16[1,2048,768]{2,1,0:T(8,128)(2,1)} %param.10), kind=kOutput, calls=%fused_computation.8 | convolution fusion | flops 2415919104 | bytes 8650752 | tf_op jit(solution)/shard_map/lsd,ldf->lsf/dot_general | solution.py:21
  139.0 11.0 %convolution_convert_fusion.1 = bf16[768,2048]{1,0:T(8,128)(2,1)} fusion(bf16[1,768,2048]{2,1,0:T(8,128)(2,1)S(1)} %copy-done, f32[768,768]{1,0:T(8,128)} %fusion.4, bf16[768,2048]{1,0:T(8,128)(2,1)} %bitcast.21, bf16[1,2048,768]{2,1,0:T(8,128)(2,1)} %param.9), kind=kOutput, calls=%fused_computation.3 | convolution fusion | flops 4836950016 | bytes 14942208 | tf_op jit(solution)/shard_map/lsf,lfd->lsd/dot_general | solution.py:25
  150.1 15.1 %all-to-all-done.2 = bf16[16,48,2048]{2,1,0:T(8,128)(2,1)} async-done(((bf16[16,48,2048]{2,1,0:T(8,128)(2,1)}), bf16[16,48,2048]{2,1,0:T(8,128)(2,1)}, u32[]{:S(2)}, u32[]{:S(2)}) %all-to-all-start.2) | async-done | bytes 3145760 | tf_op jit(solution)/shard_map/all_to_all | solution.py:110
  165.2 7.1 %all-to-all-start.1 = ((bf16[16,48,2048]{2,1,0:T(8,128)(2,1)}), bf16[16,48,2048]{2,1,0:T(8,128)(2,1)}, u32[]{:S(2)}, u32[]{:S(2)}) async-start(bf16[16,48,2048]{2,1,0:T(8,128)(2,1)} %bitcast.89), calls=%async_computation.1 | async-start | bytes 6291456 | tf_op jit(solution)/shard_map/all_to_all | solution.py:117
  172.3 1.8 fusion.269
  174.1 1.0 copy.25
  175.3 6.9 %fusion.2 = f32[768,768]{1,0:T(8,128)} fusion(bf16[768,2048]{1,0:T(8,128)(2,1)} %bitcast.40, bf16[1,2048,768]{2,1,0:T(8,128)(2,1)} %param.10), kind=kOutput, calls=%fused_computation.6 | convolution fusion | flops 2415919104 | bytes 8650752 | tf_op jit(solution)/shard_map/lsd,ldf->lsf/dot_general | solution.py:21
  182.1 11.0 %convolution_convert_fusion = bf16[768,2048]{1,0:T(8,128)(2,1)} fusion(bf16[1,768,2048]{2,1,0:T(8,128)(2,1)S(1)} %copy-done, f32[768,768]{1,0:T(8,128)} %fusion.2, bf16[768,2048]{1,0:T(8,128)(2,1)} %bitcast.40, bf16[1,2048,768]{2,1,0:T(8,128)(2,1)} %param.9), kind=kOutput, calls=%fused_computation.2 | convolution fusion | flops 4836950016 | bytes 14942208 | tf_op jit(solution)/shard_map/lsf,lfd->lsd/dot_general | solution.py:25
  193.1 15.2 %all-to-all-done.1 = bf16[16,48,2048]{2,1,0:T(8,128)(2,1)} async-done(((bf16[16,48,2048]{2,1,0:T(8,128)(2,1)}), bf16[16,48,2048]{2,1,0:T(8,128)(2,1)}, u32[]{:S(2)}, u32[]{:S(2)}) %all-to-all-start.1) | async-done | bytes 3145760 | tf_op jit(solution)/shard_map/all_to_all | solution.py:117
  208.3 7.6 %all-to-all-start.3 = ((bf16[16,48,2048]{2,1,0:T(8,128)(2,1)}), bf16[16,48,2048]{2,1,0:T(8,128)(2,1)}, u32[]{:S(2)}, u32[]{:S(2)}) async-start(bf16[16,48,2048]{2,1,0:T(8,128)(2,1)} %bitcast.88), calls=%async_computation.4 | async-start | bytes 6291456 | tf_op jit(solution)/shard_map/all_to_all | solution.py:117
  215.9 5.2 %fusion.102 = f32[512,2048]{1,0:T(8,128)S(1)} fusion(bf16[768,2048]{1,0:T(8,128)(2,1)} %bitcast.26, s32[512]{0:T(512)S(1)} %bitcast.131, s32[512]{0:T(512)S(1)} %bitcast.134, s32[512]{0:T(512)S(1)} %bitcast.137, s32[512]{0:T(512)S(1)} %bitcast.140, s32[512]{0:T(512)S(1)} %bitcast.143, s32[512]{0:T(512)S(1)} %bitcast.146, s32[512]{0:T(512)S(1)} %bitcast.149, ...), kind=kOutput, calls=%fused_computation.120 | convolution fusion | flops 1623195648 | bytes 7364608 | tf_op jit(solution)/shard_map/dot_general | solution.py:120
  221.1 6.7 %add_convert_fusion.1 = bf16[512,2048]{1,0:T(8,128)(2,1)} fusion(f32[512,2048]{1,0:T(8,128)S(1)} %fusion.102, bf16[768,2048]{1,0:T(8,128)(2,1)} %bitcast.26, s32[512]{0:T(512)S(1)} %bitcast.132, s32[512]{0:T(512)S(1)} %bitcast.135, s32[512]{0:T(512)S(1)} %bitcast.138, s32[512]{0:T(512)S(1)} %bitcast.141, s32[512]{0:T(512)S(1)} %bitcast.144, ...), kind=kOutput, calls=%fused_computation.1 | convolution fusion | flops 1625292800 | bytes 9461760 | tf_op jit(solution)/shard_map/dot_general | solution.py:120
  228.4 25.8 %all-to-all-done.3 = bf16[16,48,2048]{2,1,0:T(8,128)(2,1)} async-done(((bf16[16,48,2048]{2,1,0:T(8,128)(2,1)}), bf16[16,48,2048]{2,1,0:T(8,128)(2,1)}, u32[]{:S(2)}, u32[]{:S(2)}) %all-to-all-start.3) | async-done | bytes 3145760 | tf_op jit(solution)/shard_map/all_to_all | solution.py:117
  254.1 5.2 %fusion.133 = f32[512,2048]{1,0:T(8,128)S(1)} fusion(bf16[768,2048]{1,0:T(8,128)(2,1)} %bitcast.42, s32[512]{0:T(512)S(1)} %bitcast.107, s32[512]{0:T(512)S(1)} %bitcast.110, s32[512]{0:T(512)S(1)} %bitcast.113, s32[512]{0:T(512)S(1)} %bitcast.116, s32[512]{0:T(512)S(1)} %bitcast.119, s32[512]{0:T(512)S(1)} %bitcast.122, s32[512]{0:T(512)S(1)} %bitcast.125, ...), kind=kOutput, calls=%fused_computation.135 | convolution fusion | flops 1623195648 | bytes 7364608 | tf_op jit(solution)/shard_map/dot_general | solution.py:120
  259.3 6.8 %add_convert_fusion = bf16[512,2048]{1,0:T(8,128)(2,1)} fusion(f32[512,2048]{1,0:T(8,128)S(1)} %fusion.133, bf16[768,2048]{1,0:T(8,128)(2,1)} %bitcast.42, s32[512]{0:T(512)S(1)} %bitcast.108, s32[512]{0:T(512)S(1)} %bitcast.111, s32[512]{0:T(512)S(1)} %bitcast.114, s32[512]{0:T(512)S(1)} %bitcast.117, s32[512]{0:T(512)S(1)} %bitcast.120, ...), kind=kOutput, calls=%fused_computation | convolution fusion | flops 1625292800 | bytes 9461760 | tf_op jit(solution)/shard_map/dot_general | solution.py:120
  266.2 6.3 %reduce-scatter.3.cloned.1.call-done = bf16[512,256]{1,0:T(8,128)(2,1)} async-done(((bf16[512,2048]{1,0:T(8,128)(2,1)}), bf16[512,256]{1,0:T(8,128)(2,1)}) %reduce-scatter.3.cloned.1.call-update) | async-done | bytes 262160 | tf_op jit(solution)/shard_map/reduce_scatter | solution.py:124
  272.5 43.9 %reduce-scatter.5.cloned.1.call-done = bf16[512,256]{1,0:T(8,128)(2,1)} async-done(((bf16[512,2048]{1,0:T(8,128)(2,1)}), bf16[512,256]{1,0:T(8,128)(2,1)}) %reduce-scatter.5.cloned.1.call-update) | async-done | bytes 262160 | tf_op jit(solution)/shard_map/reduce_scatter | solution.py:124
  316.4 1.9 pad_maximum_fusion
  (48 shorter events, 5.9 us)
Async XLA Ops:
  6.5 132.5 %copy-start = (bf16[1,768,2048]{2,1,0:T(8,128)(2,1)S(1)}, bf16[1,768,2048]{2,1,0:T(8,128)(2,1)}, u32[]{:S(2)}) copy-start(bf16[1,768,2048]{2,1,0:T(8,128)(2,1)} %param.11) | copy-start | bytes 9437188
  6.5 2.5 copy-start.3
  6.5 58.7 %all-gather.3.cloned.1.call-start = ((), (), s32[]{:S(2)}) async-start(), calls=%async_computation.6 | async-start | bytes 2506752 | tf_op jit(solution)/shard_map/all_gather | solution.py:67
  8.1 2.6 copy-start.2
  13.5 99.2 %all-gather.5.cloned.1.call-start = ((), (), s32[]{:S(2)}) async-start(), calls=%async_computation.8 | async-start | bytes 2359296 | tf_op jit(solution)/shard_map/all_gather | solution.py:67
  67.1 3.3 %copy-start.1 = (f32[8,128,64]{2,1,0:T(8,128)S(1)}, f32[8,128,64]{2,1,0:T(8,128)}, u32[]{:S(2)}) copy-start(f32[8,128,64]{2,1,0:T(8,128)} %reshape.278) | copy-start | bytes 786436
  79.2 42.6 %all-to-all-start = ((bf16[16,48,2048]{2,1,0:T(8,128)(2,1)}), bf16[16,48,2048]{2,1,0:T(8,128)(2,1)}, u32[]{:S(2)}, u32[]{:S(2)}) async-start(bf16[16,48,2048]{2,1,0:T(8,128)(2,1)} %bitcast.90), calls=%async_computation | async-start | bytes 6291456 | tf_op jit(solution)/shard_map/all_to_all | solution.py:110
  121.7 43.5 %all-to-all-start.2 = ((bf16[16,48,2048]{2,1,0:T(8,128)(2,1)}), bf16[16,48,2048]{2,1,0:T(8,128)(2,1)}, u32[]{:S(2)}, u32[]{:S(2)}) async-start(bf16[16,48,2048]{2,1,0:T(8,128)(2,1)} %bitcast.91), calls=%async_computation.3 | async-start | bytes 6291456 | tf_op jit(solution)/shard_map/all_to_all | solution.py:110
  165.2 43.1 %all-to-all-start.1 = ((bf16[16,48,2048]{2,1,0:T(8,128)(2,1)}), bf16[16,48,2048]{2,1,0:T(8,128)(2,1)}, u32[]{:S(2)}, u32[]{:S(2)}) async-start(bf16[16,48,2048]{2,1,0:T(8,128)(2,1)} %bitcast.89), calls=%async_computation.1 | async-start | bytes 6291456 | tf_op jit(solution)/shard_map/all_to_all | solution.py:117
  208.3 45.9 %all-to-all-start.3 = ((bf16[16,48,2048]{2,1,0:T(8,128)(2,1)}), bf16[16,48,2048]{2,1,0:T(8,128)(2,1)}, u32[]{:S(2)}, u32[]{:S(2)}) async-start(bf16[16,48,2048]{2,1,0:T(8,128)(2,1)} %bitcast.88), calls=%async_computation.4 | async-start | bytes 6291456 | tf_op jit(solution)/shard_map/all_to_all | solution.py:117
  215.8 56.6 %reduce-scatter.3.cloned.1.call-start = ((), (), s32[]{:S(2)}) async-start(), calls=%async_computation.7 | async-start | bytes 2359296 | tf_op jit(solution)/shard_map/reduce_scatter | solution.py:124
  227.8 88.6 %reduce-scatter.5.cloned.1.call-start = ((), (), s32[]{:S(2)}) async-start(), calls=%async_computation.9 | async-start | bytes 2359296 | tf_op jit(solution)/shard_map/reduce_scatter | solution.py:124
Sparse Core Ops, SparseCore 0:
  13.6 51.5 all-gather.2
  67.0 45.7 all-gather.4
  228.0 44.4 reduce-scatter.2
  274.9 41.4 reduce-scatter.4

commit v4 on v3

--- a/solution.py
+++ b/solution.py
@@ -60,15 +60,15 @@
     blk_chunk = n_tp // CHUNKS
     rows_chunk = blk_chunk * tok_blk
     outs = []
+    partials = []
     for h in range(CHUNKS):
         piece = attn_out[h * rows_chunk:(h + 1) * rows_chunk]
         if h == 0:
             piece = jnp.concatenate([piece, info], axis=0)
-        gathered = lax.all_gather(piece, "tp", axis=1, tiled=True)
-        feats = gathered[:rows_chunk]
+        gathered = lax.all_gather(piece, "tp", axis=0)
+        feats = jnp.transpose(gathered[:, :rows_chunk], (1, 0, 2)).reshape(rows_chunk, width)
         if h == 0:
-            info_all = gathered[rows_chunk:].reshape(info_rows, n_tp, cols)
-            info_all = jnp.transpose(info_all, (1, 0, 2)).reshape(n_tp, tok_blk, info_cols)
+            info_all = gathered[:, rows_chunk:].reshape(n_tp, tok_blk, info_cols)
             info_all = info_all.astype(jnp.float32)
             expert_all = info_all[:, :, 0:top].astype(jnp.int32)
             slot_all = info_all[:, :, top:2 * top].astype(jnp.int32)
@@ -95,14 +95,13 @@
             (position[k][None, :] == row_ids[:, None]).astype(jnp.bfloat16) for k in range(top)
         )
         zero = jnp.zeros((), jnp.bfloat16)
-        w_hi = sum(
-            jnp.where(position[k][:, None] == row_ids[None, :], g_hi[k][:, None], zero)
-            for k in range(top)
-        )
-        w_lo = sum(
-            jnp.where(position[k][:, None] == row_ids[None, :], g_lo[k][:, None], zero)
-            for k in range(top)
-        )
+        w_both = jnp.concatenate([
+            sum(
+                jnp.where(position[k][:, None] == row_ids[None, :], g_part[k][:, None], zero)
+                for k in range(top)
+            )
+            for g_part in (g_hi, g_lo)
+        ], axis=1)
 
         outgoing = jnp.dot(
             select, feats, preferred_element_type=jnp.bfloat16
@@ -111,17 +110,20 @@
         rows = received.reshape(n_ctx * blk_chunk, exp_dev, capacity, width)
         rows = jnp.transpose(rows, (1, 0, 2, 3)).reshape(exp_dev, n_ctx * blk_chunk * capacity, width)
         result = expert_rows(rows, w_gate, w_up, w_down, "lsd")
+        if h > 0:
+            result, earlier = lax.optimization_barrier((result, partials[-1]))
+            outs.append(lax.psum_scatter(earlier, "tp", scatter_dimension=1, tiled=True))
         result = jnp.transpose(
             result.reshape(exp_dev, n_ctx * blk_chunk, capacity, width), (1, 0, 2, 3)
         ).reshape(n_ctx, blk_chunk * per_dest, width)
         returned = lax.all_to_all(result, "ctx", split_axis=0, concat_axis=0, tiled=True)
         returned = returned.reshape(n_rows, width)
 
-        partial = jnp.dot(w_hi, returned, preferred_element_type=jnp.float32) + jnp.dot(
-            w_lo, returned, preferred_element_type=jnp.float32
-        )
-        partial = partial.astype(jnp.bfloat16)
-        outs.append(lax.psum_scatter(partial, "tp", scatter_dimension=1, tiled=True))
+        partial = jnp.dot(
+            w_both, jnp.concatenate([returned, returned], axis=0), preferred_element_type=jnp.float32
+        ).astype(jnp.bfloat16)
+        partials.append(partial)
+    outs.append(lax.psum_scatter(partials[-1], "tp", scatter_dimension=1, tiled=True))
     return jnp.concatenate(outs, axis=0)
 
 

time: 326 us -> 325 us (level)
  waiting for transfers between devices: 187 us -> 167 us
  local copies, waits for them, and re-layouts: 9.4 us -> 26.2 us
  other arithmetic: 10.3 us -> 20.5 us
  matrix products: 71.9 us -> 64 us
    all_gather x2, waiting for transfers between devices: 77.1 us -> 55.4 us  [on_device(): gathered = lax.all_gather(piece, 'tp', axis=0)]
    add x0 -> x4, other arithmetic: none -> 10.2 us  [on_device(): sum((jnp.where(position[k][:, None] == row_ids[None, :], g_part[k][:, Non...]
    reshape x0 -> x2, local copies, waits for them, and re-layouts: none -> 8.42 us  [on_device(): jnp.transpose(gathered[:, :rows_chunk], (1, 0, 2))]
    reduce_scatter x2, waiting for transfers between devices: 50.2 us -> 42 us  [the longest x1 42 us: on_device(): lax.psum_scatter(partials[-1], 'tp', scatter_dimension=1, tiled=True)]
    dot_general x4 -> x2, matrix products: 24 us -> 16.4 us  [on_device(): jnp.dot(w_both, jnp.concatenate([returned, returned], axis=0), preferred_...]
    all_to_all x2, waiting for transfers between devices: 18.1 us -> 23.8 us  [on_device(): lax.all_to_all(outgoing, 'ctx', split_axis=0, concat_axis=0, tiled=True)]
    transpose x0 -> x2, local copies, waits for them, and re-layouts: none -> 4.23 us  [on_device(): jnp.transpose(gathered[:, :rows_chunk], (1, 0, 2))]
    all_gather x0 -> x1, local copies, waits for them, and re-layouts: none -> 4.16 us  [on_device(): gathered = lax.all_gather(piece, 'tp', axis=0)]
  transfers between devices with their start and end apart: 8 -> 8, of which waited for: 8 -> 7; matrix products, arithmetic and copies ran while one was open for 26% -> 29% of each run, Pallas kernels for 0% -> 0%
where the time goes in v4:
time: 325 us; the launch traced here: 324 us
  waiting for transfers between devices  167 us (51%)
  matrix products  64 us (20%)
  starting transfers between devices  33.2 us (10%)
  local copies, waits for them, and re-layouts  26.2 us (8%)
  other arithmetic  20.5 us (6%)
  between operations  13.3 us (4%)
    all_gather x2, waiting for transfers between devices, on_device(): gathered = lax.all_gather(piece, 'tp', axis=0)  55.4 us
    all_to_all x2, waiting for transfers between devices, on_device(): lax.all_to_all(result, 'ctx', split_axis=0, concat_axis=0, tiled=True)  44.8 us
    reduce_scatter x1, waiting for transfers between devices, on_device(): lax.psum_scatter(partials[-1], 'tp', scatter_dimension=1, tiled=True)  42 us
    all_to_all x2, waiting for transfers between devices, on_device(): lax.all_to_all(outgoing, 'ctx', split_axis=0, concat_axis=0, tiled=True)  23.8 us
    dot_general x2, matrix products, expert_rows(): jnp.einsum(hidden_form + ',lfd->' + form, hidden, w_down, preferred_eleme...  22 us
    all_to_all x2, starting transfers between devices, on_device(): lax.all_to_all(outgoing, 'ctx', split_axis=0, concat_axis=0, tiled=True)  16.4 us
    dot_general x2, matrix products, on_device(): jnp.dot(w_both, jnp.concatenate([returned, returned], axis=0), preferred_...  16.4 us
    all_to_all x2, starting transfers between devices, on_device(): lax.all_to_all(result, 'ctx', split_axis=0, concat_axis=0, tiled=True)  16.2 us
  transfers between devices with their start and end apart: 8, of which 7 were waited for; matrix products, arithmetic and copies ran while one was open for 29% of the time, Pallas kernels for 0%

profile of v4, /device:TPU:2, one launch (start us, length us, event | category | flops | bytes accessed | tf_op | source)
XLA Modules:
  0.0 323.9 jit_solution(9202737835228953843)
XLA Ops:
  11.0 1.8 fusion.160
  14.3 43.5 %all-gather.5.cloned.1.call-done = bf16[4352,256]{1,0:T(8,128)(2,1)} async-done(((bf16[544,256]{1,0:T(8,128)(2,1)}), bf16[4352,256]{1,0:T(8,128)(2,1)}) %all-gather.5.cloned.1.call-update) | async-done | bytes 2228240 | tf_op jit(solution)/shard_map/all_gather | solution.py:68
  59.7 3.3 %slice_add_fusion = (f32[8,128,8]{2,1,0:T(8,128)}, s32[8,128,8]{2,1,0:T(8,128)S(1)}) fusion(f32[8,128,64]{2,1,0:T(8,128)} %reshape.476), kind=kLoop, calls=%fused_computation.165 | loop fusion | flops 24576 | bytes 196608 | tf_op jit(solution)/shard_map/add | solution.py:75
  65.5 1.7 slice_bitcast_fusion
  67.3 2.5 copy.30
  69.8 4.2 %reshape.480 = bf16[512,2048,1]{1,0,2:T(8,128)(2,1)} reshape(bf16[512,8,256]{2,1,0:T(8,128)(2,1)} %copy.30) | data formatting | bytes 4194304 | tf_op jit(solution)/shard_map/reshape | solution.py:69
  74.0 6.0 %fusion.85 = bf16[16,48,2048]{2,1,0:T(8,128)(2,1)} fusion(bf16[512,2048,1]{1,0,2:T(8,128)(2,1)} %reshape.480, s32[512]{0:T(512)S(1)} %bitcast.129, s32[512]{0:T(512)S(1)} %bitcast.132, s32[512]{0:T(512)S(1)} %bitcast.135, s32[512]{0:T(512)S(1)} %bitcast.138, s32[512]{0:T(512)S(1)} %bitcast.141, s32[512]{0:T(512)S(1)} %bitcast.144, s32[512]{0:T(512)S(1)} %bitcast.147, ...), kind=kOutput, calls=%fused_computation.112 | convolution fusion | flops 1619656704 | bytes 5262336 | tf_op jit(solution)/shard_map/dot_general | solution.py:106
  80.0 7.3 %all-to-all-start.1 = ((bf16[16,48,2048]{2,1,0:T(8,128)(2,1)}), bf16[16,48,2048]{2,1,0:T(8,128)(2,1)}, u32[]{:S(2)}, u32[]{:S(2)}) async-start(bf16[16,48,2048]{2,1,0:T(8,128)(2,1)} %fusion.85), calls=%async_computation.1 | async-start | bytes 6291456 | tf_op jit(solution)/shard_map/all_to_all | solution.py:109
  87.2 11.9 %all-gather.7.cloned.1.call-done = bf16[4096,256]{1,0:T(8,128)(2,1)} async-done(((bf16[512,256]{1,0:T(8,128)(2,1)}), bf16[4096,256]{1,0:T(8,128)(2,1)}) %all-gather.7.cloned.1.call-update) | async-done | bytes 2097168 | tf_op jit(solution)/shard_map/all_gather | solution.py:68
  99.1 4.2 %copy.36 = bf16[8,512,256]{2,0,1:T(8,128)(2,1)} copy(bf16[8,512,256]{2,1,0:T(8,128)(2,1)} %bitcast.92) | data formatting | bytes 4194304 | tf_op jit(solution)/shard_map/all_gather | solution.py:68
  103.3 4.2 %reshape.479 = bf16[512,2048,1]{1,0,2:T(8,128)(2,1)} reshape(bf16[512,8,256]{2,1,0:T(8,128)(2,1)} %bitcast.87) | data formatting | bytes 4194304 | tf_op jit(solution)/shard_map/reshape | solution.py:69
  107.6 5.9 %fusion.76 = bf16[16,48,2048]{2,1,0:T(8,128)(2,1)} fusion(bf16[512,2048,1]{1,0,2:T(8,128)(2,1)} %reshape.479, s32[512]{0:T(512)S(1)} %bitcast.105, s32[512]{0:T(512)S(1)} %bitcast.108, s32[512]{0:T(512)S(1)} %bitcast.111, s32[512]{0:T(512)S(1)} %bitcast.114, s32[512]{0:T(512)S(1)} %bitcast.117, s32[512]{0:T(512)S(1)} %bitcast.120, s32[512]{0:T(512)S(1)} %bitcast.123, ...), kind=kOutput, calls=%fused_computation.104 | convolution fusion | flops 1619656704 | bytes 5262336 | tf_op jit(solution)/shard_map/dot_general | solution.py:106
  113.5 8.9 %all-to-all-done.1 = bf16[16,48,2048]{2,1,0:T(8,128)(2,1)} async-done(((bf16[16,48,2048]{2,1,0:T(8,128)(2,1)}), bf16[16,48,2048]{2,1,0:T(8,128)(2,1)}, u32[]{:S(2)}, u32[]{:S(2)}) %all-to-all-start.1) | async-done | bytes 3145760 | tf_op jit(solution)/shard_map/all_to_all | solution.py:109
  122.4 9.1 %all-to-all-start = ((bf16[16,48,2048]{2,1,0:T(8,128)(2,1)}), bf16[16,48,2048]{2,1,0:T(8,128)(2,1)}, u32[]{:S(2)}, u32[]{:S(2)}) async-start(bf16[16,48,2048]{2,1,0:T(8,128)(2,1)} %fusion.76), calls=%async_computation | async-start | bytes 6291456 | tf_op jit(solution)/shard_map/all_to_all | solution.py:109
  131.6 1.8 fusion.159
  134.4 6.9 %fusion.10 = f32[768,768]{1,0:T(8,128)} fusion(bf16[768,2048]{1,0:T(8,128)(2,1)} %bitcast.38, bf16[1,2048,768]{2,1,0:T(8,128)(2,1)} %param.10), kind=kOutput, calls=%fused_computation.12 | convolution fusion | flops 2415919104 | bytes 8650752 | tf_op jit(solution)/shard_map/lsd,ldf->lsf/dot_general | solution.py:21
  141.3 11.0 %convolution_convert_fusion = bf16[768,2048]{1,0:T(8,128)(2,1)} fusion(bf16[1,768,2048]{2,1,0:T(8,128)(2,1)S(1)} %copy-done, f32[768,768]{1,0:T(8,128)} %fusion.10, bf16[768,2048]{1,0:T(8,128)(2,1)} %bitcast.38, bf16[1,2048,768]{2,1,0:T(8,128)(2,1)} %param.9), kind=kOutput, calls=%fused_computation.8 | convolution fusion | flops 4836950016 | bytes 14942208 | tf_op jit(solution)/shard_map/lsf,lfd->lsd/dot_general | solution.py:25
  152.3 14.9 %all-to-all-done = bf16[16,48,2048]{2,1,0:T(8,128)(2,1)} async-done(((bf16[16,48,2048]{2,1,0:T(8,128)(2,1)}), bf16[16,48,2048]{2,1,0:T(8,128)(2,1)}, u32[]{:S(2)}, u32[]{:S(2)}) %all-to-all-start) | async-done | bytes 3145760 | tf_op jit(solution)/shard_map/all_to_all | solution.py:109
  167.2 8.3 %all-to-all-start.2 = ((bf16[16,48,2048]{2,1,0:T(8,128)(2,1)}), bf16[16,48,2048]{2,1,0:T(8,128)(2,1)}, u32[]{:S(2)}, u32[]{:S(2)}) async-start(bf16[16,48,2048]{2,1,0:T(8,128)(2,1)} %bitcast.89), calls=%async_computation.2 | async-start | bytes 6291456 | tf_op jit(solution)/shard_map/all_to_all | solution.py:119
  175.8 2.6 fusion.93
  178.4 2.5 fusion.100
  180.9 6.9 %fusion.12 = f32[768,768]{1,0:T(8,128)} fusion(bf16[768,2048]{1,0:T(8,128)(2,1)} %bitcast.20, bf16[1,2048,768]{2,1,0:T(8,128)(2,1)} %param.10), kind=kOutput, calls=%fused_computation.14 | convolution fusion | flops 2415919104 | bytes 8650752 | tf_op jit(solution)/shard_map/lsd,ldf->lsf/dot_general | solution.py:21
  187.8 11.0 %fusion.18 = bf16[1,768,2048]{2,1,0:T(8,128)(2,1)} fusion(bf16[1,768,2048]{2,1,0:T(8,128)(2,1)S(1)} %copy-done, f32[768,768]{1,0:T(8,128)} %fusion.12, bf16[768,2048]{1,0:T(8,128)(2,1)} %bitcast.20, bf16[1,2048,768]{2,1,0:T(8,128)(2,1)} %param.9), kind=kOutput, calls=%fused_computation.20 | convolution fusion | flops 4836950016 | bytes 14942208 | tf_op jit(solution)/shard_map/lsf,lfd->lsd/dot_general | solution.py:25
  198.8 14.8 %all-to-all-done.2 = bf16[16,48,2048]{2,1,0:T(8,128)(2,1)} async-done(((bf16[16,48,2048]{2,1,0:T(8,128)(2,1)}), bf16[16,48,2048]{2,1,0:T(8,128)(2,1)}, u32[]{:S(2)}, u32[]{:S(2)}) %all-to-all-start.2) | async-done | bytes 3145760 | tf_op jit(solution)/shard_map/all_to_all | solution.py:119
  213.6 8.1 %fusion.24 = bf16[512,2048]{1,0:T(8,128)(2,1)} fusion(bf16[768,2048]{1,0:T(8,128)(2,1)} %bitcast.40, bf16[512,768]{1,0:T(8,128)(2,1)} %fusion.100, bf16[512,768]{1,0:T(8,128)(2,1)} %fusion.93), kind=kOutput, calls=%fused_computation.22 | convolution fusion | flops 3238002688 | bytes 6815744 | tf_op jit(solution)/shard_map/dot_general | solution.py:122
  221.7 7.9 %all-to-all-start.3 = ((bf16[16,48,2048]{2,1,0:T(8,128)(2,1)}), bf16[16,48,2048]{2,1,0:T(8,128)(2,1)}, u32[]{:S(2)}, u32[]{:S(2)}) async-start(bf16[16,48,2048]{2,1,0:T(8,128)(2,1)} %bitcast.88), calls=%async_computation.4 | async-start | bytes 6291456 | tf_op jit(solution)/shard_map/all_to_all | solution.py:119
  230.1 2.6 fusion.107
  232.7 2.5 fusion.114
  235.2 30.0 %all-to-all-done.3 = bf16[16,48,2048]{2,1,0:T(8,128)(2,1)} async-done(((bf16[16,48,2048]{2,1,0:T(8,128)(2,1)}), bf16[16,48,2048]{2,1,0:T(8,128)(2,1)}, u32[]{:S(2)}, u32[]{:S(2)}) %all-to-all-start.3) | async-done | bytes 3145760 | tf_op jit(solution)/shard_map/all_to_all | solution.py:119
  265.2 8.3 %fusion.21 = bf16[512,2048]{1,0:T(8,128)(2,1)} fusion(bf16[768,2048]{1,0:T(8,128)(2,1)} %bitcast.44, bf16[512,768]{1,0:T(8,128)(2,1)} %fusion.114, bf16[512,768]{1,0:T(8,128)(2,1)} %fusion.107), kind=kOutput, calls=%fused_computation.21 | convolution fusion | flops 3238002688 | bytes 6815744 | tf_op jit(solution)/shard_map/dot_general | solution.py:122
  273.6 42.0 %reduce-scatter.5.cloned.1.call-done = bf16[512,256]{1,0:T(8,128)(2,1)} async-done(((bf16[512,2048]{1,0:T(8,128)(2,1)}), bf16[512,256]{1,0:T(8,128)(2,1)}) %reduce-scatter.5.cloned.1.call-update) | async-done | bytes 262160 | tf_op jit(solution)/shard_map/reduce_scatter | solution.py:126
  315.6 1.9 pad_maximum_fusion
  (55 shorter events, 12.4 us)
Async XLA Ops:
  6.5 134.7 %copy-start = (bf16[1,768,2048]{2,1,0:T(8,128)(2,1)S(1)}, bf16[1,768,2048]{2,1,0:T(8,128)(2,1)}, u32[]{:S(2)}) copy-start(bf16[1,768,2048]{2,1,0:T(8,128)(2,1)} %param.11) | copy-start | bytes 9437188
  6.5 2.5 copy-start.3
  6.5 51.3 %all-gather.5.cloned.1.call-start = ((), (), s32[]{:S(2)}) async-start(), calls=%async_computation.8 | async-start | bytes 2506752 | tf_op jit(solution)/shard_map/all_gather | solution.py:68
  8.1 2.6 copy-start.2
  13.5 85.6 %all-gather.7.cloned.1.call-start = ((), (), s32[]{:S(2)}) async-start(), calls=%async_computation.9 | async-start | bytes 2359296 | tf_op jit(solution)/shard_map/all_gather | solution.py:68
  59.7 3.3 %copy-start.1 = (f32[8,128,64]{2,1,0:T(8,128)S(1)}, f32[8,128,64]{2,1,0:T(8,128)}, u32[]{:S(2)}) copy-start(f32[8,128,64]{2,1,0:T(8,128)} %reshape.476) | copy-start | bytes 786436
  80.0 42.5 %all-to-all-start.1 = ((bf16[16,48,2048]{2,1,0:T(8,128)(2,1)}), bf16[16,48,2048]{2,1,0:T(8,128)(2,1)}, u32[]{:S(2)}, u32[]{:S(2)}) async-start(bf16[16,48,2048]{2,1,0:T(8,128)(2,1)} %fusion.85), calls=%async_computation.1 | async-start | bytes 6291456 | tf_op jit(solution)/shard_map/all_to_all | solution.py:109
  122.4 44.8 %all-to-all-start = ((bf16[16,48,2048]{2,1,0:T(8,128)(2,1)}), bf16[16,48,2048]{2,1,0:T(8,128)(2,1)}, u32[]{:S(2)}, u32[]{:S(2)}) async-start(bf16[16,48,2048]{2,1,0:T(8,128)(2,1)} %fusion.76), calls=%async_computation | async-start | bytes 6291456 | tf_op jit(solution)/shard_map/all_to_all | solution.py:109
  167.2 46.4 %all-to-all-start.2 = ((bf16[16,48,2048]{2,1,0:T(8,128)(2,1)}), bf16[16,48,2048]{2,1,0:T(8,128)(2,1)}, u32[]{:S(2)}, u32[]{:S(2)}) async-start(bf16[16,48,2048]{2,1,0:T(8,128)(2,1)} %bitcast.89), calls=%async_computation.2 | async-start | bytes 6291456 | tf_op jit(solution)/shard_map/all_to_all | solution.py:119
  175.4 98.2 %reduce-scatter.3.cloned.1.call-start = ((), (), s32[]{:S(2)}) async-start(), calls=%async_computation.6 | async-start | bytes 2359296 | tf_op jit(solution)/shard_map/reduce_scatter | solution.py:115
  221.7 43.5 %all-to-all-start.3 = ((bf16[16,48,2048]{2,1,0:T(8,128)(2,1)}), bf16[16,48,2048]{2,1,0:T(8,128)(2,1)}, u32[]{:S(2)}, u32[]{:S(2)}) async-start(bf16[16,48,2048]{2,1,0:T(8,128)(2,1)} %bitcast.88), calls=%async_computation.4 | async-start | bytes 6291456 | tf_op jit(solution)/shard_map/all_to_all | solution.py:119
  229.6 86.0 %reduce-scatter.5.cloned.1.call-start = ((), (), s32[]{:S(2)}) async-start(), calls=%async_computation.7 | async-start | bytes 2359296 | tf_op jit(solution)/shard_map/reduce_scatter | solution.py:126
Sparse Core Ops, SparseCore 0:
  13.6 44.1 all-gather.4
  59.6 39.4 all-gather.6
  221.8 40.3 reduce-scatter.2
  273.7 41.8 reduce-scatter.4

commit v5 on v4

--- a/solution.py
+++ b/solution.py
@@ -101,7 +101,7 @@
                 for k in range(top)
             )
             for g_part in (g_hi, g_lo)
-        ], axis=1)
+        ], axis=0)
 
         outgoing = jnp.dot(
             select, feats, preferred_element_type=jnp.bfloat16
@@ -119,9 +119,8 @@
         returned = lax.all_to_all(result, "ctx", split_axis=0, concat_axis=0, tiled=True)
         returned = returned.reshape(n_rows, width)
 
-        partial = jnp.dot(
-            w_both, jnp.concatenate([returned, returned], axis=0), preferred_element_type=jnp.float32
-        ).astype(jnp.bfloat16)
+        both = jnp.dot(w_both, returned, preferred_element_type=jnp.float32)
+        partial = (both[:rows_chunk] + both[rows_chunk:]).astype(jnp.bfloat16)
         partials.append(partial)
     outs.append(lax.psum_scatter(partials[-1], "tp", scatter_dimension=1, tiled=True))
     return jnp.concatenate(outs, axis=0)

time: 325 us -> 325 us (level)
  matrix products: 64 us -> 58.2 us
  other arithmetic: 20.5 us -> 24.5 us
    dot_general x2, matrix products: 16.4 us -> 10.6 us  [on_device(): both = jnp.dot(w_both, returned, preferred_element_type=jnp.float32)]
    convert_element_type x0 -> x2, other arithmetic: none -> 3.97 us  [on_device(): partial = (both[:rows_chunk] + both[rows_chunk:]).astype(jnp.bfloat16)]
  transfers between devices with their start and end apart: 8 -> 8, of which waited for: 7 -> 8; matrix products, arithmetic and copies ran while one was open for 29% -> 28% of each run, Pallas kernels for 0% -> 0%
where the time goes in v5:
time: 325 us; the launch traced here: 324 us
  waiting for transfers between devices  170 us (52%)
  matrix products  58.2 us (18%)
  starting transfers between devices  32.6 us (10%)
  local copies, waits for them, and re-layouts  26.2 us (8%)
  other arithmetic  24.5 us (8%)
  between operations  13.3 us (4%)
    all_gather x2, waiting for transfers between devices, on_device(): gathered = lax.all_gather(piece, 'tp', axis=0)  55.4 us
    all_to_all x2, waiting for transfers between devices, on_device(): lax.all_to_all(result, 'ctx', split_axis=0, concat_axis=0, tiled=True)  44.6 us
    reduce_scatter x1, waiting for transfers between devices, on_device(): lax.psum_scatter(partials[-1], 'tp', scatter_dimension=1, tiled=True)  43.6 us
    all_to_all x2, waiting for transfers between devices, on_device(): lax.all_to_all(outgoing, 'ctx', split_axis=0, concat_axis=0, tiled=True)  23.8 us
    dot_general x2, matrix products, expert_rows(): jnp.einsum(hidden_form + ',lfd->' + form, hidden, w_down, preferred_eleme...  22 us
    all_to_all x2, starting transfers between devices, on_device(): lax.all_to_all(outgoing, 'ctx', split_axis=0, concat_axis=0, tiled=True)  16.4 us
    all_to_all x2, starting transfers between devices, on_device(): lax.all_to_all(result, 'ctx', split_axis=0, concat_axis=0, tiled=True)  15.8 us
    dot_general x2, matrix products, expert_rows(): jnp.einsum(form + ',ldf->' + hidden_form, features, w_up, preferred_eleme...  13.8 us
  transfers between devices with their start and end apart: 8, of which 8 were waited for; matrix products, arithmetic and copies ran while one was open for 28% of the time, Pallas kernels for 0%

profile of v5, /device:TPU:2, one launch (start us, length us, event | category | flops | bytes accessed | tf_op | source)
XLA Modules:
  0.0 324.3 jit_solution(7048273092398909764)
XLA Ops:
  11.0 1.8 fusion.150
  14.3 43.5 %all-gather.5.cloned.1.call-done = bf16[4352,256]{1,0:T(8,128)(2,1)} async-done(((bf16[544,256]{1,0:T(8,128)(2,1)}), bf16[4352,256]{1,0:T(8,128)(2,1)}) %all-gather.5.cloned.1.call-update) | async-done | bytes 2228240 | tf_op jit(solution)/shard_map/all_gather | solution.py:68
  59.7 3.3 %slice_add_fusion.2 = (f32[8,128,8]{2,1,0:T(8,128)}, s32[8,128,8]{2,1,0:T(8,128)S(1)}) fusion(f32[8,128,64]{2,1,0:T(8,128)} %reshape.476), kind=kLoop, calls=%fused_computation.161 | loop fusion | flops 24576 | bytes 196608 | tf_op jit(solution)/shard_map/add | solution.py:75
  67.3 2.5 copy.30
  69.8 4.2 %reshape.480 = bf16[512,2048,1]{1,0,2:T(8,128)(2,1)} reshape(bf16[512,8,256]{2,1,0:T(8,128)(2,1)} %copy.30) | data formatting | bytes 4194304 | tf_op jit(solution)/shard_map/reshape | solution.py:69
  74.0 6.0 %fusion.75 = bf16[16,48,2048]{2,1,0:T(8,128)(2,1)} fusion(bf16[512,2048,1]{1,0,2:T(8,128)(2,1)} %reshape.480, s32[512]{0:T(512)S(1)} %bitcast.131, s32[512]{0:T(512)S(1)} %bitcast.134, s32[512]{0:T(512)S(1)} %bitcast.137, s32[512]{0:T(512)S(1)} %bitcast.140, s32[512]{0:T(512)S(1)} %bitcast.143, s32[512]{0:T(512)S(1)} %bitcast.146, s32[512]{0:T(512)S(1)} %bitcast.149, ...), kind=kOutput, calls=%fused_computation.108 | convolution fusion | flops 1619656704 | bytes 5262336 | tf_op jit(solution)/shard_map/dot_general | solution.py:106
  80.0 7.3 %all-to-all-start.1 = ((bf16[16,48,2048]{2,1,0:T(8,128)(2,1)}), bf16[16,48,2048]{2,1,0:T(8,128)(2,1)}, u32[]{:S(2)}, u32[]{:S(2)}) async-start(bf16[16,48,2048]{2,1,0:T(8,128)(2,1)} %fusion.75), calls=%async_computation.1 | async-start | bytes 6291456 | tf_op jit(solution)/shard_map/all_to_all | solution.py:109
  87.2 11.9 %all-gather.7.cloned.1.call-done = bf16[4096,256]{1,0:T(8,128)(2,1)} async-done(((bf16[512,256]{1,0:T(8,128)(2,1)}), bf16[4096,256]{1,0:T(8,128)(2,1)}) %all-gather.7.cloned.1.call-update) | async-done | bytes 2097168 | tf_op jit(solution)/shard_map/all_gather | solution.py:68
  99.1 4.2 %copy.36 = bf16[8,512,256]{2,0,1:T(8,128)(2,1)} copy(bf16[8,512,256]{2,1,0:T(8,128)(2,1)} %bitcast.94) | data formatting | bytes 4194304 | tf_op jit(solution)/shard_map/all_gather | solution.py:68
  103.3 4.2 %reshape.479 = bf16[512,2048,1]{1,0,2:T(8,128)(2,1)} reshape(bf16[512,8,256]{2,1,0:T(8,128)(2,1)} %bitcast.89) | data formatting | bytes 4194304 | tf_op jit(solution)/shard_map/reshape | solution.py:69
  107.6 5.9 %fusion.66 = bf16[16,48,2048]{2,1,0:T(8,128)(2,1)} fusion(bf16[512,2048,1]{1,0,2:T(8,128)(2,1)} %reshape.479, s32[512]{0:T(512)S(1)} %bitcast.107, s32[512]{0:T(512)S(1)} %bitcast.110, s32[512]{0:T(512)S(1)} %bitcast.113, s32[512]{0:T(512)S(1)} %bitcast.116, s32[512]{0:T(512)S(1)} %bitcast.119, s32[512]{0:T(512)S(1)} %bitcast.122, s32[512]{0:T(512)S(1)} %bitcast.125, ...), kind=kOutput, calls=%fused_computation.100 | convolution fusion | flops 1619656704 | bytes 5262336 | tf_op jit(solution)/shard_map/dot_general | solution.py:106
  113.5 8.9 %all-to-all-done.1 = bf16[16,48,2048]{2,1,0:T(8,128)(2,1)} async-done(((bf16[16,48,2048]{2,1,0:T(8,128)(2,1)}), bf16[16,48,2048]{2,1,0:T(8,128)(2,1)}, u32[]{:S(2)}, u32[]{:S(2)}) %all-to-all-start.1) | async-done | bytes 3145760 | tf_op jit(solution)/shard_map/all_to_all | solution.py:109
  122.4 9.1 %all-to-all-start = ((bf16[16,48,2048]{2,1,0:T(8,128)(2,1)}), bf16[16,48,2048]{2,1,0:T(8,128)(2,1)}, u32[]{:S(2)}, u32[]{:S(2)}) async-start(bf16[16,48,2048]{2,1,0:T(8,128)(2,1)} %fusion.66), calls=%async_computation | async-start | bytes 6291456 | tf_op jit(solution)/shard_map/all_to_all | solution.py:109
  134.4 6.9 %fusion.4 = f32[768,768]{1,0:T(8,128)} fusion(bf16[768,2048]{1,0:T(8,128)(2,1)} %bitcast.38, bf16[1,2048,768]{2,1,0:T(8,128)(2,1)} %param.10), kind=kOutput, calls=%fused_computation.8 | convolution fusion | flops 2415919104 | bytes 8650752 | tf_op jit(solution)/shard_map/lsd,ldf->lsf/dot_general | solution.py:21
  141.3 11.0 %convolution_convert_fusion = bf16[768,2048]{1,0:T(8,128)(2,1)} fusion(bf16[1,768,2048]{2,1,0:T(8,128)(2,1)S(1)} %copy-done, f32[768,768]{1,0:T(8,128)} %fusion.4, bf16[768,2048]{1,0:T(8,128)(2,1)} %bitcast.38, bf16[1,2048,768]{2,1,0:T(8,128)(2,1)} %param.9), kind=kOutput, calls=%fused_computation.4 | convolution fusion | flops 4836950016 | bytes 14942208 | tf_op jit(solution)/shard_map/lsf,lfd->lsd/dot_general | solution.py:25
  152.3 14.9 %all-to-all-done = bf16[16,48,2048]{2,1,0:T(8,128)(2,1)} async-done(((bf16[16,48,2048]{2,1,0:T(8,128)(2,1)}), bf16[16,48,2048]{2,1,0:T(8,128)(2,1)}, u32[]{:S(2)}, u32[]{:S(2)}) %all-to-all-start) | async-done | bytes 3145760 | tf_op jit(solution)/shard_map/all_to_all | solution.py:109
  167.2 8.3 %all-to-all-start.2 = ((bf16[16,48,2048]{2,1,0:T(8,128)(2,1)}), bf16[16,48,2048]{2,1,0:T(8,128)(2,1)}, u32[]{:S(2)}, u32[]{:S(2)}) async-start(bf16[16,48,2048]{2,1,0:T(8,128)(2,1)} %bitcast.91), calls=%async_computation.2 | async-start | bytes 6291456 | tf_op jit(solution)/shard_map/all_to_all | solution.py:119
  175.5 2.6 fusion.83
  178.1 2.5 fusion.90
  180.6 6.9 %fusion.6 = f32[768,768]{1,0:T(8,128)} fusion(bf16[768,2048]{1,0:T(8,128)(2,1)} %bitcast.20, bf16[1,2048,768]{2,1,0:T(8,128)(2,1)} %param.10), kind=kOutput, calls=%fused_computation.10 | convolution fusion | flops 2415919104 | bytes 8650752 | tf_op jit(solution)/shard_map/lsd,ldf->lsf/dot_general | solution.py:21
  187.5 11.0 %fusion.12 = bf16[1,768,2048]{2,1,0:T(8,128)(2,1)} fusion(bf16[1,768,2048]{2,1,0:T(8,128)(2,1)S(1)} %copy-done, f32[768,768]{1,0:T(8,128)} %fusion.6, bf16[768,2048]{1,0:T(8,128)(2,1)} %bitcast.20, bf16[1,2048,768]{2,1,0:T(8,128)(2,1)} %param.9), kind=kOutput, calls=%fused_computation.16 | convolution fusion | flops 4836950016 | bytes 14942208 | tf_op jit(solution)/shard_map/lsf,lfd->lsd/dot_general | solution.py:25
  198.5 15.1 %all-to-all-done.2 = bf16[16,48,2048]{2,1,0:T(8,128)(2,1)} async-done(((bf16[16,48,2048]{2,1,0:T(8,128)(2,1)}), bf16[16,48,2048]{2,1,0:T(8,128)(2,1)}, u32[]{:S(2)}, u32[]{:S(2)}) %all-to-all-start.2) | async-done | bytes 3145760 | tf_op jit(solution)/shard_map/all_to_all | solution.py:119
  213.6 5.8 %fusion.19 = f32[1024,2048]{1,0:T(8,128)S(1)} fusion(bf16[768,2048]{1,0:T(8,128)(2,1)} %bitcast.40, bf16[512,768]{1,0:T(8,128)(2,1)} %fusion.90, bf16[512,768]{1,0:T(8,128)(2,1)} %fusion.83), kind=kOutput, calls=%fused_computation.21 | convolution fusion | flops 3224371200 | bytes 13107200 | tf_op jit(solution)/shard_map/dot_general | solution.py:122
  219.4 2.0 fusion.1
  221.4 7.5 %all-to-all-start.3 = ((bf16[16,48,2048]{2,1,0:T(8,128)(2,1)}), bf16[16,48,2048]{2,1,0:T(8,128)(2,1)S(1)}, u32[]{:S(2)}, u32[]{:S(2)}) async-start(bf16[16,48,2048]{2,1,0:T(8,128)(2,1)} %bitcast.43), calls=%async_computation.4 | async-start | bytes 6291456 | tf_op jit(solution)/shard_map/all_to_all | solution.py:119
  230.1 2.6 fusion.97
  232.7 2.5 fusion.104
  235.2 29.5 %all-to-all-done.3 = bf16[16,48,2048]{2,1,0:T(8,128)(2,1)S(1)} async-done(((bf16[16,48,2048]{2,1,0:T(8,128)(2,1)}), bf16[16,48,2048]{2,1,0:T(8,128)(2,1)S(1)}, u32[]{:S(2)}, u32[]{:S(2)}) %all-to-all-start.3) | async-done | bytes 3145760 | tf_op jit(solution)/shard_map/all_to_all | solution.py:119
  264.8 4.8 %fusion.23 = f32[1024,2048]{1,0:T(8,128)S(1)} fusion(bf16[768,2048]{1,0:T(8,128)(2,1)S(1)} %bitcast.90, bf16[512,768]{1,0:T(8,128)(2,1)} %fusion.104, bf16[512,768]{1,0:T(8,128)(2,1)} %fusion.97), kind=kOutput, calls=%fused_computation.25 | convolution fusion | flops 3224371200 | bytes 13107200 | tf_op jit(solution)/shard_map/dot_general | solution.py:122
  269.6 2.0 fusion
  272.2 43.6 %reduce-scatter.5.cloned.1.call-done = bf16[512,256]{1,0:T(8,128)(2,1)} async-done(((bf16[512,2048]{1,0:T(8,128)(2,1)}), bf16[512,256]{1,0:T(8,128)(2,1)}) %reduce-scatter.5.cloned.1.call-update) | async-done | bytes 262160 | tf_op jit(solution)/shard_map/reduce_scatter | solution.py:125
  315.9 1.9 pad_maximum_fusion
  (59 shorter events, 17.0 us)
Async XLA Ops:
  6.5 134.7 %copy-start = (bf16[1,768,2048]{2,1,0:T(8,128)(2,1)S(1)}, bf16[1,768,2048]{2,1,0:T(8,128)(2,1)}, u32[]{:S(2)}) copy-start(bf16[1,768,2048]{2,1,0:T(8,128)(2,1)} %param.11) | copy-start | bytes 9437188
  6.5 2.5 copy-start.4
  6.5 51.3 %all-gather.5.cloned.1.call-start = ((), (), s32[]{:S(2)}) async-start(), calls=%async_computation.8 | async-start | bytes 2506752 | tf_op jit(solution)/shard_map/all_gather | solution.py:68
  8.1 2.6 copy-start.3
  13.5 85.6 %all-gather.7.cloned.1.call-start = ((), (), s32[]{:S(2)}) async-start(), calls=%async_computation.9 | async-start | bytes 2359296 | tf_op jit(solution)/shard_map/all_gather | solution.py:68
  59.7 3.3 %copy-start.2 = (f32[8,128,64]{2,1,0:T(8,128)S(1)}, f32[8,128,64]{2,1,0:T(8,128)}, u32[]{:S(2)}) copy-start(f32[8,128,64]{2,1,0:T(8,128)} %reshape.476) | copy-start | bytes 786436
  80.0 42.5 %all-to-all-start.1 = ((bf16[16,48,2048]{2,1,0:T(8,128)(2,1)}), bf16[16,48,2048]{2,1,0:T(8,128)(2,1)}, u32[]{:S(2)}, u32[]{:S(2)}) async-start(bf16[16,48,2048]{2,1,0:T(8,128)(2,1)} %fusion.75), calls=%async_computation.1 | async-start | bytes 6291456 | tf_op jit(solution)/shard_map/all_to_all | solution.py:109
  122.4 44.8 %all-to-all-start = ((bf16[16,48,2048]{2,1,0:T(8,128)(2,1)}), bf16[16,48,2048]{2,1,0:T(8,128)(2,1)}, u32[]{:S(2)}, u32[]{:S(2)}) async-start(bf16[16,48,2048]{2,1,0:T(8,128)(2,1)} %fusion.66), calls=%async_computation | async-start | bytes 6291456 | tf_op jit(solution)/shard_map/all_to_all | solution.py:109
  167.2 46.4 %all-to-all-start.2 = ((bf16[16,48,2048]{2,1,0:T(8,128)(2,1)}), bf16[16,48,2048]{2,1,0:T(8,128)(2,1)}, u32[]{:S(2)}, u32[]{:S(2)}) async-start(bf16[16,48,2048]{2,1,0:T(8,128)(2,1)} %bitcast.91), calls=%async_computation.2 | async-start | bytes 6291456 | tf_op jit(solution)/shard_map/all_to_all | solution.py:119
  221.4 43.4 %all-to-all-start.3 = ((bf16[16,48,2048]{2,1,0:T(8,128)(2,1)}), bf16[16,48,2048]{2,1,0:T(8,128)(2,1)S(1)}, u32[]{:S(2)}, u32[]{:S(2)}) async-start(bf16[16,48,2048]{2,1,0:T(8,128)(2,1)} %bitcast.43), calls=%async_computation.4 | async-start | bytes 6291456 | tf_op jit(solution)/shard_map/all_to_all | solution.py:119
  228.9 43.4 %reduce-scatter.3.cloned.1.call-start = ((), (), s32[]{:S(2)}) async-start(), calls=%async_computation.6 | async-start | bytes 2359296 | tf_op jit(solution)/shard_map/reduce_scatter | solution.py:115
  229.6 86.3 %reduce-scatter.5.cloned.1.call-start = ((), (), s32[]{:S(2)}) async-start(), calls=%async_computation.7 | async-start | bytes 2359296 | tf_op jit(solution)/shard_map/reduce_scatter | solution.py:125
  271.5 46.2 %copy-start.1 = (bf16[1,768,2048]{2,1,0:T(8,128)(2,1)S(1)}, bf16[1,768,2048]{2,1,0:T(8,128)(2,1)}, u32[]{:S(2)}) copy-start(bf16[1,768,2048]{2,1,0:T(8,128)(2,1)} %param.11) | copy-start | bytes 9437188
Sparse Core Ops, SparseCore 0:
  13.6 44.1 all-gather.4
  59.6 39.4 all-gather.6
  232.2 39.9 reduce-scatter.2
  274.6 41.1 reduce-scatter.4

commit v6 on v5

--- a/solution.py
+++ b/solution.py
@@ -45,17 +45,15 @@
     per_dest = exp_dev * capacity
 
     slot_of = slot_numbers(routing.reshape(1, tok_blk * top), experts).reshape(tok_blk, top)
-    g1 = bf16_part(gates)
-    rest = gates - g1
-    g2 = bf16_part(rest)
-    g3 = rest - g2
-    info = jnp.concatenate(
-        [routing.astype(jnp.float32), slot_of.astype(jnp.float32), g1, g2, g3], axis=1
-    ).astype(jnp.bfloat16)
-    info_cols = 64
-    info = jnp.pad(info, ((0, 0), (0, info_cols - info.shape[1])))
-    info_rows = tok_blk * info_cols // cols
-    info = info.reshape(info_rows, cols)
+    info = jnp.concatenate([routing.astype(jnp.float32), slot_of.astype(jnp.float32), gates], axis=1)
+    info_all = lax.all_gather(info, "tp", axis=0)
+    expert_all = info_all[:, :, 0:top].astype(jnp.int32)
+    slot_all = info_all[:, :, top:2 * top].astype(jnp.int32)
+    gates_all = info_all[:, :, 2 * top:3 * top]
+    dest_ctx = expert_all // (n_tp * exp_dev)
+    dest_tp = (expert_all // exp_dev) % n_tp
+    dest_loc = expert_all % exp_dev
+    mine = dest_tp == me_tp
 
     blk_chunk = n_tp // CHUNKS
     rows_chunk = blk_chunk * tok_blk
@@ -63,22 +61,8 @@
     partials = []
     for h in range(CHUNKS):
         piece = attn_out[h * rows_chunk:(h + 1) * rows_chunk]
-        if h == 0:
-            piece = jnp.concatenate([piece, info], axis=0)
         gathered = lax.all_gather(piece, "tp", axis=0)
-        feats = jnp.transpose(gathered[:, :rows_chunk], (1, 0, 2)).reshape(rows_chunk, width)
-        if h == 0:
-            info_all = gathered[:, rows_chunk:].reshape(n_tp, tok_blk, info_cols)
-            info_all = info_all.astype(jnp.float32)
-            expert_all = info_all[:, :, 0:top].astype(jnp.int32)
-            slot_all = info_all[:, :, top:2 * top].astype(jnp.int32)
-            gates_all = (
-                info_all[:, :, 2 * top:3 * top] + info_all[:, :, 3 * top:4 * top]
-            ) + info_all[:, :, 4 * top:5 * top]
-            dest_ctx = expert_all // (n_tp * exp_dev)
-            dest_tp = (expert_all // exp_dev) % n_tp
-            dest_loc = expert_all % exp_dev
-            mine = dest_tp == me_tp
+        feats = jnp.transpose(gathered, (1, 0, 2)).reshape(rows_chunk, width)
 
         blocks = slice(h * blk_chunk, (h + 1) * blk_chunk)
         b_loc = jnp.arange(blk_chunk, dtype=jnp.int32)[:, None, None]

time: 325 us -> 313 us (0.963)
  blocking collectives: 0 us -> 28.3 us
  waiting for transfers between devices: 170 us -> 142 us
  other arithmetic: 24.5 us -> 18.1 us
  local copies, waits for them, and re-layouts: 26.2 us -> 20.2 us
    all_gather x0 -> x1, blocking collectives: none -> 28.3 us  [on_device(): info_all = lax.all_gather(info, 'tp', axis=0)]
    all_gather x2, waiting for transfers between devices: 55.4 us -> 31.5 us  [on_device(): gathered = lax.all_gather(piece, 'tp', axis=0)]
    transpose x2 -> x1, local copies, waits for them, and re-layouts: 4.23 us -> 0.01 us  [on_device(): position = jnp.transpose(position.reshape(rows_chunk, top))]
    all_gather x1 -> x2, local copies, waits for them, and re-layouts: 4.16 us -> 8.21 us  [on_device(): gathered = lax.all_gather(piece, 'tp', axis=0)]
    add x1 -> x0, other arithmetic: 3.26 us -> none  [on_device(): info_all[:, :, 2 * top:3 * top] + info_all[:, :, 3 * top:4 * top] + info_...]
    reshape x7 -> x2, local copies, waits for them, and re-layouts: 10.8 us -> 8.42 us  [on_device(): feats = jnp.transpose(gathered, (1, 0, 2)).reshape(rows_chunk, width)]
  transfers between devices with their start and end apart: 8 -> 8, of which waited for: 8 -> 7; matrix products, arithmetic and copies ran while one was open for 28% -> 27% of each run, Pallas kernels for 0% -> 0%
where the time goes in v6:
time: 313 us
  waiting for transfers between devices  142 us (45%)
  matrix products  58.2 us (19%)
  starting transfers between devices  32.2 us (10%)
  blocking collectives  28.3 us (9%)
  local copies, waits for them, and re-layouts  20.2 us (6%)
  other arithmetic  18.1 us (6%)
  between operations  13.3 us (4%)
    all_to_all x2, waiting for transfers between devices, on_device(): lax.all_to_all(result, 'ctx', split_axis=0, concat_axis=0, tiled=True)  44.7 us
    reduce_scatter x1, waiting for transfers between devices, on_device(): lax.psum_scatter(partials[-1], 'tp', scatter_dimension=1, tiled=True)  43 us
    all_gather x2, waiting for transfers between devices, on_device(): gathered = lax.all_gather(piece, 'tp', axis=0)  31.5 us
    all_gather x1, blocking collectives, on_device(): info_all = lax.all_gather(info, 'tp', axis=0)  28.3 us
    dot_general x2, matrix products, expert_rows(): jnp.einsum(hidden_form + ',lfd->' + form, hidden, w_down, preferred_eleme...  22 us
    all_to_all x2, waiting for transfers between devices, on_device(): lax.all_to_all(outgoing, 'ctx', split_axis=0, concat_axis=0, tiled=True)  21.6 us
    all_to_all x2, starting transfers between devices, on_device(): lax.all_to_all(outgoing, 'ctx', split_axis=0, concat_axis=0, tiled=True)  16 us
    all_to_all x2, starting transfers between devices, on_device(): lax.all_to_all(result, 'ctx', split_axis=0, concat_axis=0, tiled=True)  15.8 us
  transfers between devices with their start and end apart: 8, of which 7 were waited for; matrix products, arithmetic and copies ran while one was open for 27% of the time, Pallas kernels for 0%

profile of v6, /device:TPU:2, one launch (start us, length us, event | category | flops | bytes accessed | tf_op | source)
XLA Modules:
  0.0 312.5 jit_solution(9840921284093991558)
XLA Ops:
  6.5 2.0 fusion.150
  12.6 28.3 %all-gather = f32[1024,24]{0,1:T(8,128)S(1)} all-gather(f32[128,24]{0,1:T(8,128)S(1)} %pad_maximum_fusion.1), channel_id=2, replica_groups=mesh['ctx'=16,'tp'=8,'dp'=2] {'tp'}, dimensions={0}, use_global_device_ids=true | all-gather | bytes 110592 | tf_op jit(solution)/shard_map/all_gather | solution.py:49
  41.1 11.8 %all-gather.8.cloned.1.call-done = bf16[4096,256]{1,0:T(8,128)(2,1)} async-done(((bf16[512,256]{1,0:T(8,128)(2,1)}), bf16[4096,256]{1,0:T(8,128)(2,1)}) %all-gather.8.cloned.1.call-update) | async-done | bytes 2097168 | tf_op jit(solution)/shard_map/all_gather | solution.py:64
  52.9 4.1 %copy.48 = bf16[8,512,256]{2,0,1:T(8,128)(2,1)} copy(bf16[8,512,256]{2,1,0:T(8,128)(2,1)} %bitcast.135) | data formatting | bytes 4194304 | tf_op jit(solution)/shard_map/all_gather | solution.py:64
  57.0 4.2 %reshape.472 = bf16[512,2048,1]{1,0,2:T(8,128)(2,1)} reshape(bf16[512,8,256]{2,1,0:T(8,128)(2,1)} %bitcast.130) | data formatting | bytes 4194304 | tf_op jit(solution)/shard_map/reshape | solution.py:65
  61.2 6.0 %fusion.75 = bf16[16,48,2048]{2,1,0:T(8,128)(2,1)} fusion(bf16[512,2048,1]{1,0,2:T(8,128)(2,1)} %reshape.472, s32[512]{0:T(512)S(1)} %bitcast.171, s32[512]{0:T(512)S(1)} %bitcast.174, s32[512]{0:T(512)S(1)} %bitcast.177, s32[512]{0:T(512)S(1)} %bitcast.180, s32[512]{0:T(512)S(1)} %bitcast.183, s32[512]{0:T(512)S(1)} %bitcast.186, s32[512]{0:T(512)S(1)} %bitcast.189, ...), kind=kOutput, calls=%fused_computation.108 | convolution fusion | flops 1619656704 | bytes 5262336 | tf_op jit(solution)/shard_map/dot_general | solution.py:90
  67.1 7.6 %all-to-all-start.1 = ((bf16[16,48,2048]{2,1,0:T(8,128)(2,1)}), bf16[16,48,2048]{2,1,0:T(8,128)(2,1)}, u32[]{:S(2)}, u32[]{:S(2)}) async-start(bf16[16,48,2048]{2,1,0:T(8,128)(2,1)} %fusion.75), calls=%async_computation.1 | async-start | bytes 6291456 | tf_op jit(solution)/shard_map/all_to_all | solution.py:93
  74.7 19.7 %all-gather.6.cloned.1.call-done = bf16[4096,256]{1,0:T(8,128)(2,1)} async-done(((bf16[512,256]{1,0:T(8,128)(2,1)}), bf16[4096,256]{1,0:T(8,128)(2,1)}) %all-gather.6.cloned.1.call-update) | async-done | bytes 2097168 | tf_op jit(solution)/shard_map/all_gather | solution.py:64
  94.4 4.2 %copy.49 = bf16[8,512,256]{2,0,1:T(8,128)(2,1)} copy(bf16[8,512,256]{2,1,0:T(8,128)(2,1)} %bitcast.134) | data formatting | bytes 4194304 | tf_op jit(solution)/shard_map/all_gather | solution.py:64
  98.6 4.2 %reshape.471 = bf16[512,2048,1]{1,0,2:T(8,128)(2,1)} reshape(bf16[512,8,256]{2,1,0:T(8,128)(2,1)} %bitcast.131) | data formatting | bytes 4194304 | tf_op jit(solution)/shard_map/reshape | solution.py:65
  102.8 5.9 %fusion.66 = bf16[16,48,2048]{2,1,0:T(8,128)(2,1)} fusion(bf16[512,2048,1]{1,0,2:T(8,128)(2,1)} %reshape.471, s32[512]{0:T(512)S(1)} %bitcast.147, s32[512]{0:T(512)S(1)} %bitcast.150, s32[512]{0:T(512)S(1)} %bitcast.153, s32[512]{0:T(512)S(1)} %bitcast.156, s32[512]{0:T(512)S(1)} %bitcast.159, s32[512]{0:T(512)S(1)} %bitcast.162, s32[512]{0:T(512)S(1)} %bitcast.165, ...), kind=kOutput, calls=%fused_computation.100 | convolution fusion | flops 1619656704 | bytes 5262336 | tf_op jit(solution)/shard_map/dot_general | solution.py:90
  108.7 1.5 all-to-all-done.1
  110.2 8.5 %all-to-all-start = ((bf16[16,48,2048]{2,1,0:T(8,128)(2,1)}), bf16[16,48,2048]{2,1,0:T(8,128)(2,1)}, u32[]{:S(2)}, u32[]{:S(2)}) async-start(bf16[16,48,2048]{2,1,0:T(8,128)(2,1)} %fusion.66), calls=%async_computation | async-start | bytes 6291456 | tf_op jit(solution)/shard_map/all_to_all | solution.py:93
  118.8 6.9 %fusion.4 = f32[768,768]{1,0:T(8,128)} fusion(bf16[768,2048]{1,0:T(8,128)(2,1)} %bitcast.35, bf16[1,2048,768]{2,1,0:T(8,128)(2,1)} %param.10), kind=kOutput, calls=%fused_computation.8 | convolution fusion | flops 2415919104 | bytes 8650752 | tf_op jit(solution)/shard_map/lsd,ldf->lsf/dot_general | solution.py:21
  125.6 11.0 %convolution_convert_fusion = bf16[768,2048]{1,0:T(8,128)(2,1)} fusion(bf16[1,768,2048]{2,1,0:T(8,128)(2,1)S(1)} %copy-done, f32[768,768]{1,0:T(8,128)} %fusion.4, bf16[768,2048]{1,0:T(8,128)(2,1)} %bitcast.35, bf16[1,2048,768]{2,1,0:T(8,128)(2,1)} %param.9), kind=kOutput, calls=%fused_computation.4 | convolution fusion | flops 4836950016 | bytes 14942208 | tf_op jit(solution)/shard_map/lsf,lfd->lsd/dot_general | solution.py:25
  136.7 20.0 %all-to-all-done = bf16[16,48,2048]{2,1,0:T(8,128)(2,1)} async-done(((bf16[16,48,2048]{2,1,0:T(8,128)(2,1)}), bf16[16,48,2048]{2,1,0:T(8,128)(2,1)}, u32[]{:S(2)}, u32[]{:S(2)}) %all-to-all-start) | async-done | bytes 3145760 | tf_op jit(solution)/shard_map/all_to_all | solution.py:93
  156.7 7.8 %all-to-all-start.2 = ((bf16[16,48,2048]{2,1,0:T(8,128)(2,1)}), bf16[16,48,2048]{2,1,0:T(8,128)(2,1)}, u32[]{:S(2)}, u32[]{:S(2)}) async-start(bf16[16,48,2048]{2,1,0:T(8,128)(2,1)} %bitcast.133), calls=%async_computation.2 | async-start | bytes 6291456 | tf_op jit(solution)/shard_map/all_to_all | solution.py:103
  164.5 2.6 fusion.83
  167.1 2.5 fusion.90
  169.6 6.9 %fusion.6 = f32[768,768]{1,0:T(8,128)} fusion(bf16[768,2048]{1,0:T(8,128)(2,1)} %bitcast.18, bf16[1,2048,768]{2,1,0:T(8,128)(2,1)} %param.10), kind=kOutput, calls=%fused_computation.10 | convolution fusion | flops 2415919104 | bytes 8650752 | tf_op jit(solution)/shard_map/lsd,ldf->lsf/dot_general | solution.py:21
  176.5 11.0 %fusion.12 = bf16[1,768,2048]{2,1,0:T(8,128)(2,1)} fusion(bf16[1,768,2048]{2,1,0:T(8,128)(2,1)S(1)} %copy-done, f32[768,768]{1,0:T(8,128)} %fusion.6, bf16[768,2048]{1,0:T(8,128)(2,1)} %bitcast.18, bf16[1,2048,768]{2,1,0:T(8,128)(2,1)} %param.9), kind=kOutput, calls=%fused_computation.16 | convolution fusion | flops 4836950016 | bytes 14942208 | tf_op jit(solution)/shard_map/lsf,lfd->lsd/dot_general | solution.py:25
  187.5 12.8 %all-to-all-done.2 = bf16[16,48,2048]{2,1,0:T(8,128)(2,1)} async-done(((bf16[16,48,2048]{2,1,0:T(8,128)(2,1)}), bf16[16,48,2048]{2,1,0:T(8,128)(2,1)}, u32[]{:S(2)}, u32[]{:S(2)}) %all-to-all-start.2) | async-done | bytes 3145760 | tf_op jit(solution)/shard_map/all_to_all | solution.py:103
  200.2 5.8 %fusion.19 = f32[1024,2048]{1,0:T(8,128)S(1)} fusion(bf16[768,2048]{1,0:T(8,128)(2,1)} %bitcast.37, bf16[512,768]{1,0:T(8,128)(2,1)} %fusion.90, bf16[512,768]{1,0:T(8,128)(2,1)} %fusion.83), kind=kOutput, calls=%fused_computation.21 | convolution fusion | flops 3224371200 | bytes 13107200 | tf_op jit(solution)/shard_map/dot_general | solution.py:106
  206.0 2.0 fusion.1
  208.0 8.0 %all-to-all-start.3 = ((bf16[16,48,2048]{2,1,0:T(8,128)(2,1)}), bf16[16,48,2048]{2,1,0:T(8,128)(2,1)S(1)}, u32[]{:S(2)}, u32[]{:S(2)}) async-start(bf16[16,48,2048]{2,1,0:T(8,128)(2,1)} %bitcast.39), calls=%async_computation.4 | async-start | bytes 6291456 | tf_op jit(solution)/shard_map/all_to_all | solution.py:103
  217.2 2.6 fusion.97
  219.8 2.5 fusion.104
  222.3 31.9 %all-to-all-done.3 = bf16[16,48,2048]{2,1,0:T(8,128)(2,1)S(1)} async-done(((bf16[16,48,2048]{2,1,0:T(8,128)(2,1)}), bf16[16,48,2048]{2,1,0:T(8,128)(2,1)S(1)}, u32[]{:S(2)}, u32[]{:S(2)}) %all-to-all-start.3) | async-done | bytes 3145760 | tf_op jit(solution)/shard_map/all_to_all | solution.py:103
  254.2 4.8 %fusion.23 = f32[1024,2048]{1,0:T(8,128)S(1)} fusion(bf16[768,2048]{1,0:T(8,128)(2,1)S(1)} %bitcast.132, bf16[512,768]{1,0:T(8,128)(2,1)} %fusion.104, bf16[512,768]{1,0:T(8,128)(2,1)} %fusion.97), kind=kOutput, calls=%fused_computation.25 | convolution fusion | flops 3224371200 | bytes 13107200 | tf_op jit(solution)/shard_map/dot_general | solution.py:106
  259.0 2.0 fusion
  261.1 43.0 %reduce-scatter.5.cloned.1.call-done = bf16[512,256]{1,0:T(8,128)(2,1)} async-done(((bf16[512,2048]{1,0:T(8,128)(2,1)}), bf16[512,256]{1,0:T(8,128)(2,1)}) %reduce-scatter.5.cloned.1.call-update) | async-done | bytes 262160 | tf_op jit(solution)/shard_map/reduce_scatter | solution.py:109
  304.1 1.9 pad_maximum_fusion
  (47 shorter events, 5.4 us)
Async XLA Ops:
  6.5 119.1 %copy-start = (bf16[1,768,2048]{2,1,0:T(8,128)(2,1)S(1)}, bf16[1,768,2048]{2,1,0:T(8,128)(2,1)}, u32[]{:S(2)}) copy-start(bf16[1,768,2048]{2,1,0:T(8,128)(2,1)} %param.11) | copy-start | bytes 9437188
  6.5 2.8 copy-start.2
  6.5 46.4 %all-gather.8.cloned.1.call-start = ((), (), s32[]{:S(2)}) async-start(), calls=%async_computation.9 | async-start | bytes 2359296 | tf_op jit(solution)/shard_map/all_gather | solution.py:64
  8.6 85.8 %all-gather.6.cloned.1.call-start = ((), (), s32[]{:S(2)}) async-start(), calls=%async_computation.8 | async-start | bytes 2359296 | tf_op jit(solution)/shard_map/all_gather | solution.py:64
  10.1 2.5 copy-start.3
  67.1 43.1 %all-to-all-start.1 = ((bf16[16,48,2048]{2,1,0:T(8,128)(2,1)}), bf16[16,48,2048]{2,1,0:T(8,128)(2,1)}, u32[]{:S(2)}, u32[]{:S(2)}) async-start(bf16[16,48,2048]{2,1,0:T(8,128)(2,1)} %fusion.75), calls=%async_computation.1 | async-start | bytes 6291456 | tf_op jit(solution)/shard_map/all_to_all | solution.py:93
  110.2 46.5 %all-to-all-start = ((bf16[16,48,2048]{2,1,0:T(8,128)(2,1)}), bf16[16,48,2048]{2,1,0:T(8,128)(2,1)}, u32[]{:S(2)}, u32[]{:S(2)}) async-start(bf16[16,48,2048]{2,1,0:T(8,128)(2,1)} %fusion.66), calls=%async_computation | async-start | bytes 6291456 | tf_op jit(solution)/shard_map/all_to_all | solution.py:93
  156.7 43.5 %all-to-all-start.2 = ((bf16[16,48,2048]{2,1,0:T(8,128)(2,1)}), bf16[16,48,2048]{2,1,0:T(8,128)(2,1)}, u32[]{:S(2)}, u32[]{:S(2)}) async-start(bf16[16,48,2048]{2,1,0:T(8,128)(2,1)} %bitcast.133), calls=%async_computation.2 | async-start | bytes 6291456 | tf_op jit(solution)/shard_map/all_to_all | solution.py:103
  208.0 46.2 %all-to-all-start.3 = ((bf16[16,48,2048]{2,1,0:T(8,128)(2,1)}), bf16[16,48,2048]{2,1,0:T(8,128)(2,1)S(1)}, u32[]{:S(2)}, u32[]{:S(2)}) async-start(bf16[16,48,2048]{2,1,0:T(8,128)(2,1)} %bitcast.39), calls=%async_computation.4 | async-start | bytes 6291456 | tf_op jit(solution)/shard_map/all_to_all | solution.py:103
  216.0 45.0 %reduce-scatter.3.cloned.1.call-start = ((), (), s32[]{:S(2)}) async-start(), calls=%async_computation.6 | async-start | bytes 2359296 | tf_op jit(solution)/shard_map/reduce_scatter | solution.py:99
  216.8 87.3 %reduce-scatter.5.cloned.1.call-start = ((), (), s32[]{:S(2)}) async-start(), calls=%async_computation.7 | async-start | bytes 2359296 | tf_op jit(solution)/shard_map/reduce_scatter | solution.py:109
  261.0 45.0 %copy-start.1 = (bf16[1,768,2048]{2,1,0:T(8,128)(2,1)S(1)}, bf16[1,768,2048]{2,1,0:T(8,128)(2,1)}, u32[]{:S(2)}) copy-start(bf16[1,768,2048]{2,1,0:T(8,128)(2,1)} %param.11) | copy-start | bytes 9437188
Sparse Core Ops, SparseCore 0:
  9.1 43.7 all-gather.7
  54.7 39.6 all-gather.5
  219.4 40.7 reduce-scatter.2
  262.6 41.4 reduce-scatter.4

commit v7 on v6

--- a/solution.py
+++ b/solution.py
@@ -62,7 +62,7 @@
     for h in range(CHUNKS):
         piece = attn_out[h * rows_chunk:(h + 1) * rows_chunk]
         gathered = lax.all_gather(piece, "tp", axis=0)
-        feats = jnp.transpose(gathered, (1, 0, 2)).reshape(rows_chunk, width)
+        feats = gathered.reshape(n_tp, rows_chunk, cols)
 
         blocks = slice(h * blk_chunk, (h + 1) * blk_chunk)
         b_loc = jnp.arange(blk_chunk, dtype=jnp.int32)[:, None, None]
@@ -87,9 +87,9 @@
             for g_part in (g_hi, g_lo)
         ], axis=0)
 
-        outgoing = jnp.dot(
-            select, feats, preferred_element_type=jnp.bfloat16
-        ).reshape(n_ctx, blk_chunk * per_dest, width)
+        outgoing = jnp.einsum(
+            "rt,stf->rsf", select, feats, preferred_element_type=jnp.bfloat16
+        ).reshape(n_ctx, blk_chunk * per_dest, n_tp, cols)
         received = lax.all_to_all(outgoing, "ctx", split_axis=0, concat_axis=0, tiled=True)
         rows = received.reshape(n_ctx * blk_chunk, exp_dev, capacity, width)
         rows = jnp.transpose(rows, (1, 0, 2, 3)).reshape(exp_dev, n_ctx * blk_chunk * capacity, width)

time: 313 us -> 307 us (0.981)
  matrix products: 58.2 us -> 49.6 us
    unnamed x11 -> x21, local copies, waits for them, and re-layouts: 0.15 us -> 9.65 us
    all_gather x2 -> x0, local copies, waits for them, and re-layouts: 8.21 us -> none  [on_device(): gathered = lax.all_gather(piece, 'tp', axis=0)]
    all_gather x2, waiting for transfers between devices: 31.5 us -> 37.9 us  [on_device(): gathered = lax.all_gather(piece, 'tp', axis=0)]
    dot_general x2, matrix products: 13.8 us -> 8.06 us  [expert_rows(): jnp.einsum(form + ',ldf->' + hidden_form, features, w_up, preferred_eleme...]
  transfers between devices with their start and end apart: 8 -> 8, of which waited for: 7 -> 7; matrix products, arithmetic and copies ran while one was open for 27% -> 24% of each run, Pallas kernels for 0% -> 0%
where the time goes in v7:
time: 307 us; the launch traced here: 306 us
  waiting for transfers between devices  145 us (47%)
  matrix products  49.6 us (16%)
  starting transfers between devices  32.1 us (10%)
  blocking collectives  28.3 us (9%)
  local copies, waits for them, and re-layouts  20 us (7%)
  other arithmetic  18 us (6%)
  between operations  13.4 us (4%)
    reduce_scatter x1, waiting for transfers between devices, on_device(): lax.psum_scatter(partials[-1], 'tp', scatter_dimension=1, tiled=True)  43.3 us
    all_to_all x2, waiting for transfers between devices, on_device(): lax.all_to_all(result, 'ctx', split_axis=0, concat_axis=0, tiled=True)  42.7 us
    all_gather x2, waiting for transfers between devices, on_device(): gathered = lax.all_gather(piece, 'tp', axis=0)  37.9 us
    all_gather x1, blocking collectives, on_device(): info_all = lax.all_gather(info, 'tp', axis=0)  28.3 us
    dot_general x2, matrix products, expert_rows(): jnp.einsum(hidden_form + ',lfd->' + form, hidden, w_down, preferred_eleme...  22 us
    all_to_all x2, waiting for transfers between devices, on_device(): lax.all_to_all(outgoing, 'ctx', split_axis=0, concat_axis=0, tiled=True)  19.5 us
    all_to_all x2, starting transfers between devices, on_device(): lax.all_to_all(outgoing, 'ctx', split_axis=0, concat_axis=0, tiled=True)  16.1 us
    all_to_all x2, starting transfers between devices, on_device(): lax.all_to_all(result, 'ctx', split_axis=0, concat_axis=0, tiled=True)  15.7 us
  transfers between devices with their start and end apart: 8, of which 7 were waited for; matrix products, arithmetic and copies ran while one was open for 24% of the time, Pallas kernels for 0%

profile of v7, /device:TPU:2, one launch (start us, length us, event | category | flops | bytes accessed | tf_op | source)
XLA Modules:
  0.0 306.3 jit_solution(2025134372665787714)
XLA Ops:
  6.5 2.0 fusion.180
  12.6 28.3 %all-gather = f32[1024,24]{0,1:T(8,128)S(1)} all-gather(f32[128,24]{0,1:T(8,128)S(1)} %pad_maximum_fusion.1), channel_id=2, replica_groups=mesh['ctx'=16,'tp'=8,'dp'=2] {'tp'}, dimensions={0}, use_global_device_ids=true | all-gather | bytes 110592 | tf_op jit(solution)/shard_map/all_gather | solution.py:49
  41.1 11.8 %all-gather.8.cloned.1.call-done = bf16[4096,256]{1,0:T(8,128)(2,1)} async-done(((bf16[512,256]{1,0:T(8,128)(2,1)}), bf16[4096,256]{1,0:T(8,128)(2,1)}) %all-gather.8.cloned.1.call-update) | async-done | bytes 2097168 | tf_op jit(solution)/shard_map/all_gather | solution.py:64
  52.9 4.5 %fusion.77 = bf16[768,8,256]{2,0,1:T(8,128)(2,1)S(1)} fusion(bf16[8,512,256]{2,1,0:T(8,128)(2,1)} %bitcast.201, s32[512]{0:T(512)S(1)} %bitcast.179, s32[512]{0:T(512)S(1)} %bitcast.182, s32[512]{0:T(512)S(1)} %bitcast.185, s32[512]{0:T(512)S(1)} %bitcast.188, s32[512]{0:T(512)S(1)} %bitcast.191, s32[512]{0:T(512)S(1)} %bitcast.194, s32[512]{0:T(512)S(1)} %bitcast.197, ...), kind=kOutput, calls=%fused_computation.109 | convolution fusion | flops 1623195648 | bytes 5259264 | tf_op jit(solution)/shard_map/rt,stf->rsf/dot_general | solution.py:90
  57.4 3.5 %copy.30 = bf16[16,48,8,256]{3,2,1,0:T(8,128)(2,1)} copy(bf16[16,48,8,256]{3,1,0,2:T(8,128)(2,1)S(1)} %bitcast.142) | data formatting | bytes 6291456 | tf_op jit(solution)/shard_map/reshape | solution.py:92
  60.9 7.6 %all-to-all-start.1 = ((bf16[16,48,8,256]{3,2,1,0:T(8,128)(2,1)}), bf16[16,48,8,256]{3,2,1,0:T(8,128)(2,1)}, u32[]{:S(2)}, u32[]{:S(2)}) async-start(bf16[16,48,8,256]{3,2,1,0:T(8,128)(2,1)} %copy.30), calls=%async_computation.1 | async-start | bytes 6291456 | tf_op jit(solution)/shard_map/all_to_all | solution.py:93
  68.4 26.1 %all-gather.6.cloned.1.call-done = bf16[4096,256]{1,0:T(8,128)(2,1)} async-done(((bf16[512,256]{1,0:T(8,128)(2,1)}), bf16[4096,256]{1,0:T(8,128)(2,1)}) %all-gather.6.cloned.1.call-update) | async-done | bytes 2097168 | tf_op jit(solution)/shard_map/all_gather | solution.py:64
  94.6 4.5 %fusion.94 = bf16[768,8,256]{2,0,1:T(8,128)(2,1)S(1)} fusion(bf16[8,512,256]{2,1,0:T(8,128)(2,1)} %bitcast.200, s32[512]{0:T(512)S(1)} %bitcast.155, s32[512]{0:T(512)S(1)} %bitcast.158, s32[512]{0:T(512)S(1)} %bitcast.161, s32[512]{0:T(512)S(1)} %bitcast.164, s32[512]{0:T(512)S(1)} %bitcast.167, s32[512]{0:T(512)S(1)} %bitcast.170, s32[512]{0:T(512)S(1)} %bitcast.173, ...), kind=kOutput, calls=%fused_computation.118 | convolution fusion | flops 1623195648 | bytes 5259264 | tf_op jit(solution)/shard_map/rt,stf->rsf/dot_general | solution.py:90
  99.0 3.5 %copy.29 = bf16[16,48,8,256]{3,2,1,0:T(8,128)(2,1)} copy(bf16[16,48,8,256]{3,1,0,2:T(8,128)(2,1)S(1)} %bitcast.143) | data formatting | bytes 6291456 | tf_op jit(solution)/shard_map/reshape | solution.py:92
  103.9 8.5 %all-to-all-start = ((bf16[16,48,8,256]{3,2,1,0:T(8,128)(2,1)}), bf16[16,48,8,256]{3,2,1,0:T(8,128)(2,1)}, u32[]{:S(2)}, u32[]{:S(2)}) async-start(bf16[16,48,8,256]{3,2,1,0:T(8,128)(2,1)} %copy.29), calls=%async_computation | async-start | bytes 6291456 | tf_op jit(solution)/shard_map/all_to_all | solution.py:93
  112.5 3.1 %copy.36 = bf16[96,8,8,256]{3,1,2,0:T(8,128)(2,1)S(1)} copy(bf16[96,8,8,256]{3,2,1,0:T(8,128)(2,1)} %bitcast.62) | data formatting | bytes 6291456
  115.7 1.6 copy-done.2
  117.3 4.0 %fusion.4 = f32[768,768]{1,0:T(8,128)} fusion(bf16[768,2048]{1,0:T(8,128)(2,1)S(1)} %bitcast.138, bf16[1,2048,768]{2,1,0:T(8,128)(2,1)S(1)} %copy-done.6), kind=kOutput, calls=%fused_computation.8 | convolution fusion | flops 2415919104 | bytes 8650752 | tf_op jit(solution)/shard_map/lsd,ldf->lsf/dot_general | solution.py:21
  121.3 11.0 %convolution_convert_fusion = bf16[768,2048]{1,0:T(8,128)(2,1)} fusion(bf16[1,768,2048]{2,1,0:T(8,128)(2,1)S(1)} %copy-done, f32[768,768]{1,0:T(8,128)} %fusion.4, bf16[768,2048]{1,0:T(8,128)(2,1)} %bitcast.139, bf16[1,2048,768]{2,1,0:T(8,128)(2,1)} %param.9), kind=kOutput, calls=%fused_computation.4 | convolution fusion | flops 4836950016 | bytes 14942208 | tf_op jit(solution)/shard_map/lsf,lfd->lsd/dot_general | solution.py:25
  132.3 18.1 %all-to-all-done = bf16[16,48,8,256]{3,2,1,0:T(8,128)(2,1)} async-done(((bf16[16,48,8,256]{3,2,1,0:T(8,128)(2,1)}), bf16[16,48,8,256]{3,2,1,0:T(8,128)(2,1)}, u32[]{:S(2)}, u32[]{:S(2)}) %all-to-all-start) | async-done | bytes 3145760 | tf_op jit(solution)/shard_map/all_to_all | solution.py:93
  150.4 7.8 %all-to-all-start.2 = ((bf16[16,48,2048]{2,1,0:T(8,128)(2,1)}), bf16[16,48,2048]{2,1,0:T(8,128)(2,1)}, u32[]{:S(2)}, u32[]{:S(2)}) async-start(bf16[16,48,2048]{2,1,0:T(8,128)(2,1)} %bitcast.137), calls=%async_computation.2 | async-start | bytes 6291456 | tf_op jit(solution)/shard_map/all_to_all | solution.py:103
  158.2 2.6 fusion.115
  160.8 2.5 fusion.122
  163.3 3.1 %copy.33 = bf16[96,8,8,256]{3,1,2,0:T(8,128)(2,1)S(1)} copy(bf16[96,8,8,256]{3,2,1,0:T(8,128)(2,1)} %bitcast.51) | data formatting | bytes 6291456
  168.1 4.0 %fusion.6 = f32[768,768]{1,0:T(8,128)} fusion(bf16[768,2048]{1,0:T(8,128)(2,1)S(1)} %bitcast.140, bf16[1,2048,768]{2,1,0:T(8,128)(2,1)S(1)} %copy-done.7), kind=kOutput, calls=%fused_computation.10 | convolution fusion | flops 2415919104 | bytes 8650752 | tf_op jit(solution)/shard_map/lsd,ldf->lsf/dot_general | solution.py:21
  172.1 11.0 %fusion.12 = bf16[1,768,2048]{2,1,0:T(8,128)(2,1)} fusion(bf16[1,768,2048]{2,1,0:T(8,128)(2,1)S(1)} %copy-done, f32[768,768]{1,0:T(8,128)} %fusion.6, bf16[768,2048]{1,0:T(8,128)(2,1)} %bitcast.141, bf16[1,2048,768]{2,1,0:T(8,128)(2,1)} %param.9), kind=kOutput, calls=%fused_computation.16 | convolution fusion | flops 4836950016 | bytes 14942208 | tf_op jit(solution)/shard_map/lsf,lfd->lsd/dot_general | solution.py:25
  183.1 10.8 %all-to-all-done.2 = bf16[16,48,2048]{2,1,0:T(8,128)(2,1)} async-done(((bf16[16,48,2048]{2,1,0:T(8,128)(2,1)}), bf16[16,48,2048]{2,1,0:T(8,128)(2,1)}, u32[]{:S(2)}, u32[]{:S(2)}) %all-to-all-start.2) | async-done | bytes 3145760 | tf_op jit(solution)/shard_map/all_to_all | solution.py:103
  194.0 5.8 %fusion.19 = f32[1024,2048]{1,0:T(8,128)S(1)} fusion(bf16[768,2048]{1,0:T(8,128)(2,1)} %bitcast.37, bf16[512,768]{1,0:T(8,128)(2,1)} %fusion.122, bf16[512,768]{1,0:T(8,128)(2,1)} %fusion.115), kind=kOutput, calls=%fused_computation.19 | convolution fusion | flops 3224371200 | bytes 13107200 | tf_op jit(solution)/shard_map/dot_general | solution.py:106
  199.7 2.0 fusion.1
  201.7 8.0 %all-to-all-start.3 = ((bf16[16,48,2048]{2,1,0:T(8,128)(2,1)}), bf16[16,48,2048]{2,1,0:T(8,128)(2,1)S(1)}, u32[]{:S(2)}, u32[]{:S(2)}) async-start(bf16[16,48,2048]{2,1,0:T(8,128)(2,1)} %bitcast.39), calls=%async_computation.4 | async-start | bytes 6291456 | tf_op jit(solution)/shard_map/all_to_all | solution.py:103
  210.8 2.6 fusion.129
  213.4 2.5 fusion.136
  215.9 31.9 %all-to-all-done.3 = bf16[16,48,2048]{2,1,0:T(8,128)(2,1)S(1)} async-done(((bf16[16,48,2048]{2,1,0:T(8,128)(2,1)}), bf16[16,48,2048]{2,1,0:T(8,128)(2,1)S(1)}, u32[]{:S(2)}, u32[]{:S(2)}) %all-to-all-start.3) | async-done | bytes 3145760 | tf_op jit(solution)/shard_map/all_to_all | solution.py:103
  247.9 4.8 %fusion.23 = f32[1024,2048]{1,0:T(8,128)S(1)} fusion(bf16[768,2048]{1,0:T(8,128)(2,1)S(1)} %bitcast.136, bf16[512,768]{1,0:T(8,128)(2,1)} %fusion.136, bf16[512,768]{1,0:T(8,128)(2,1)} %fusion.129), kind=kOutput, calls=%fused_computation.23 | convolution fusion | flops 3224371200 | bytes 13107200 | tf_op jit(solution)/shard_map/dot_general | solution.py:106
  252.7 1.9 fusion
  254.6 43.3 %reduce-scatter.5.cloned.1.call-done = bf16[512,256]{1,0:T(8,128)(2,1)} async-done(((bf16[512,2048]{1,0:T(8,128)(2,1)}), bf16[512,256]{1,0:T(8,128)(2,1)}) %reduce-scatter.5.cloned.1.call-update) | async-done | bytes 262160 | tf_op jit(solution)/shard_map/reduce_scatter | solution.py:109
  297.9 1.9 pad_maximum_fusion
  (54 shorter events, 8.5 us)
Async XLA Ops:
  6.5 114.8 %copy-start = (bf16[1,768,2048]{2,1,0:T(8,128)(2,1)S(1)}, bf16[1,768,2048]{2,1,0:T(8,128)(2,1)}, u32[]{:S(2)}) copy-start(bf16[1,768,2048]{2,1,0:T(8,128)(2,1)} %param.11) | copy-start | bytes 9437188
  6.5 2.8 copy-start.4
  6.5 46.4 %all-gather.8.cloned.1.call-start = ((), (), s32[]{:S(2)}) async-start(), calls=%async_computation.9 | async-start | bytes 2359296 | tf_op jit(solution)/shard_map/all_gather | solution.py:64
  8.6 86.0 %all-gather.6.cloned.1.call-start = ((), (), s32[]{:S(2)}) async-start(), calls=%async_computation.8 | async-start | bytes 2359296 | tf_op jit(solution)/shard_map/all_gather | solution.py:64
  10.1 2.5 copy-start.5
  60.9 43.1 %all-to-all-start.1 = ((bf16[16,48,8,256]{3,2,1,0:T(8,128)(2,1)}), bf16[16,48,8,256]{3,2,1,0:T(8,128)(2,1)}, u32[]{:S(2)}, u32[]{:S(2)}) async-start(bf16[16,48,8,256]{3,2,1,0:T(8,128)(2,1)} %copy.30), calls=%async_computation.1 | async-start | bytes 6291456 | tf_op jit(solution)/shard_map/all_to_all | solution.py:93
  103.9 46.5 %all-to-all-start = ((bf16[16,48,8,256]{3,2,1,0:T(8,128)(2,1)}), bf16[16,48,8,256]{3,2,1,0:T(8,128)(2,1)}, u32[]{:S(2)}, u32[]{:S(2)}) async-start(bf16[16,48,8,256]{3,2,1,0:T(8,128)(2,1)} %copy.29), calls=%async_computation | async-start | bytes 6291456 | tf_op jit(solution)/shard_map/all_to_all | solution.py:93
  112.5 4.8 %copy-start.6 = (bf16[1,2048,768]{2,1,0:T(8,128)(2,1)S(1)}, bf16[1,2048,768]{2,1,0:T(8,128)(2,1)}, u32[]{:S(2)}) copy-start(bf16[1,2048,768]{2,1,0:T(8,128)(2,1)} %param.10) | copy-start | bytes 9437188
  115.7 1.6 copy-start.2
  150.4 43.5 %all-to-all-start.2 = ((bf16[16,48,2048]{2,1,0:T(8,128)(2,1)}), bf16[16,48,2048]{2,1,0:T(8,128)(2,1)}, u32[]{:S(2)}, u32[]{:S(2)}) async-start(bf16[16,48,2048]{2,1,0:T(8,128)(2,1)} %bitcast.137), calls=%async_computation.2 | async-start | bytes 6291456 | tf_op jit(solution)/shard_map/all_to_all | solution.py:103
  163.3 4.8 %copy-start.7 = (bf16[1,2048,768]{2,1,0:T(8,128)(2,1)S(1)}, bf16[1,2048,768]{2,1,0:T(8,128)(2,1)}, u32[]{:S(2)}) copy-start(bf16[1,2048,768]{2,1,0:T(8,128)(2,1)} %param.10) | copy-start | bytes 9437188
  166.4 1.6 copy-start.3
  201.7 46.1 %all-to-all-start.3 = ((bf16[16,48,2048]{2,1,0:T(8,128)(2,1)}), bf16[16,48,2048]{2,1,0:T(8,128)(2,1)S(1)}, u32[]{:S(2)}, u32[]{:S(2)}) async-start(bf16[16,48,2048]{2,1,0:T(8,128)(2,1)} %bitcast.39), calls=%async_computation.4 | async-start | bytes 6291456 | tf_op jit(solution)/shard_map/all_to_all | solution.py:103
  209.7 45.0 %reduce-scatter.3.cloned.1.call-start = ((), (), s32[]{:S(2)}) async-start(), calls=%async_computation.6 | async-start | bytes 2359296 | tf_op jit(solution)/shard_map/reduce_scatter | solution.py:99
  210.4 87.5 %reduce-scatter.5.cloned.1.call-start = ((), (), s32[]{:S(2)}) async-start(), calls=%async_computation.7 | async-start | bytes 2359296 | tf_op jit(solution)/shard_map/reduce_scatter | solution.py:109
  254.6 45.2 %copy-start.1 = (bf16[1,768,2048]{2,1,0:T(8,128)(2,1)S(1)}, bf16[1,768,2048]{2,1,0:T(8,128)(2,1)}, u32[]{:S(2)}) copy-start(bf16[1,768,2048]{2,1,0:T(8,128)(2,1)} %param.11) | copy-start | bytes 9437188
Sparse Core Ops, SparseCore 0:
  9.1 43.7 all-gather.7
  54.7 39.8 all-gather.5
  213.0 40.8 reduce-scatter.2
  256.3 41.5 reduce-scatter.4

commit v8 on v7

--- a/solution.py
+++ b/solution.py
@@ -58,7 +58,6 @@
     blk_chunk = n_tp // CHUNKS
     rows_chunk = blk_chunk * tok_blk
     outs = []
-    partials = []
     for h in range(CHUNKS):
         piece = attn_out[h * rows_chunk:(h + 1) * rows_chunk]
         gathered = lax.all_gather(piece, "tp", axis=0)
@@ -94,9 +93,6 @@
         rows = received.reshape(n_ctx * blk_chunk, exp_dev, capacity, width)
         rows = jnp.transpose(rows, (1, 0, 2, 3)).reshape(exp_dev, n_ctx * blk_chunk * capacity, width)
         result = expert_rows(rows, w_gate, w_up, w_down, "lsd")
-        if h > 0:
-            result, earlier = lax.optimization_barrier((result, partials[-1]))
-            outs.append(lax.psum_scatter(earlier, "tp", scatter_dimension=1, tiled=True))
         result = jnp.transpose(
             result.reshape(exp_dev, n_ctx * blk_chunk, capacity, width), (1, 0, 2, 3)
         ).reshape(n_ctx, blk_chunk * per_dest, width)
@@ -105,8 +101,7 @@
 
         both = jnp.dot(w_both, returned, preferred_element_type=jnp.float32)
         partial = (both[:rows_chunk] + both[rows_chunk:]).astype(jnp.bfloat16)
-        partials.append(partial)
-    outs.append(lax.psum_scatter(partials[-1], "tp", scatter_dimension=1, tiled=True))
+        outs.append(lax.psum_scatter(partial, "tp", scatter_dimension=1, tiled=True))
     return jnp.concatenate(outs, axis=0)
 
 

time: 307 us -> 304 us (level)
    all_to_all x2, waiting for transfers between devices: 42.7 us -> 35.6 us  [on_device(): lax.all_to_all(result, 'ctx', split_axis=0, concat_axis=0, tiled=True)]
    reduce_scatter x2, waiting for transfers between devices: 43.3 us -> 48.1 us  [on_device(): lax.psum_scatter(partial, 'tp', scatter_dimension=1, tiled=True)]
  transfers between devices with their start and end apart: 8 -> 8, of which waited for: 7 -> 8; matrix products, arithmetic and copies ran while one was open for 24% -> 27% of each run, Pallas kernels for 0% -> 0%
where the time goes in v8:
time: 304 us; the launch traced here: 303 us
  waiting for transfers between devices  142 us (47%)
  matrix products  49.6 us (16%)
  starting transfers between devices  32.1 us (11%)
  blocking collectives  28.3 us (9%)
  local copies, waits for them, and re-layouts  20 us (7%)
  other arithmetic  18 us (6%)
  between operations  13.3 us (4%)
    reduce_scatter x2, waiting for transfers between devices, on_device(): lax.psum_scatter(partial, 'tp', scatter_dimension=1, tiled=True)  48.1 us
    all_gather x2, waiting for transfers between devices, on_device(): gathered = lax.all_gather(piece, 'tp', axis=0)  37.9 us
    all_to_all x2, waiting for transfers between devices, on_device(): lax.all_to_all(result, 'ctx', split_axis=0, concat_axis=0, tiled=True)  35.6 us
    all_gather x1, blocking collectives, on_device(): info_all = lax.all_gather(info, 'tp', axis=0)  28.3 us
    dot_general x2, matrix products, expert_rows(): jnp.einsum(hidden_form + ',lfd->' + form, hidden, w_down, preferred_eleme...  22 us
    all_to_all x2, waiting for transfers between devices, on_device(): lax.all_to_all(outgoing, 'ctx', split_axis=0, concat_axis=0, tiled=True)  19.5 us
    all_to_all x2, starting transfers between devices, on_device(): lax.all_to_all(outgoing, 'ctx', split_axis=0, concat_axis=0, tiled=True)  16.1 us
    all_to_all x2, starting transfers between devices, on_device(): lax.all_to_all(result, 'ctx', split_axis=0, concat_axis=0, tiled=True)  15.7 us
  transfers between devices with their start and end apart: 8, of which 8 were waited for; matrix products, arithmetic and copies ran while one was open for 27% of the time, Pallas kernels for 0%

profile of v8, /device:TPU:2, one launch (start us, length us, event | category | flops | bytes accessed | tf_op | source)
XLA Modules:
  0.0 303.3 jit_solution(7451028848380125201)
XLA Ops:
  6.5 2.0 fusion.177
  12.6 28.3 %all-gather = f32[1024,24]{0,1:T(8,128)S(1)} all-gather(f32[128,24]{0,1:T(8,128)S(1)} %pad_maximum_fusion.1), channel_id=2, replica_groups=mesh['ctx'=16,'tp'=8,'dp'=2] {'tp'}, dimensions={0}, use_global_device_ids=true | all-gather | bytes 110592 | tf_op jit(solution)/shard_map/all_gather | solution.py:49
  41.1 11.8 %all-gather.6.cloned.1.call-done = bf16[4096,256]{1,0:T(8,128)(2,1)} async-done(((bf16[512,256]{1,0:T(8,128)(2,1)}), bf16[4096,256]{1,0:T(8,128)(2,1)}) %all-gather.6.cloned.1.call-update) | async-done | bytes 2097168 | tf_op jit(solution)/shard_map/all_gather | solution.py:63
  52.9 4.5 %fusion.91 = bf16[768,8,256]{2,0,1:T(8,128)(2,1)S(1)} fusion(bf16[8,512,256]{2,1,0:T(8,128)(2,1)} %bitcast.198, s32[512]{0:T(512)S(1)} %bitcast.176, s32[512]{0:T(512)S(1)} %bitcast.179, s32[512]{0:T(512)S(1)} %bitcast.182, s32[512]{0:T(512)S(1)} %bitcast.185, s32[512]{0:T(512)S(1)} %bitcast.188, s32[512]{0:T(512)S(1)} %bitcast.191, s32[512]{0:T(512)S(1)} %bitcast.194, ...), kind=kOutput, calls=%fused_computation.117 | convolution fusion | flops 1623195648 | bytes 5259264 | tf_op jit(solution)/shard_map/rt,stf->rsf/dot_general | solution.py:89
  57.4 3.5 %copy.29 = bf16[16,48,8,256]{3,2,1,0:T(8,128)(2,1)} copy(bf16[16,48,8,256]{3,1,0,2:T(8,128)(2,1)S(1)} %bitcast.139) | data formatting | bytes 6291456 | tf_op jit(solution)/shard_map/reshape | solution.py:91
  60.9 7.6 %all-to-all-start = ((bf16[16,48,8,256]{3,2,1,0:T(8,128)(2,1)}), bf16[16,48,8,256]{3,2,1,0:T(8,128)(2,1)}, u32[]{:S(2)}, u32[]{:S(2)}) async-start(bf16[16,48,8,256]{3,2,1,0:T(8,128)(2,1)} %copy.29), calls=%async_computation | async-start | bytes 6291456 | tf_op jit(solution)/shard_map/all_to_all | solution.py:92
  68.4 26.1 %all-gather.8.cloned.1.call-done = bf16[4096,256]{1,0:T(8,128)(2,1)} async-done(((bf16[512,256]{1,0:T(8,128)(2,1)}), bf16[4096,256]{1,0:T(8,128)(2,1)}) %all-gather.8.cloned.1.call-update) | async-done | bytes 2097168 | tf_op jit(solution)/shard_map/all_gather | solution.py:63
  94.6 4.5 %fusion.74 = bf16[768,8,256]{2,0,1:T(8,128)(2,1)S(1)} fusion(bf16[8,512,256]{2,1,0:T(8,128)(2,1)} %bitcast.197, s32[512]{0:T(512)S(1)} %bitcast.152, s32[512]{0:T(512)S(1)} %bitcast.155, s32[512]{0:T(512)S(1)} %bitcast.158, s32[512]{0:T(512)S(1)} %bitcast.161, s32[512]{0:T(512)S(1)} %bitcast.164, s32[512]{0:T(512)S(1)} %bitcast.167, s32[512]{0:T(512)S(1)} %bitcast.170, ...), kind=kOutput, calls=%fused_computation.108 | convolution fusion | flops 1623195648 | bytes 5259264 | tf_op jit(solution)/shard_map/rt,stf->rsf/dot_general | solution.py:89
  99.0 3.5 %copy.30 = bf16[16,48,8,256]{3,2,1,0:T(8,128)(2,1)} copy(bf16[16,48,8,256]{3,1,0,2:T(8,128)(2,1)S(1)} %bitcast.140) | data formatting | bytes 6291456 | tf_op jit(solution)/shard_map/reshape | solution.py:91
  103.9 8.5 %all-to-all-start.2 = ((bf16[16,48,8,256]{3,2,1,0:T(8,128)(2,1)}), bf16[16,48,8,256]{3,2,1,0:T(8,128)(2,1)}, u32[]{:S(2)}, u32[]{:S(2)}) async-start(bf16[16,48,8,256]{3,2,1,0:T(8,128)(2,1)} %copy.30), calls=%async_computation.3 | async-start | bytes 6291456 | tf_op jit(solution)/shard_map/all_to_all | solution.py:92
  112.5 3.1 %copy.34 = bf16[96,8,8,256]{3,1,2,0:T(8,128)(2,1)S(1)} copy(bf16[96,8,8,256]{3,2,1,0:T(8,128)(2,1)} %bitcast.54) | data formatting | bytes 6291456
  117.3 4.0 %fusion.6 = f32[768,768]{1,0:T(8,128)} fusion(bf16[768,2048]{1,0:T(8,128)(2,1)S(1)} %bitcast.135, bf16[1,2048,768]{2,1,0:T(8,128)(2,1)S(1)} %copy-done.6), kind=kOutput, calls=%fused_computation.10 | convolution fusion | flops 2415919104 | bytes 8650752 | tf_op jit(solution)/shard_map/lsd,ldf->lsf/dot_general | solution.py:21
  121.3 11.0 %convolution_convert_fusion.1 = bf16[768,2048]{1,0:T(8,128)(2,1)} fusion(bf16[1,768,2048]{2,1,0:T(8,128)(2,1)S(1)} %copy-done, f32[768,768]{1,0:T(8,128)} %fusion.6, bf16[768,2048]{1,0:T(8,128)(2,1)} %bitcast.136, bf16[1,2048,768]{2,1,0:T(8,128)(2,1)} %param.9), kind=kOutput, calls=%fused_computation.5 | convolution fusion | flops 4836950016 | bytes 14942208 | tf_op jit(solution)/shard_map/lsf,lfd->lsd/dot_general | solution.py:25
  132.3 18.1 %all-to-all-done.2 = bf16[16,48,8,256]{3,2,1,0:T(8,128)(2,1)} async-done(((bf16[16,48,8,256]{3,2,1,0:T(8,128)(2,1)}), bf16[16,48,8,256]{3,2,1,0:T(8,128)(2,1)}, u32[]{:S(2)}, u32[]{:S(2)}) %all-to-all-start.2) | async-done | bytes 3145760 | tf_op jit(solution)/shard_map/all_to_all | solution.py:92
  150.4 7.8 %all-to-all-start.1 = ((bf16[16,48,2048]{2,1,0:T(8,128)(2,1)}), bf16[16,48,2048]{2,1,0:T(8,128)(2,1)}, u32[]{:S(2)}, u32[]{:S(2)}) async-start(bf16[16,48,2048]{2,1,0:T(8,128)(2,1)} %bitcast.134), calls=%async_computation.1 | async-start | bytes 6291456 | tf_op jit(solution)/shard_map/all_to_all | solution.py:99
  158.2 2.6 fusion.112
  160.8 2.5 fusion.119
  163.3 3.1 %copy.37 = bf16[96,8,8,256]{3,1,2,0:T(8,128)(2,1)S(1)} copy(bf16[96,8,8,256]{3,2,1,0:T(8,128)(2,1)} %bitcast.65) | data formatting | bytes 6291456
  168.1 4.0 %fusion.4 = f32[768,768]{1,0:T(8,128)} fusion(bf16[768,2048]{1,0:T(8,128)(2,1)S(1)} %bitcast.137, bf16[1,2048,768]{2,1,0:T(8,128)(2,1)S(1)} %copy-done.7), kind=kOutput, calls=%fused_computation.8 | convolution fusion | flops 2415919104 | bytes 8650752 | tf_op jit(solution)/shard_map/lsd,ldf->lsf/dot_general | solution.py:21
  172.1 11.0 %convolution_convert_fusion = bf16[768,2048]{1,0:T(8,128)(2,1)} fusion(bf16[1,768,2048]{2,1,0:T(8,128)(2,1)S(1)} %copy-done, f32[768,768]{1,0:T(8,128)} %fusion.4, bf16[768,2048]{1,0:T(8,128)(2,1)} %bitcast.138, bf16[1,2048,768]{2,1,0:T(8,128)(2,1)} %param.9), kind=kOutput, calls=%fused_computation.4 | convolution fusion | flops 4836950016 | bytes 14942208 | tf_op jit(solution)/shard_map/lsf,lfd->lsd/dot_general | solution.py:25
  183.1 10.8 %all-to-all-done.1 = bf16[16,48,2048]{2,1,0:T(8,128)(2,1)} async-done(((bf16[16,48,2048]{2,1,0:T(8,128)(2,1)}), bf16[16,48,2048]{2,1,0:T(8,128)(2,1)}, u32[]{:S(2)}, u32[]{:S(2)}) %all-to-all-start.1) | async-done | bytes 3145760 | tf_op jit(solution)/shard_map/all_to_all | solution.py:99
  194.0 8.0 %all-to-all-start.3 = ((bf16[16,48,2048]{2,1,0:T(8,128)(2,1)}), bf16[16,48,2048]{2,1,0:T(8,128)(2,1)S(1)}, u32[]{:S(2)}, u32[]{:S(2)}) async-start(bf16[16,48,2048]{2,1,0:T(8,128)(2,1)} %bitcast.132), calls=%async_computation.4 | async-start | bytes 6291456 | tf_op jit(solution)/shard_map/all_to_all | solution.py:99
  201.9 5.8 %fusion.16 = f32[1024,2048]{1,0:T(8,128)S(1)} fusion(bf16[768,2048]{1,0:T(8,128)(2,1)} %bitcast.24, bf16[512,768]{1,0:T(8,128)(2,1)} %fusion.119, bf16[512,768]{1,0:T(8,128)(2,1)} %fusion.112), kind=kOutput, calls=%fused_computation.18 | convolution fusion | flops 3224371200 | bytes 13107200 | tf_op jit(solution)/shard_map/dot_general | solution.py:102
  207.7 2.0 fusion.1
  210.2 2.6 fusion.126
  212.8 2.5 fusion.133
  215.3 24.8 %all-to-all-done.3 = bf16[16,48,2048]{2,1,0:T(8,128)(2,1)S(1)} async-done(((bf16[16,48,2048]{2,1,0:T(8,128)(2,1)}), bf16[16,48,2048]{2,1,0:T(8,128)(2,1)S(1)}, u32[]{:S(2)}, u32[]{:S(2)}) %all-to-all-start.3) | async-done | bytes 3145760 | tf_op jit(solution)/shard_map/all_to_all | solution.py:99
  240.1 4.8 %fusion.20 = f32[1024,2048]{1,0:T(8,128)S(1)} fusion(bf16[768,2048]{1,0:T(8,128)(2,1)S(1)} %bitcast.133, bf16[512,768]{1,0:T(8,128)(2,1)} %fusion.133, bf16[512,768]{1,0:T(8,128)(2,1)} %fusion.126), kind=kOutput, calls=%fused_computation.22 | convolution fusion | flops 3224371200 | bytes 13107200 | tf_op jit(solution)/shard_map/dot_general | solution.py:102
  244.9 1.9 fusion
  246.8 3.9 %reduce-scatter.3.cloned.1.call-done = bf16[512,256]{1,0:T(8,128)(2,1)} async-done(((bf16[512,2048]{1,0:T(8,128)(2,1)}), bf16[512,256]{1,0:T(8,128)(2,1)}) %reduce-scatter.3.cloned.1.call-update) | async-done | bytes 262160 | tf_op jit(solution)/shard_map/reduce_scatter | solution.py:104
  250.7 44.2 %reduce-scatter.5.cloned.1.call-done = bf16[512,256]{1,0:T(8,128)(2,1)} async-done(((bf16[512,2048]{1,0:T(8,128)(2,1)}), bf16[512,256]{1,0:T(8,128)(2,1)}) %reduce-scatter.5.cloned.1.call-update) | async-done | bytes 262160 | tf_op jit(solution)/shard_map/reduce_scatter | solution.py:104
  294.9 1.9 pad_maximum_fusion
  (54 shorter events, 9.4 us)
Async XLA Ops:
  6.5 114.8 %copy-start = (bf16[1,768,2048]{2,1,0:T(8,128)(2,1)S(1)}, bf16[1,768,2048]{2,1,0:T(8,128)(2,1)}, u32[]{:S(2)}) copy-start(bf16[1,768,2048]{2,1,0:T(8,128)(2,1)} %param.11) | copy-start | bytes 9437188
  6.5 2.8 copy-start.4
  6.5 46.4 %all-gather.6.cloned.1.call-start = ((), (), s32[]{:S(2)}) async-start(), calls=%async_computation.8 | async-start | bytes 2359296 | tf_op jit(solution)/shard_map/all_gather | solution.py:63
  8.6 86.0 %all-gather.8.cloned.1.call-start = ((), (), s32[]{:S(2)}) async-start(), calls=%async_computation.9 | async-start | bytes 2359296 | tf_op jit(solution)/shard_map/all_gather | solution.py:63
  10.1 2.5 copy-start.5
  60.9 43.1 %all-to-all-start = ((bf16[16,48,8,256]{3,2,1,0:T(8,128)(2,1)}), bf16[16,48,8,256]{3,2,1,0:T(8,128)(2,1)}, u32[]{:S(2)}, u32[]{:S(2)}) async-start(bf16[16,48,8,256]{3,2,1,0:T(8,128)(2,1)} %copy.29), calls=%async_computation | async-start | bytes 6291456 | tf_op jit(solution)/shard_map/all_to_all | solution.py:92
  103.9 46.5 %all-to-all-start.2 = ((bf16[16,48,8,256]{3,2,1,0:T(8,128)(2,1)}), bf16[16,48,8,256]{3,2,1,0:T(8,128)(2,1)}, u32[]{:S(2)}, u32[]{:S(2)}) async-start(bf16[16,48,8,256]{3,2,1,0:T(8,128)(2,1)} %copy.30), calls=%async_computation.3 | async-start | bytes 6291456 | tf_op jit(solution)/shard_map/all_to_all | solution.py:92
  112.5 4.8 %copy-start.6 = (bf16[1,2048,768]{2,1,0:T(8,128)(2,1)S(1)}, bf16[1,2048,768]{2,1,0:T(8,128)(2,1)}, u32[]{:S(2)}) copy-start(bf16[1,2048,768]{2,1,0:T(8,128)(2,1)} %param.10) | copy-start | bytes 9437188
  115.7 1.6 copy-start.2
  150.4 43.5 %all-to-all-start.1 = ((bf16[16,48,2048]{2,1,0:T(8,128)(2,1)}), bf16[16,48,2048]{2,1,0:T(8,128)(2,1)}, u32[]{:S(2)}, u32[]{:S(2)}) async-start(bf16[16,48,2048]{2,1,0:T(8,128)(2,1)} %bitcast.134), calls=%async_computation.1 | async-start | bytes 6291456 | tf_op jit(solution)/shard_map/all_to_all | solution.py:99
  163.3 4.8 %copy-start.7 = (bf16[1,2048,768]{2,1,0:T(8,128)(2,1)S(1)}, bf16[1,2048,768]{2,1,0:T(8,128)(2,1)}, u32[]{:S(2)}) copy-start(bf16[1,2048,768]{2,1,0:T(8,128)(2,1)} %param.10) | copy-start | bytes 9437188
  166.4 1.6 copy-start.3
  194.0 46.1 %all-to-all-start.3 = ((bf16[16,48,2048]{2,1,0:T(8,128)(2,1)}), bf16[16,48,2048]{2,1,0:T(8,128)(2,1)S(1)}, u32[]{:S(2)}, u32[]{:S(2)}) async-start(bf16[16,48,2048]{2,1,0:T(8,128)(2,1)} %bitcast.132), calls=%async_computation.4 | async-start | bytes 6291456 | tf_op jit(solution)/shard_map/all_to_all | solution.py:99
  201.9 48.8 %reduce-scatter.3.cloned.1.call-start = ((), (), s32[]{:S(2)}) async-start(), calls=%async_computation.6 | async-start | bytes 2359296 | tf_op jit(solution)/shard_map/reduce_scatter | solution.py:104
  209.7 85.2 %reduce-scatter.5.cloned.1.call-start = ((), (), s32[]{:S(2)}) async-start(), calls=%async_computation.7 | async-start | bytes 2359296 | tf_op jit(solution)/shard_map/reduce_scatter | solution.py:104
  246.8 50.0 %copy-start.1 = (bf16[1,768,2048]{2,1,0:T(8,128)(2,1)S(1)}, bf16[1,768,2048]{2,1,0:T(8,128)(2,1)}, u32[]{:S(2)}) copy-start(bf16[1,768,2048]{2,1,0:T(8,128)(2,1)} %param.11) | copy-start | bytes 9437188
Sparse Core Ops, SparseCore 0:
  9.1 43.7 all-gather.5
  54.7 39.8 all-gather.7
  209.9 40.7 reduce-scatter.2
  253.1 41.7 reduce-scatter.4

commit v9 on v8

--- a/solution.py
+++ b/solution.py
@@ -86,6 +86,7 @@
             for g_part in (g_hi, g_lo)
         ], axis=0)
 
+        select = lax.optimization_barrier(select)
         outgoing = jnp.einsum(
             "rt,stf->rsf", select, feats, preferred_element_type=jnp.bfloat16
         ).reshape(n_ctx, blk_chunk * per_dest, n_tp, cols)

time: 304 us -> 303 us (level)
  other arithmetic: 18 us -> 22.9 us
  waiting for transfers between devices: 142 us -> 138 us
    add x0 -> x2, other arithmetic: none -> 4.97 us  [on_device(): sum(((position[k][None, :] == row_ids[:, None]).astype(jnp.bfloat16) for...]
    all_gather x2, waiting for transfers between devices: 37.9 us -> 33.8 us  [on_device(): gathered = lax.all_gather(piece, 'tp', axis=0)]
  transfers between devices with their start and end apart: 8 -> 8, of which waited for: 8 -> 8; matrix products, arithmetic and copies ran while one was open for 27% -> 28% of each run, Pallas kernels for 0% -> 0%
where the time goes in v9:
time: 303 us; the launch traced here: 302 us
  waiting for transfers between devices  138 us (46%)
  matrix products  47.9 us (16%)
  starting transfers between devices  31.9 us (11%)
  blocking collectives  28.3 us (9%)
  other arithmetic  22.9 us (8%)
  local copies, waits for them, and re-layouts  20.1 us (7%)
  between operations  13.4 us (4%)
    reduce_scatter x2, waiting for transfers between devices, on_device(): lax.psum_scatter(partial, 'tp', scatter_dimension=1, tiled=True)  47.9 us
    all_to_all x2, waiting for transfers between devices, on_device(): lax.all_to_all(result, 'ctx', split_axis=0, concat_axis=0, tiled=True)  35.7 us
    all_gather x2, waiting for transfers between devices, on_device(): gathered = lax.all_gather(piece, 'tp', axis=0)  33.8 us
    all_gather x1, blocking collectives, on_device(): info_all = lax.all_gather(info, 'tp', axis=0)  28.3 us
    dot_general x2, matrix products, expert_rows(): jnp.einsum(hidden_form + ',lfd->' + form, hidden, w_down, preferred_eleme...  22 us
    all_to_all x2, waiting for transfers between devices, on_device(): lax.all_to_all(outgoing, 'ctx', split_axis=0, concat_axis=0, tiled=True)  19.6 us
    all_to_all x2, starting transfers between devices, on_device(): lax.all_to_all(outgoing, 'ctx', split_axis=0, concat_axis=0, tiled=True)  16 us
    all_to_all x2, starting transfers between devices, on_device(): lax.all_to_all(result, 'ctx', split_axis=0, concat_axis=0, tiled=True)  15.5 us
  transfers between devices with their start and end apart: 8, of which 8 were waited for; matrix products, arithmetic and copies ran while one was open for 28% of the time, Pallas kernels for 0%

profile of v9, /device:TPU:2, one launch (start us, length us, event | category | flops | bytes accessed | tf_op | source)
XLA Modules:
  0.0 302.1 jit_solution(13275907540772808570)
XLA Ops:
  6.5 2.1 fusion.145
  12.7 28.3 %all-gather = f32[1024,24]{0,1:T(8,128)S(1)} all-gather(f32[128,24]{0,1:T(8,128)S(1)} %pad_maximum_fusion.1), channel_id=2, replica_groups=mesh['ctx'=16,'tp'=8,'dp'=2] {'tp'}, dimensions={0}, use_global_device_ids=true | all-gather | bytes 110592 | tf_op jit(solution)/shard_map/all_gather | solution.py:49
  41.1 2.5 fusion.79
  43.6 9.4 %all-gather.6.cloned.1.call-done = bf16[4096,256]{1,0:T(8,128)(2,1)} async-done(((bf16[512,256]{1,0:T(8,128)(2,1)}), bf16[4096,256]{1,0:T(8,128)(2,1)}) %all-gather.6.cloned.1.call-update) | async-done | bytes 2097168 | tf_op jit(solution)/shard_map/all_gather | solution.py:63
  53.0 3.6 %fusion.116 = bf16[768,8,256]{2,0,1:T(8,128)(2,1)S(1)} fusion(bf16[8,512,256]{2,1,0:T(8,128)(2,1)} %bitcast.198, bf16[768,512]{1,0:T(8,128)(2,1)} %fusion.79), kind=kOutput, calls=%fused_computation.150 | convolution fusion | flops 1610612736 | bytes 6029312 | tf_op jit(solution)/shard_map/rt,stf->rsf/dot_general | solution.py:90
  56.6 3.5 %copy.29 = bf16[16,48,8,256]{3,2,1,0:T(8,128)(2,1)} copy(bf16[16,48,8,256]{3,1,0,2:T(8,128)(2,1)S(1)} %bitcast.135) | data formatting | bytes 6291456 | tf_op jit(solution)/shard_map/reshape | solution.py:92
  60.1 7.5 %all-to-all-start = ((bf16[16,48,8,256]{3,2,1,0:T(8,128)(2,1)}), bf16[16,48,8,256]{3,2,1,0:T(8,128)(2,1)}, u32[]{:S(2)}, u32[]{:S(2)}) async-start(bf16[16,48,8,256]{3,2,1,0:T(8,128)(2,1)} %copy.29), calls=%async_computation | async-start | bytes 6291456 | tf_op jit(solution)/shard_map/all_to_all | solution.py:93
  67.6 2.5 fusion.72
  70.1 24.3 %all-gather.8.cloned.1.call-done = bf16[4096,256]{1,0:T(8,128)(2,1)} async-done(((bf16[512,256]{1,0:T(8,128)(2,1)}), bf16[4096,256]{1,0:T(8,128)(2,1)}) %all-gather.8.cloned.1.call-update) | async-done | bytes 2097168 | tf_op jit(solution)/shard_map/all_gather | solution.py:63
  94.5 3.6 %fusion.114 = bf16[768,8,256]{2,0,1:T(8,128)(2,1)S(1)} fusion(bf16[8,512,256]{2,1,0:T(8,128)(2,1)} %bitcast.197, bf16[768,512]{1,0:T(8,128)(2,1)} %fusion.72), kind=kOutput, calls=%fused_computation.148 | convolution fusion | flops 1610612736 | bytes 6029312 | tf_op jit(solution)/shard_map/rt,stf->rsf/dot_general | solution.py:90
  98.1 3.5 %copy.30 = bf16[16,48,8,256]{3,2,1,0:T(8,128)(2,1)} copy(bf16[16,48,8,256]{3,1,0,2:T(8,128)(2,1)S(1)} %bitcast.136) | data formatting | bytes 6291456 | tf_op jit(solution)/shard_map/reshape | solution.py:92
  103.1 8.5 %all-to-all-start.2 = ((bf16[16,48,8,256]{3,2,1,0:T(8,128)(2,1)}), bf16[16,48,8,256]{3,2,1,0:T(8,128)(2,1)}, u32[]{:S(2)}, u32[]{:S(2)}) async-start(bf16[16,48,8,256]{3,2,1,0:T(8,128)(2,1)} %copy.30), calls=%async_computation.3 | async-start | bytes 6291456 | tf_op jit(solution)/shard_map/all_to_all | solution.py:93
  111.7 3.1 %copy.34 = bf16[96,8,8,256]{3,1,2,0:T(8,128)(2,1)S(1)} copy(bf16[96,8,8,256]{3,2,1,0:T(8,128)(2,1)} %bitcast.54) | data formatting | bytes 6291456
  116.4 4.0 %fusion.6 = f32[768,768]{1,0:T(8,128)} fusion(bf16[768,2048]{1,0:T(8,128)(2,1)S(1)} %bitcast.137, bf16[1,2048,768]{2,1,0:T(8,128)(2,1)S(1)} %copy-done.6), kind=kOutput, calls=%fused_computation.10 | convolution fusion | flops 2415919104 | bytes 8650752 | tf_op jit(solution)/shard_map/lsd,ldf->lsf/dot_general | solution.py:21
  120.5 11.0 %convolution_convert_fusion.1 = bf16[768,2048]{1,0:T(8,128)(2,1)} fusion(bf16[1,768,2048]{2,1,0:T(8,128)(2,1)S(1)} %copy-done, f32[768,768]{1,0:T(8,128)} %fusion.6, bf16[768,2048]{1,0:T(8,128)(2,1)} %bitcast.138, bf16[1,2048,768]{2,1,0:T(8,128)(2,1)} %param.9), kind=kOutput, calls=%fused_computation.5 | convolution fusion | flops 4836950016 | bytes 14942208 | tf_op jit(solution)/shard_map/lsf,lfd->lsd/dot_general | solution.py:25
  131.5 18.1 %all-to-all-done.2 = bf16[16,48,8,256]{3,2,1,0:T(8,128)(2,1)} async-done(((bf16[16,48,8,256]{3,2,1,0:T(8,128)(2,1)}), bf16[16,48,8,256]{3,2,1,0:T(8,128)(2,1)}, u32[]{:S(2)}, u32[]{:S(2)}) %all-to-all-start.2) | async-done | bytes 3145760 | tf_op jit(solution)/shard_map/all_to_all | solution.py:93
  149.5 7.7 %all-to-all-start.1 = ((bf16[16,48,2048]{2,1,0:T(8,128)(2,1)}), bf16[16,48,2048]{2,1,0:T(8,128)(2,1)}, u32[]{:S(2)}, u32[]{:S(2)}) async-start(bf16[16,48,2048]{2,1,0:T(8,128)(2,1)} %bitcast.134), calls=%async_computation.1 | async-start | bytes 6291456 | tf_op jit(solution)/shard_map/all_to_all | solution.py:100
  157.3 2.6 fusion.92
  159.8 2.5 fusion.99
  162.4 3.1 %copy.37 = bf16[96,8,8,256]{3,1,2,0:T(8,128)(2,1)S(1)} copy(bf16[96,8,8,256]{3,2,1,0:T(8,128)(2,1)} %bitcast.65) | data formatting | bytes 6291456
  167.1 4.0 %fusion.4 = f32[768,768]{1,0:T(8,128)} fusion(bf16[768,2048]{1,0:T(8,128)(2,1)S(1)} %bitcast.139, bf16[1,2048,768]{2,1,0:T(8,128)(2,1)S(1)} %copy-done.7), kind=kOutput, calls=%fused_computation.8 | convolution fusion | flops 2415919104 | bytes 8650752 | tf_op jit(solution)/shard_map/lsd,ldf->lsf/dot_general | solution.py:21
  171.2 11.0 %convolution_convert_fusion = bf16[768,2048]{1,0:T(8,128)(2,1)} fusion(bf16[1,768,2048]{2,1,0:T(8,128)(2,1)S(1)} %copy-done, f32[768,768]{1,0:T(8,128)} %fusion.4, bf16[768,2048]{1,0:T(8,128)(2,1)} %bitcast.140, bf16[1,2048,768]{2,1,0:T(8,128)(2,1)} %param.9), kind=kOutput, calls=%fused_computation.4 | convolution fusion | flops 4836950016 | bytes 14942208 | tf_op jit(solution)/shard_map/lsf,lfd->lsd/dot_general | solution.py:25
  182.2 10.9 %all-to-all-done.1 = bf16[16,48,2048]{2,1,0:T(8,128)(2,1)} async-done(((bf16[16,48,2048]{2,1,0:T(8,128)(2,1)}), bf16[16,48,2048]{2,1,0:T(8,128)(2,1)}, u32[]{:S(2)}, u32[]{:S(2)}) %all-to-all-start.1) | async-done | bytes 3145760 | tf_op jit(solution)/shard_map/all_to_all | solution.py:100
  193.1 7.8 %all-to-all-start.3 = ((bf16[16,48,2048]{2,1,0:T(8,128)(2,1)}), bf16[16,48,2048]{2,1,0:T(8,128)(2,1)S(1)}, u32[]{:S(2)}, u32[]{:S(2)}) async-start(bf16[16,48,2048]{2,1,0:T(8,128)(2,1)} %bitcast.132), calls=%async_computation.4 | async-start | bytes 6291456 | tf_op jit(solution)/shard_map/all_to_all | solution.py:100
  200.9 5.8 %fusion.16 = f32[1024,2048]{1,0:T(8,128)S(1)} fusion(bf16[768,2048]{1,0:T(8,128)(2,1)} %bitcast.24, bf16[512,768]{1,0:T(8,128)(2,1)} %fusion.99, bf16[512,768]{1,0:T(8,128)(2,1)} %fusion.92), kind=kOutput, calls=%fused_computation.18 | convolution fusion | flops 3224371200 | bytes 13107200 | tf_op jit(solution)/shard_map/dot_general | solution.py:103
  206.7 2.0 fusion.1
  209.2 2.6 fusion.106
  211.8 2.5 fusion.113
  214.3 24.8 %all-to-all-done.3 = bf16[16,48,2048]{2,1,0:T(8,128)(2,1)S(1)} async-done(((bf16[16,48,2048]{2,1,0:T(8,128)(2,1)}), bf16[16,48,2048]{2,1,0:T(8,128)(2,1)S(1)}, u32[]{:S(2)}, u32[]{:S(2)}) %all-to-all-start.3) | async-done | bytes 3145760 | tf_op jit(solution)/shard_map/all_to_all | solution.py:100
  239.1 4.8 %fusion.20 = f32[1024,2048]{1,0:T(8,128)S(1)} fusion(bf16[768,2048]{1,0:T(8,128)(2,1)S(1)} %bitcast.133, bf16[512,768]{1,0:T(8,128)(2,1)} %fusion.113, bf16[512,768]{1,0:T(8,128)(2,1)} %fusion.106), kind=kOutput, calls=%fused_computation.22 | convolution fusion | flops 3224371200 | bytes 13107200 | tf_op jit(solution)/shard_map/dot_general | solution.py:103
  245.8 4.1 %reduce-scatter.3.cloned.1.call-done = bf16[512,256]{1,0:T(8,128)(2,1)} async-done(((bf16[512,2048]{1,0:T(8,128)(2,1)}), bf16[512,256]{1,0:T(8,128)(2,1)}) %reduce-scatter.3.cloned.1.call-update) | async-done | bytes 262160 | tf_op jit(solution)/shard_map/reduce_scatter | solution.py:105
  249.9 43.8 %reduce-scatter.5.cloned.1.call-done = bf16[512,256]{1,0:T(8,128)(2,1)} async-done(((bf16[512,2048]{1,0:T(8,128)(2,1)}), bf16[512,256]{1,0:T(8,128)(2,1)}) %reduce-scatter.5.cloned.1.call-update) | async-done | bytes 262160 | tf_op jit(solution)/shard_map/reduce_scatter | solution.py:105
  (56 shorter events, 13.3 us)
Async XLA Ops:
  6.5 113.9 %copy-start = (bf16[1,768,2048]{2,1,0:T(8,128)(2,1)S(1)}, bf16[1,768,2048]{2,1,0:T(8,128)(2,1)}, u32[]{:S(2)}) copy-start(bf16[1,768,2048]{2,1,0:T(8,128)(2,1)} %param.11) | copy-start | bytes 9437188
  6.5 2.8 copy-start.4
  6.5 46.5 %all-gather.6.cloned.1.call-start = ((), (), s32[]{:S(2)}) async-start(), calls=%async_computation.8 | async-start | bytes 2359296 | tf_op jit(solution)/shard_map/all_gather | solution.py:63
  8.6 85.8 %all-gather.8.cloned.1.call-start = ((), (), s32[]{:S(2)}) async-start(), calls=%async_computation.9 | async-start | bytes 2359296 | tf_op jit(solution)/shard_map/all_gather | solution.py:63
  10.1 2.5 copy-start.5
  60.1 43.0 %all-to-all-start = ((bf16[16,48,8,256]{3,2,1,0:T(8,128)(2,1)}), bf16[16,48,8,256]{3,2,1,0:T(8,128)(2,1)}, u32[]{:S(2)}, u32[]{:S(2)}) async-start(bf16[16,48,8,256]{3,2,1,0:T(8,128)(2,1)} %copy.29), calls=%async_computation | async-start | bytes 6291456 | tf_op jit(solution)/shard_map/all_to_all | solution.py:93
  103.1 46.4 %all-to-all-start.2 = ((bf16[16,48,8,256]{3,2,1,0:T(8,128)(2,1)}), bf16[16,48,8,256]{3,2,1,0:T(8,128)(2,1)}, u32[]{:S(2)}, u32[]{:S(2)}) async-start(bf16[16,48,8,256]{3,2,1,0:T(8,128)(2,1)} %copy.30), calls=%async_computation.3 | async-start | bytes 6291456 | tf_op jit(solution)/shard_map/all_to_all | solution.py:93
  111.7 4.8 %copy-start.6 = (bf16[1,2048,768]{2,1,0:T(8,128)(2,1)S(1)}, bf16[1,2048,768]{2,1,0:T(8,128)(2,1)}, u32[]{:S(2)}) copy-start(bf16[1,2048,768]{2,1,0:T(8,128)(2,1)} %param.10) | copy-start | bytes 9437188
  114.8 1.6 copy-start.2
  149.5 43.6 %all-to-all-start.1 = ((bf16[16,48,2048]{2,1,0:T(8,128)(2,1)}), bf16[16,48,2048]{2,1,0:T(8,128)(2,1)}, u32[]{:S(2)}, u32[]{:S(2)}) async-start(bf16[16,48,2048]{2,1,0:T(8,128)(2,1)} %bitcast.134), calls=%async_computation.1 | async-start | bytes 6291456 | tf_op jit(solution)/shard_map/all_to_all | solution.py:100
  162.4 4.8 %copy-start.7 = (bf16[1,2048,768]{2,1,0:T(8,128)(2,1)S(1)}, bf16[1,2048,768]{2,1,0:T(8,128)(2,1)}, u32[]{:S(2)}) copy-start(bf16[1,2048,768]{2,1,0:T(8,128)(2,1)} %param.10) | copy-start | bytes 9437188
  165.5 1.6 copy-start.3
  193.1 46.0 %all-to-all-start.3 = ((bf16[16,48,2048]{2,1,0:T(8,128)(2,1)}), bf16[16,48,2048]{2,1,0:T(8,128)(2,1)S(1)}, u32[]{:S(2)}, u32[]{:S(2)}) async-start(bf16[16,48,2048]{2,1,0:T(8,128)(2,1)} %bitcast.132), calls=%async_computation.4 | async-start | bytes 6291456 | tf_op jit(solution)/shard_map/all_to_all | solution.py:100
  200.9 49.0 %reduce-scatter.3.cloned.1.call-start = ((), (), s32[]{:S(2)}) async-start(), calls=%async_computation.6 | async-start | bytes 2359296 | tf_op jit(solution)/shard_map/reduce_scatter | solution.py:105
  208.7 85.0 %reduce-scatter.5.cloned.1.call-start = ((), (), s32[]{:S(2)}) async-start(), calls=%async_computation.7 | async-start | bytes 2359296 | tf_op jit(solution)/shard_map/reduce_scatter | solution.py:105
  245.8 49.8 %copy-start.1 = (bf16[1,768,2048]{2,1,0:T(8,128)(2,1)S(1)}, bf16[1,768,2048]{2,1,0:T(8,128)(2,1)}, u32[]{:S(2)}) copy-start(bf16[1,768,2048]{2,1,0:T(8,128)(2,1)} %param.11) | copy-start | bytes 9437188
Sparse Core Ops, SparseCore 0:
  9.1 43.8 all-gather.5
  54.8 39.6 all-gather.7
  208.9 41.0 reduce-scatter.2
  252.3 41.3 reduce-scatter.4
